TPU v7x, 32 devices: a whole 2x2x4 slice. The times are simulated.
32 devices in a mesh: row: 4 (over y, core), col: 8 (over z, x).
Axes of the slice: x: 2, y: 2, z: 4, core: 2. Of those that a mesh axis runs over, the one named last changes fastest.
Arguments:
- incoming: bfloat16 [8, 32, 16, 1024], P('row', 'col'), may hold values from -6 to 6
- cell_type: int32 [8, 32], P('row', 'col'), may hold values from 0 to 1
- bank: bfloat16 [4, 8, 1024, 1024], P('row', 'col'), may hold values from -0.1875 to 0.1875
- owner: int32 [2], replicated, may hold values from 0 to 31
- port_cell: int32 [16], replicated, may hold values from 0 to 255
- excite: float32 [16, 1024], replicated, may hold values from -6 to 6
Outputs:
- outgoing: bfloat16 [8, 32, 16, 1024], P('row', 'col')
All inputs are finite; a program needn't handle non-finite values.
Results may differ from a plain program's by a relative error of at most 0.0057.
Values may be sent and summed in bfloat16 or wider, within the bound.
No kernel may reach another device: no remote copies, remote signals or barrier semaphores. Data moves between devices by JAX's collectives and lax.ppermute only.
A program may use at most 64 MiB of HBM per device.

v0:
```python
import jax
import jax.numpy as jnp
from jax import lax
from jax.sharding import PartitionSpec as P

TYPES = 2
SWEEPS = 3


def with_halo(block, sides, width):
    for axis, dim in sides:
        count = lax.axis_size(axis)
        forward = [(i, i + 1) for i in range(count - 1)]
        backward = [(target, source) for source, target in forward]
        low = lax.ppermute(
            lax.slice_in_dim(block, block.shape[dim] - width, None, axis=dim), axis, forward
        )
        high = lax.ppermute(lax.slice_in_dim(block, 0, width, axis=dim), axis, backward)
        block = jnp.concatenate([low, block, high], axis=dim)
    return block


def from_root(array, axis, root):
    mine = lax.axis_index(axis) == root
    return lax.psum(jnp.where(mine, array, jnp.zeros_like(array)), axis)


def pass_traces(outgoing):
    face_len = outgoing.shape[-1] // 4
    west_face = outgoing[..., :face_len]
    east_face = outgoing[..., face_len : 2 * face_len]
    north_face = outgoing[..., 2 * face_len : 3 * face_len]
    south_face = outgoing[..., 3 * face_len :]
    side_send = jnp.stack([west_face[:, 0], east_face[:, -1]], axis=1)
    side_got = with_halo(side_send, (("col", 1),), 1)
    new_west = jnp.concatenate([side_got[:, 0][:, None], east_face[:, :-1]], axis=1)
    new_east = jnp.concatenate([west_face[:, 1:], side_got[:, 3][:, None]], axis=1)
    end_send = jnp.stack([north_face[0], south_face[-1]], axis=0)
    end_got = with_halo(end_send, (("row", 0),), 1)
    new_north = jnp.concatenate([end_got[0][None], south_face[:-1]], axis=0)
    new_south = jnp.concatenate([north_face[1:], end_got[3][None]], axis=0)
    return jnp.concatenate([new_west, new_east, new_north, new_south], axis=-1)


def local(incoming, cell_type, bank, owner, port_cell, excite):
    cell_rows, cell_cols, port_count, order = incoming.shape
    col_count = lax.axis_size("col")
    own_operator = bank[0, 0]
    gathered = []
    for kind_id in range(TYPES):
        copied = from_root(own_operator, ("row", "col"), owner[kind_id])
        gathered.append(copied)
    operators = jnp.stack(gathered, axis=0)
    row_ids = lax.axis_index("row") * cell_rows + jnp.arange(cell_rows, dtype=jnp.int32)
    col_ids = lax.axis_index("col") * cell_cols + jnp.arange(cell_cols, dtype=jnp.int32)
    flat_ids = row_ids[:, None] * (cell_cols * col_count) + col_ids[None, :]
    port_hits = (flat_ids[:, :, None] == port_cell[None, None, :]).astype(jnp.float32)
    source = port_hits[..., None] * excite[None, None]
    cell_count = cell_rows * cell_cols
    kinds = cell_type.reshape(cell_count)
    traces = incoming
    outgoing = incoming
    for sweep_id in range(SWEEPS):

        def per_cell(item):
            trace_rows, kind_id = item
            chosen = lax.dynamic_index_in_dim(operators, kind_id, 0, keepdims=False)
            return jnp.dot(trace_rows, chosen, preferred_element_type=jnp.float32)

        products = lax.map(per_cell, (traces.reshape(cell_count, port_count, order), kinds))
        products = products.reshape(cell_rows, cell_cols, port_count, order)
        outgoing = (products + source).astype(jnp.bfloat16)
        if sweep_id + 1 < SWEEPS:
            traces = pass_traces(outgoing)
    return outgoing


def solution(mesh):
    in_specs = (
        P("row", "col", None, None),
        P("row", "col"),
        P("row", "col", None, None),
        P(),
        P(),
        P(),
    )
    out_specs = P("row", "col", None, None)
    return jax.shard_map(local, mesh=mesh, in_specs=in_specs, out_specs=out_specs, check_vma=False)
```

profile of v0, /device:TPU:9, one launch (start us, length us, event | category | flops | bytes accessed | tf_op | source)
XLA Modules:
  0.0 304.9 jit_solution(13254193794620416738)
XLA Ops:
  9.1 3.9 %select_bitcast_fusion = (bf16[1,1024,1024]{2,1,0:T(8,128)(2,1)}, bf16[1,1024,1024]{2,1,0:T(8,128)(2,1)}) fusion(bf16[1,1,1024,1024]{3,2,1,0:T(8,128)(2,1)} %param.14, pred[]{:T(512)S(6)} %eq.24, pred[]{:T(512)S(6)} %eq.23), kind=kLoop, calls=%fused_computation.24 | loop fusion | flops 2097152 | bytes 6291458 | tf_op jit(solution)/shard_map/stack | solution.py:53
  13.9 140.4 %all-reduce.3.cloned.1.call-done = (bf16[1,1024,1024]{2,1,0:T(8,128)(2,1)}, bf16[1,1024,1024]{2,1,0:T(8,128)(2,1)}) async-done(((bf16[1,1024,1024]{2,1,0:T(8,128)(2,1)}, bf16[1,1024,1024]{2,1,0:T(8,128)(2,1)}), (bf16[1,1024,1024]{2,1,0:T(8,128)(2,1)}, bf16[1,1024,1024]{2,1,0:T(8,128)(2,1)})) %all-reduce.3.cloned.1.call-update) | async-done | bytes 4194320 | tf_op jit(solution)/shard_map/psum | solution.py:25
  158.6 36.3 %while.30 = (s32[]{:T(128)}, f32[8,16,1024]{2,1,0:T(8,128)S(1)}, bf16[8,16,1024]{2,1,0:T(8,128)(2,1)}, s32[8]{0:T(128)S(1)}, bf16[2,1024,1024]{2,1,0:T(8,128)(2,1)}, /*index=5*/s32[]{:T(128)}, s32[]{:T(128)}, s32[]{:T(128)}) while((s32[]{:T(128)}, f32[8,16,1024]{2,1,0:T(8,128)S(1)}, bf16[8,16,1024]{2,1,0:T(8,128)(2,1)}, s32[8]{0:T(128)S(1)}, ...), condition=%wide.region_3.4_spmd, body=%wide.region_2.3_spmd.sunk | while | flops 33554436 | bytes 2196615 | solution.py:70
  161.1 2.0 fusion.57
  165.7 2.0 fusion.57
  170.2 2.0 fusion.57
  174.7 2.0 fusion.57
  179.3 2.0 fusion.57
  183.8 2.0 fusion.57
  188.3 2.0 fusion.57
  192.9 2.0 fusion.57
  195.0 4.8 %collective-permute-start.2 = (bf16[1,4,16,256]{3,2,1,0:T(8,128)(2,1)S(1)}, bf16[1,4,16,256]{3,2,1,0:T(8,128)(2,1)S(1)}, u32[]{:S(2)}, u32[]{:S(2)}) collective-permute-start(bf16[1,4,16,256]{3,2,1,0:T(8,128)(2,1)S(1)} %get-tuple-element.135), channel_id=1, source_target_pairs={{0,8},{8,16},{16,24},{1,9},{9,17},{17,25},{2,10},{10,18},{18,26},{... | collective-permute-start | bytes 98312 | tf_op jit(solution)/shard_map/ppermute | solution.py:15
  201.8 3.0 collective-permute-start
  204.7 3.2 %collective-permute-start.1 = (bf16[2,1,16,256]{3,2,1,0:T(8,128)(2,1)S(1)}, bf16[2,1,16,256]{3,2,1,0:T(8,128)(2,1)S(1)}, u32[]{:S(2)}, u32[]{:S(2)}) collective-permute-start(bf16[2,1,16,256]{3,2,1,0:T(8,128)(2,1)S(1)} %get-tuple-element.132), channel_id=1, source_target_pairs={{1,0},{2,1},{3,2},{4,3},{5,4},{6,5},{7,6},{9,8},{10,9},{11,10},{12... | collective-permute-start | bytes 49160 | tf_op jit(solution)/shard_map/ppermute | solution.py:18
  209.3 36.1 %while.31 = (s32[]{:T(128)}, f32[8,16,1024]{2,1,0:T(8,128)S(1)}, bf16[8,16,1024]{2,1,0:T(8,128)(2,1)S(1)}, s32[8]{0:T(128)S(1)}, bf16[2,1024,1024]{2,1,0:T(8,128)(2,1)}, /*index=5*/s32[]{:T(128)}, s32[]{:T(128)}, s32[]{:T(128)}) while((s32[]{:T(128)}, f32[8,16,1024]{2,1,0:T(8,128)S(1)}, bf16[8,16,1024]{2,1,0:T(8,128)(2,1)S(1)}, ...), condition=%wide.region_5.6_spmd, body=%wide.region_4.5_spmd.sunk | while | flops 33554436 | bytes 2196615 | solution.py:70
  211.9 2.0 fusion.60
  216.4 2.0 fusion.60
  220.9 2.0 fusion.60
  225.4 2.0 fusion.60
  245.6 5.1 %collective-permute-start.6 = (bf16[1,4,16,256]{3,2,1,0:T(8,128)(2,1)S(1)}, bf16[1,4,16,256]{3,2,1,0:T(8,128)(2,1)S(1)}, u32[]{:S(2)}, u32[]{:S(2)}) collective-permute-start(bf16[1,4,16,256]{3,2,1,0:T(8,128)(2,1)S(1)} %get-tuple-element.127), channel_id=1, source_target_pairs={{0,8},{8,16},{16,24},{1,9},{9,17},{17,25},{2,10},{10,18},{18,26},{... | collective-permute-start | bytes 98312 | tf_op jit(solution)/shard_map/ppermute | solution.py:15
  252.6 4.0 %collective-permute-start.4 = (bf16[2,1,16,256]{3,2,1,0:T(8,128)(2,1)S(1)}, bf16[2,1,16,256]{3,2,1,0:T(8,128)(2,1)S(1)}, u32[]{:S(2)}, u32[]{:S(2)}) collective-permute-start(bf16[2,1,16,256]{3,2,1,0:T(8,128)(2,1)S(1)} %get-tuple-element.123), channel_id=1, source_target_pairs={{0,1},{1,2},{2,3},{3,4},{4,5},{5,6},{6,7},{8,9},{9,10},{10,11},{11... | collective-permute-start | bytes 49160 | tf_op jit(solution)/shard_map/ppermute | solution.py:15
  256.6 2.2 collective-permute-start.5
  258.8 2.3 collective-permute-done.5
  261.2 36.1 %while.32 = (s32[]{:T(128)}, f32[8,16,1024]{2,1,0:T(8,128)S(1)}, bf16[8,16,1024]{2,1,0:T(8,128)(2,1)S(1)}, s32[8]{0:T(128)S(1)}, bf16[2,1024,1024]{2,1,0:T(8,128)(2,1)}, /*index=5*/s32[]{:T(128)}, s32[]{:T(128)}, s32[]{:T(128)}) while((s32[]{:T(128)}, f32[8,16,1024]{2,1,0:T(8,128)S(1)}, bf16[8,16,1024]{2,1,0:T(8,128)(2,1)S(1)}, ...), condition=%wide.region_7.8_spmd, body=%wide.region_6.7_spmd.sunk | while | flops 33554436 | bytes 2196615 | solution.py:70
  (79 shorter events, 52.0 us)
Async XLA Ops:
  6.5 147.7 %all-reduce.3.cloned.1.call-start = ((), (), s32[]{:S(2)}) async-start(), calls=%async_computation | async-start | bytes 8388608 | tf_op jit(solution)/shard_map/psum | solution.py:25
  13.0 0.7 copy-start.4
  13.0 0.8 copy-start.3
  154.3 2.2 copy-start.1
  156.7 1.9 copy-start
  158.6 36.3 %copy-start.2 = (f32[16,1024]{1,0:T(8,128)S(1)}, f32[16,1024]{1,0:T(8,128)}, u32[]{:S(2)}) copy-start(f32[16,1024]{1,0:T(8,128)} %param.17) | copy-start | bytes 196612
  195.0 14.2 %collective-permute-start.2 = (bf16[1,4,16,256]{3,2,1,0:T(8,128)(2,1)S(1)}, bf16[1,4,16,256]{3,2,1,0:T(8,128)(2,1)S(1)}, u32[]{:S(2)}, u32[]{:S(2)}) collective-permute-start(bf16[1,4,16,256]{3,2,1,0:T(8,128)(2,1)S(1)} %get-tuple-element.135), channel_id=1, source_target_pairs={{0,8},{8,16},{16,24},{1,9},{9,17},{17,25},{2,10},{10,18},{18,26},{... | collective-permute-start | bytes 98312 | tf_op jit(solution)/shard_map/ppermute | solution.py:15
  199.9 9.4 %collective-permute-start.3 = (bf16[1,4,16,256]{3,2,1,0:T(8,128)(2,1)S(1)}, bf16[1,4,16,256]{3,2,1,0:T(8,128)(2,1)S(1)}, u32[]{:S(2)}, u32[]{:S(2)}) collective-permute-start(bf16[1,4,16,256]{3,2,1,0:T(8,128)(2,1)S(1)} %get-tuple-element.136), channel_id=1, source_target_pairs={{8,0},{16,8},{24,16},{9,1},{17,9},{25,17},{10,2},{18,10},{26,18},{... | collective-permute-start | bytes 98312 | tf_op jit(solution)/shard_map/ppermute | solution.py:18
  201.8 6.2 %collective-permute-start = (bf16[2,1,16,256]{3,2,1,0:T(8,128)(2,1)S(1)}, bf16[2,1,16,256]{3,2,1,0:T(8,128)(2,1)S(1)}, u32[]{:S(2)}, u32[]{:S(2)}) collective-permute-start(bf16[2,1,16,256]{3,2,1,0:T(8,128)(2,1)S(1)} %get-tuple-element.131), channel_id=1, source_target_pairs={{0,1},{1,2},{2,3},{3,4},{4,5},{5,6},{6,7},{8,9},{9,10},{10,11},{11... | collective-permute-start | bytes 49160 | tf_op jit(solution)/shard_map/ppermute | solution.py:15
  204.7 4.5 %collective-permute-start.1 = (bf16[2,1,16,256]{3,2,1,0:T(8,128)(2,1)S(1)}, bf16[2,1,16,256]{3,2,1,0:T(8,128)(2,1)S(1)}, u32[]{:S(2)}, u32[]{:S(2)}) collective-permute-start(bf16[2,1,16,256]{3,2,1,0:T(8,128)(2,1)S(1)} %get-tuple-element.132), channel_id=1, source_target_pairs={{1,0},{2,1},{3,2},{4,3},{5,4},{6,5},{7,6},{9,8},{10,9},{11,10},{12... | collective-permute-start | bytes 49160 | tf_op jit(solution)/shard_map/ppermute | solution.py:18
  245.6 15.5 %collective-permute-start.6 = (bf16[1,4,16,256]{3,2,1,0:T(8,128)(2,1)S(1)}, bf16[1,4,16,256]{3,2,1,0:T(8,128)(2,1)S(1)}, u32[]{:S(2)}, u32[]{:S(2)}) collective-permute-start(bf16[1,4,16,256]{3,2,1,0:T(8,128)(2,1)S(1)} %get-tuple-element.127), channel_id=1, source_target_pairs={{0,8},{8,16},{16,24},{1,9},{9,17},{17,25},{2,10},{10,18},{18,26},{... | collective-permute-start | bytes 98312 | tf_op jit(solution)/shard_map/ppermute | solution.py:15
  250.7 10.4 %collective-permute-start.7 = (bf16[1,4,16,256]{3,2,1,0:T(8,128)(2,1)S(1)}, bf16[1,4,16,256]{3,2,1,0:T(8,128)(2,1)S(1)}, u32[]{:S(2)}, u32[]{:S(2)}) collective-permute-start(bf16[1,4,16,256]{3,2,1,0:T(8,128)(2,1)S(1)} %get-tuple-element.128), channel_id=1, source_target_pairs={{8,0},{16,8},{24,16},{9,1},{17,9},{25,17},{10,2},{18,10},{26,18},{... | collective-permute-start | bytes 98312 | tf_op jit(solution)/shard_map/ppermute | solution.py:18
  252.6 6.2 %collective-permute-start.4 = (bf16[2,1,16,256]{3,2,1,0:T(8,128)(2,1)S(1)}, bf16[2,1,16,256]{3,2,1,0:T(8,128)(2,1)S(1)}, u32[]{:S(2)}, u32[]{:S(2)}) collective-permute-start(bf16[2,1,16,256]{3,2,1,0:T(8,128)(2,1)S(1)} %get-tuple-element.123), channel_id=1, source_target_pairs={{0,1},{1,2},{2,3},{3,4},{4,5},{5,6},{6,7},{8,9},{9,10},{10,11},{11... | collective-permute-start | bytes 49160 | tf_op jit(solution)/shard_map/ppermute | solution.py:15
  256.6 4.5 %collective-permute-start.5 = (bf16[2,1,16,256]{3,2,1,0:T(8,128)(2,1)S(1)}, bf16[2,1,16,256]{3,2,1,0:T(8,128)(2,1)S(1)}, u32[]{:S(2)}, u32[]{:S(2)}) collective-permute-start(bf16[2,1,16,256]{3,2,1,0:T(8,128)(2,1)S(1)} %get-tuple-element.124), channel_id=1, source_target_pairs={{1,0},{2,1},{3,2},{4,3},{5,4},{6,5},{7,6},{9,8},{10,9},{11,10},{12... | collective-permute-start | bytes 49160 | tf_op jit(solution)/shard_map/ppermute | solution.py:18
Sparse Core Ops, SparseCore 0:
  13.1 141.1 all-reduce.2
where the time goes:
time: 308 us; the launch traced here: 305 us
  waiting for transfers between devices  144 us (47%)
  matrix products  47.8 us (16%)
  loops' own time  45.4 us (15%)
  starting transfers between devices  26.1 us (8%)
  local copies, waits for them, and re-layouts  21.8 us (7%)
  between operations  14.8 us (5%)
  other arithmetic  5.13 us (2%)
    psum x1, waiting for transfers between devices, from_root(): return lax.psum(jnp.where(mine, array, jnp.zeros_like(array)), axis)  140 us
    dot_general x24, matrix products, per_cell(): return jnp.dot(trace_rows, chosen, preferred_element_type=jnp.float32)  47.8 us
    another operation x3, loops' own time, local(): lax.map(per_cell, (traces.reshape(cell_count, port_count, order), kinds))  45.4 us
    ppermute x4, starting transfers between devices, with_halo(): lax.ppermute(lax.slice_in_dim(block, block.shape[dim] - width, None, axis...  16.8 us
    dynamic_slice x24, local copies, waits for them, and re-layouts, local(): lax.map(per_cell, (traces.reshape(cell_count, port_count, order), kinds))  15.3 us
    ppermute x4, starting transfers between devices, with_halo(): lax.ppermute(lax.slice_in_dim(block, 0, width, axis=dim), axis, backward)  9.26 us
  transfers between devices with their start and end apart: 9, of which 3 were waited for; matrix products, arithmetic and copies ran while one was open for 0% of the time, Pallas kernels for 0%

commit v1 on v0

--- a/solution.py
+++ b/solution.py
@@ -20,11 +20,6 @@
     return block
 
 
-def from_root(array, axis, root):
-    mine = lax.axis_index(axis) == root
-    return lax.psum(jnp.where(mine, array, jnp.zeros_like(array)), axis)
-
-
 def pass_traces(outgoing):
     face_len = outgoing.shape[-1] // 4
     west_face = outgoing[..., :face_len]
@@ -42,34 +37,42 @@
     return jnp.concatenate([new_west, new_east, new_north, new_south], axis=-1)
 
 
+def masked_stack(own_operator, owner):
+    me = lax.axis_index("row") * lax.axis_size("col") + lax.axis_index("col")
+    return jnp.stack(
+        [jnp.where(me == owner[k], own_operator, jnp.zeros_like(own_operator)) for k in range(TYPES)],
+        axis=0,
+    )
+
+
+def broadcast(own_operator, owner):
+    return lax.psum(masked_stack(own_operator, owner), ("row", "col"))
+
+
 def local(incoming, cell_type, bank, owner, port_cell, excite):
     cell_rows, cell_cols, port_count, order = incoming.shape
     col_count = lax.axis_size("col")
-    own_operator = bank[0, 0]
-    gathered = []
-    for kind_id in range(TYPES):
-        copied = from_root(own_operator, ("row", "col"), owner[kind_id])
-        gathered.append(copied)
-    operators = jnp.stack(gathered, axis=0)
+    operators = broadcast(bank[0, 0], owner)
     row_ids = lax.axis_index("row") * cell_rows + jnp.arange(cell_rows, dtype=jnp.int32)
     col_ids = lax.axis_index("col") * cell_cols + jnp.arange(cell_cols, dtype=jnp.int32)
     flat_ids = row_ids[:, None] * (cell_cols * col_count) + col_ids[None, :]
     port_hits = (flat_ids[:, :, None] == port_cell[None, None, :]).astype(jnp.float32)
     source = port_hits[..., None] * excite[None, None]
-    cell_count = cell_rows * cell_cols
-    kinds = cell_type.reshape(cell_count)
+    kinds = cell_type[:, :, None, None]
     traces = incoming
     outgoing = incoming
     for sweep_id in range(SWEEPS):
-
-        def per_cell(item):
-            trace_rows, kind_id = item
-            chosen = lax.dynamic_index_in_dim(operators, kind_id, 0, keepdims=False)
-            return jnp.dot(trace_rows, chosen, preferred_element_type=jnp.float32)
-
-        products = lax.map(per_cell, (traces.reshape(cell_count, port_count, order), kinds))
-        products = products.reshape(cell_rows, cell_cols, port_count, order)
-        outgoing = (products + source).astype(jnp.bfloat16)
+        rows = traces.reshape(cell_rows * cell_cols * port_count, order)
+        products = [
+            jnp.dot(rows, operators[k], preferred_element_type=jnp.float32).reshape(
+                cell_rows, cell_cols, port_count, order
+            )
+            for k in range(TYPES)
+        ]
+        chosen = products[0]
+        for k in range(1, TYPES):
+            chosen = jnp.where(kinds == k, products[k], chosen)
+        outgoing = (chosen + source).astype(jnp.bfloat16)
         if sweep_id + 1 < SWEEPS:
             traces = pass_traces(outgoing)
     return outgoing

time: 308 us -> 200 us (0.65)
  loops' own time: 45.4 us -> 0 us
  matrix products: 47.8 us -> 6.77 us
  local copies, waits for them, and re-layouts: 21.8 us -> 2.02 us
    another operation x3 -> x0, loops' own time: 45.4 us -> none  [local(): lax.map(per_cell, (traces.reshape(cell_count, port_count, order), kinds))]
    dot_general x24 -> x6, matrix products: 47.8 us -> 6.77 us  [local(): jnp.dot(rows, operators[k], preferred_element_type=jnp.float32)]
    dynamic_slice x24 -> x0, local copies, waits for them, and re-layouts: 15.3 us -> none  [local(): lax.map(per_cell, (traces.reshape(cell_count, port_count, order), kinds))]
    unnamed x11 -> x10, local copies, waits for them, and re-layouts: 4.76 us -> 0.64 us
where the time goes in v1:
time: 200 us; the launch traced here: 198 us
  waiting for transfers between devices  144 us (72%)
  starting transfers between devices  26.2 us (13%)
  between operations  14.9 us (7%)
  matrix products  6.77 us (3%)
  other arithmetic  4.51 us (2%)
  local copies, waits for them, and re-layouts  2.02 us (1%)
    psum x1, waiting for transfers between devices, broadcast(): return lax.psum(masked_stack(own_operator, owner), ('row', 'col'))  140 us
    ppermute x4, starting transfers between devices, with_halo(): lax.ppermute(lax.slice_in_dim(block, block.shape[dim] - width, None, axis...  17 us
    ppermute x4, starting transfers between devices, with_halo(): lax.ppermute(lax.slice_in_dim(block, 0, width, axis=dim), axis, backward)  9.2 us
    dot_general x6, matrix products, local(): jnp.dot(rows, operators[k], preferred_element_type=jnp.float32)  6.77 us
  transfers between devices with their start and end apart: 9, of which 3 were waited for; matrix products, arithmetic and copies ran while one was open for 0% of the time, Pallas kernels for 0%

profile of v1, /device:TPU:9, one launch (start us, length us, event | category | flops | bytes accessed | tf_op | source)
XLA Modules:
  0.0 198.1 jit_solution(9105974524779818889)
XLA Ops:
  6.5 1.3 fusion.43
  9.1 1.9 select_bitcast_fusion.1
  11.0 2.4 %pad_maximum_fusion = bf16[2,1024,1024]{2,1,0:T(8,128)(2,1)} fusion(bf16[1,1024,1024]{2,1,0:T(8,128)(2,1)S(1)} %get-tuple-element.6, bf16[1,1024,1024]{2,1,0:T(8,128)(2,1)S(1)} %get-tuple-element.5), kind=kLoop, calls=%fused_computation | loop fusion | flops 2097152 | bytes 8388608 | tf_op jit(solution)/shard_map/stack | solution.py:42
  13.4 0.6 copy-done.4
  14.1 0.1 broadcast_add_fusion
  14.1 0.1 compare_convert_fusion
  14.2 140.1 %all-reduce.2.cloned.1.call-done = bf16[2,1024,1024]{2,1,0:T(8,128)(2,1)} async-done(((bf16[2,1024,1024]{2,1,0:T(8,128)(2,1)}), bf16[2,1024,1024]{2,1,0:T(8,128)(2,1)}) %all-reduce.2.cloned.1.call-update) | async-done | bytes 4194320 | tf_op jit(solution)/shard_map/psum | solution.py:49
  154.3 2.0 %fusion.8 = f32[1024,128]{0,1:T(8,128)S(1)} fusion(bf16[128,1024]{1,0:T(8,128)(2,1)S(1)} %bitcast.49, bf16[2,1024,1024]{2,1,0:T(8,128)(2,1)} %all-reduce.2.cloned.1.call-done), kind=kOutput, calls=%fused_computation.9 | convolution fusion | flops 268435456 | bytes 2883584 | tf_op jit(solution)/shard_map/dot_general | solution.py:67
  156.4 2.2 %fusion.10 = f32[1024,128]{0,1:T(8,128)S(1)} fusion(bf16[128,1024]{1,0:T(8,128)(2,1)S(1)} %bitcast.50, bf16[2,1024,1024]{2,1,0:T(8,128)(2,1)} %all-reduce.2.cloned.1.call-done), kind=kOutput, calls=%fused_computation.11 | convolution fusion | flops 268435456 | bytes 2883584 | tf_op jit(solution)/shard_map/dot_general | solution.py:67
  158.6 0.1 fusion.36
  158.7 5.0 %collective-permute-start.2 = (bf16[1,4,16,256]{3,2,1,0:T(8,128)(2,1)S(1)}, bf16[1,4,16,256]{3,2,1,0:T(8,128)(2,1)S(1)}, u32[]{:S(2)}, u32[]{:S(2)}) collective-permute-start(bf16[1,4,16,256]{3,2,1,0:T(8,128)(2,1)S(1)} %get-tuple-element.19), channel_id=1, source_target_pairs={{0,8},{8,16},{16,24},{1,9},{9,17},{17,25},{2,10},{10,18},{18,26},{... | collective-permute-start | bytes 98312 | tf_op jit(solution)/shard_map/ppermute | solution.py:15
  163.7 1.9 collective-permute-start.3
  165.6 2.9 %collective-permute-start = (bf16[2,1,16,256]{3,2,1,0:T(8,128)(2,1)S(1)}, bf16[2,1,16,256]{3,2,1,0:T(8,128)(2,1)S(1)}, u32[]{:S(2)}, u32[]{:S(2)}) collective-permute-start(bf16[2,1,16,256]{3,2,1,0:T(8,128)(2,1)S(1)} %get-tuple-element.15), channel_id=1, source_target_pairs={{0,1},{1,2},{2,3},{3,4},{4,5},{5,6},{6,7},{8,9},{9,10},{10,11},{11... | collective-permute-start | bytes 49160 | tf_op jit(solution)/shard_map/ppermute | solution.py:15
  168.5 3.3 %collective-permute-start.1 = (bf16[2,1,16,256]{3,2,1,0:T(8,128)(2,1)S(1)}, bf16[2,1,16,256]{3,2,1,0:T(8,128)(2,1)S(1)}, u32[]{:S(2)}, u32[]{:S(2)}) collective-permute-start(bf16[2,1,16,256]{3,2,1,0:T(8,128)(2,1)S(1)} %get-tuple-element.16), channel_id=1, source_target_pairs={{1,0},{2,1},{3,2},{4,3},{5,4},{6,5},{7,6},{9,8},{10,9},{11,10},{12... | collective-permute-start | bytes 49160 | tf_op jit(solution)/shard_map/ppermute | solution.py:18
  171.9 1.1 collective-permute-done.1
  173.0 0.4 fusion.6
  173.5 0.5 fusion.30
  174.0 5.1 %collective-permute-start.6 = (bf16[1,4,16,256]{3,2,1,0:T(8,128)(2,1)S(1)}, bf16[1,4,16,256]{3,2,1,0:T(8,128)(2,1)S(1)}, u32[]{:S(2)}, u32[]{:S(2)}) collective-permute-start(bf16[1,4,16,256]{3,2,1,0:T(8,128)(2,1)S(1)} %get-tuple-element.11), channel_id=1, source_target_pairs={{0,8},{8,16},{16,24},{1,9},{9,17},{17,25},{2,10},{10,18},{18,26},{... | collective-permute-start | bytes 98312 | tf_op jit(solution)/shard_map/ppermute | solution.py:15
  179.1 1.9 collective-permute-start.7
  181.0 4.1 %collective-permute-start.4 = (bf16[2,1,16,256]{3,2,1,0:T(8,128)(2,1)S(1)}, bf16[2,1,16,256]{3,2,1,0:T(8,128)(2,1)S(1)}, u32[]{:S(2)}, u32[]{:S(2)}) collective-permute-start(bf16[2,1,16,256]{3,2,1,0:T(8,128)(2,1)S(1)} %get-tuple-element.7), channel_id=1, source_target_pairs={{0,1},{1,2},{2,3},{3,4},{4,5},{5,6},{6,7},{8,9},{9,10},{10,11},{11... | collective-permute-start | bytes 49160 | tf_op jit(solution)/shard_map/ppermute | solution.py:15
  185.1 2.1 %collective-permute-start.5 = (bf16[2,1,16,256]{3,2,1,0:T(8,128)(2,1)S(1)}, bf16[2,1,16,256]{3,2,1,0:T(8,128)(2,1)S(1)}, u32[]{:S(2)}, u32[]{:S(2)}) collective-permute-start(bf16[2,1,16,256]{3,2,1,0:T(8,128)(2,1)S(1)} %get-tuple-element.8), channel_id=1, source_target_pairs={{1,0},{2,1},{3,2},{4,3},{5,4},{6,5},{7,6},{9,8},{10,9},{11,10},{12... | collective-permute-start | bytes 49160 | tf_op jit(solution)/shard_map/ppermute | solution.py:18
  187.2 2.4 %collective-permute-done.5 = bf16[2,1,16,256]{3,2,1,0:T(8,128)(2,1)S(1)} collective-permute-done((bf16[2,1,16,256]{3,2,1,0:T(8,128)(2,1)S(1)}, bf16[2,1,16,256]{3,2,1,0:T(8,128)(2,1)S(1)}, u32[]{:S(2)}, u32[]{:S(2)}) %collective-permute-start.5) | collective-permute-done | bytes 16416 | tf_op jit(solution)/shard_map/ppermute | solution.py:18
  189.6 0.4 fusion.4
  190.1 1.2 fusion.33
  (26 shorter events, 0.1 us)
Async XLA Ops:
  6.5 147.8 %copy-start = (bf16[2,4,16,1024]{3,2,1,0:T(8,128)(2,1)S(1)}, bf16[2,4,16,1024]{3,2,1,0:T(8,128)(2,1)}, u32[]{:S(2)}) copy-start(bf16[2,4,16,1024]{3,2,1,0:T(8,128)(2,1)} %param.6) | copy-start | bytes 786436
  6.5 147.8 %all-reduce.2.cloned.1.call-start = ((), (), s32[]{:S(2)}) async-start(), calls=%async_computation | async-start | bytes 8388608 | tf_op jit(solution)/shard_map/psum | solution.py:49
  13.4 0.7 copy-start.4
  13.4 0.8 copy-start.2
  156.3 2.2 %copy-start.1 = (f32[16,1024]{1,0:T(8,128)S(1)}, f32[16,1024]{1,0:T(8,128)}, u32[]{:S(2)}) copy-start(f32[16,1024]{1,0:T(8,128)} %param.11) | copy-start | bytes 196612
  156.3 16.7 %copy-start.3 = (bf16[2,1024,1024]{2,1,0:T(8,128)(2,1)S(1)}, bf16[2,1024,1024]{2,1,0:T(8,128)(2,1)}, u32[]{:S(2)}) copy-start(bf16[2,1024,1024]{2,1,0:T(8,128)(2,1)} %all-reduce.2.cloned.1.call-done) | copy-start | bytes 12582916
  158.7 14.3 %collective-permute-start.2 = (bf16[1,4,16,256]{3,2,1,0:T(8,128)(2,1)S(1)}, bf16[1,4,16,256]{3,2,1,0:T(8,128)(2,1)S(1)}, u32[]{:S(2)}, u32[]{:S(2)}) collective-permute-start(bf16[1,4,16,256]{3,2,1,0:T(8,128)(2,1)S(1)} %get-tuple-element.19), channel_id=1, source_target_pairs={{0,8},{8,16},{16,24},{1,9},{9,17},{17,25},{2,10},{10,18},{18,26},{... | collective-permute-start | bytes 98312 | tf_op jit(solution)/shard_map/ppermute | solution.py:15
  163.7 9.3 %collective-permute-start.3 = (bf16[1,4,16,256]{3,2,1,0:T(8,128)(2,1)S(1)}, bf16[1,4,16,256]{3,2,1,0:T(8,128)(2,1)S(1)}, u32[]{:S(2)}, u32[]{:S(2)}) collective-permute-start(bf16[1,4,16,256]{3,2,1,0:T(8,128)(2,1)S(1)} %get-tuple-element.20), channel_id=1, source_target_pairs={{8,0},{16,8},{24,16},{9,1},{17,9},{25,17},{10,2},{18,10},{26,18},{... | collective-permute-start | bytes 98312 | tf_op jit(solution)/shard_map/ppermute | solution.py:18
  165.6 6.2 %collective-permute-start = (bf16[2,1,16,256]{3,2,1,0:T(8,128)(2,1)S(1)}, bf16[2,1,16,256]{3,2,1,0:T(8,128)(2,1)S(1)}, u32[]{:S(2)}, u32[]{:S(2)}) collective-permute-start(bf16[2,1,16,256]{3,2,1,0:T(8,128)(2,1)S(1)} %get-tuple-element.15), channel_id=1, source_target_pairs={{0,1},{1,2},{2,3},{3,4},{4,5},{5,6},{6,7},{8,9},{9,10},{10,11},{11... | collective-permute-start | bytes 49160 | tf_op jit(solution)/shard_map/ppermute | solution.py:15
  168.5 4.5 %collective-permute-start.1 = (bf16[2,1,16,256]{3,2,1,0:T(8,128)(2,1)S(1)}, bf16[2,1,16,256]{3,2,1,0:T(8,128)(2,1)S(1)}, u32[]{:S(2)}, u32[]{:S(2)}) collective-permute-start(bf16[2,1,16,256]{3,2,1,0:T(8,128)(2,1)S(1)} %get-tuple-element.16), channel_id=1, source_target_pairs={{1,0},{2,1},{3,2},{4,3},{5,4},{6,5},{7,6},{9,8},{10,9},{11,10},{12... | collective-permute-start | bytes 49160 | tf_op jit(solution)/shard_map/ppermute | solution.py:18
  174.0 15.6 %collective-permute-start.6 = (bf16[1,4,16,256]{3,2,1,0:T(8,128)(2,1)S(1)}, bf16[1,4,16,256]{3,2,1,0:T(8,128)(2,1)S(1)}, u32[]{:S(2)}, u32[]{:S(2)}) collective-permute-start(bf16[1,4,16,256]{3,2,1,0:T(8,128)(2,1)S(1)} %get-tuple-element.11), channel_id=1, source_target_pairs={{0,8},{8,16},{16,24},{1,9},{9,17},{17,25},{2,10},{10,18},{18,26},{... | collective-permute-start | bytes 98312 | tf_op jit(solution)/shard_map/ppermute | solution.py:15
  179.1 10.5 %collective-permute-start.7 = (bf16[1,4,16,256]{3,2,1,0:T(8,128)(2,1)S(1)}, bf16[1,4,16,256]{3,2,1,0:T(8,128)(2,1)S(1)}, u32[]{:S(2)}, u32[]{:S(2)}) collective-permute-start(bf16[1,4,16,256]{3,2,1,0:T(8,128)(2,1)S(1)} %get-tuple-element.12), channel_id=1, source_target_pairs={{8,0},{16,8},{24,16},{9,1},{17,9},{25,17},{10,2},{18,10},{26,18},{... | collective-permute-start | bytes 98312 | tf_op jit(solution)/shard_map/ppermute | solution.py:18
  181.0 6.2 %collective-permute-start.4 = (bf16[2,1,16,256]{3,2,1,0:T(8,128)(2,1)S(1)}, bf16[2,1,16,256]{3,2,1,0:T(8,128)(2,1)S(1)}, u32[]{:S(2)}, u32[]{:S(2)}) collective-permute-start(bf16[2,1,16,256]{3,2,1,0:T(8,128)(2,1)S(1)} %get-tuple-element.7), channel_id=1, source_target_pairs={{0,1},{1,2},{2,3},{3,4},{4,5},{5,6},{6,7},{8,9},{9,10},{10,11},{11... | collective-permute-start | bytes 49160 | tf_op jit(solution)/shard_map/ppermute | solution.py:15
  185.1 4.5 %collective-permute-start.5 = (bf16[2,1,16,256]{3,2,1,0:T(8,128)(2,1)S(1)}, bf16[2,1,16,256]{3,2,1,0:T(8,128)(2,1)S(1)}, u32[]{:S(2)}, u32[]{:S(2)}) collective-permute-start(bf16[2,1,16,256]{3,2,1,0:T(8,128)(2,1)S(1)} %get-tuple-element.8), channel_id=1, source_target_pairs={{1,0},{2,1},{3,2},{4,3},{5,4},{6,5},{7,6},{9,8},{10,9},{11,10},{12... | collective-permute-start | bytes 49160 | tf_op jit(solution)/shard_map/ppermute | solution.py:18
Sparse Core Ops, SparseCore 0:
  13.5 140.7 all-reduce.1

commit v2 on v1

--- a/solution.py
+++ b/solution.py
@@ -37,22 +37,73 @@
     return jnp.concatenate([new_west, new_east, new_north, new_south], axis=-1)
 
 
-def masked_stack(own_operator, owner):
-    me = lax.axis_index("row") * lax.axis_size("col") + lax.axis_index("col")
-    return jnp.stack(
-        [jnp.where(me == owner[k], own_operator, jnp.zeros_like(own_operator)) for k in range(TYPES)],
-        axis=0,
-    )
+def device_bits(axis):
+    count = lax.axis_size(axis)
+    bits = count.bit_length() - 1
+    return bits if (1 << bits) == count else None
 
 
-def broadcast(own_operator, owner):
-    return lax.psum(masked_stack(own_operator, owner), ("row", "col"))
+def swap(block, bit, col_bits):
+    count = lax.axis_size("col") * lax.axis_size("row")
+    pairs = [(i, i ^ (1 << bit)) for i in range(count)]
+    return lax.ppermute(block, ("row", "col"), pairs)
+
+
+def scatter_gather(block, owner, order, col_bits, me):
+    done_mask = 0
+    full = (1 << len(order)) - 1
+    for bit in order:
+        half = block.shape[1] // 2
+        mine = ((me >> bit) & 1) == 1
+        low, high = block[:, :half], block[:, half:]
+        keep = jnp.where(mine, high, low)
+        give = jnp.where(mine, low, high)
+        got = swap(give, bit, col_bits)
+        outside = full & ~done_mask
+        have = ((me ^ owner) & outside) == 0
+        block = jnp.where(have[:, None, None], keep, got)
+        done_mask |= 1 << bit
+    for bit in reversed(order):
+        mine = ((me >> bit) & 1) == 1
+        got = swap(block, bit, col_bits)
+        block = jnp.where(
+            mine, jnp.concatenate([got, block], axis=1), jnp.concatenate([block, got], axis=1)
+        )
+    return block
+
+
+def broadcast_parts(own_operator, owner):
+    col_bits = device_bits("col")
+    row_bits = device_bits("row")
+    me = lax.axis_index("row") * lax.axis_size("col") + lax.axis_index("col")
+    stacked = jnp.stack([own_operator] * TYPES, axis=0)
+    order_len = None if col_bits is None or row_bits is None else col_bits + row_bits
+    if order_len is None or row_bits < 1 or col_bits < 1 or (own_operator.shape[0] >> order_len) < 8:
+        mask = (me == owner)[:, None, None]
+        return [lax.psum(jnp.where(mask, stacked, jnp.zeros_like(stacked)), ("row", "col"))]
+    core = col_bits
+    middle = list(range(col_bits - 1)) + list(range(col_bits + 1, col_bits + row_bits))
+    last = [col_bits - 1]
+    streams = max(1, min(3, len(middle)))
+    width = own_operator.shape[1]
+    unit = width // 128
+    sizes = [unit // streams + (1 if s < unit % streams else 0) for s in range(streams)]
+    parts = []
+    offset = 0
+    for s in range(streams):
+        cols = sizes[s] * 128
+        rotated = middle[s:] + middle[:s]
+        order = [core] + rotated + last
+        piece = stacked[:, :, offset : offset + cols]
+        parts.append(scatter_gather(piece, owner, order, col_bits, me))
+        offset += cols
+    return parts
 
 
 def local(incoming, cell_type, bank, owner, port_cell, excite):
     cell_rows, cell_cols, port_count, order = incoming.shape
     col_count = lax.axis_size("col")
-    operators = broadcast(bank[0, 0], owner)
+    parts = broadcast_parts(bank[0, 0], owner)
     row_ids = lax.axis_index("row") * cell_rows + jnp.arange(cell_rows, dtype=jnp.int32)
     col_ids = lax.axis_index("col") * cell_cols + jnp.arange(cell_cols, dtype=jnp.int32)
     flat_ids = row_ids[:, None] * (cell_cols * col_count) + col_ids[None, :]
@@ -64,9 +115,9 @@
     for sweep_id in range(SWEEPS):
         rows = traces.reshape(cell_rows * cell_cols * port_count, order)
         products = [
-            jnp.dot(rows, operators[k], preferred_element_type=jnp.float32).reshape(
-                cell_rows, cell_cols, port_count, order
-            )
+            jnp.concatenate(
+                [jnp.dot(rows, part[k], preferred_element_type=jnp.float32) for part in parts], axis=-1
+            ).reshape(cell_rows, cell_cols, port_count, order)
             for k in range(TYPES)
         ]
         chosen = products[0]

time: 200 us -> 133 us (0.67)
  waiting for transfers between devices: 144 us -> 36.1 us
  starting transfers between devices: 26.2 us -> 74.5 us
  between operations: 14.9 us -> 0.66 us
  other arithmetic: 4.51 us -> 12 us
    psum x1 -> x0, waiting for transfers between devices: 140 us -> none  [broadcast(): return lax.psum(masked_stack(own_operator, owner), ('row', 'col'))]
    ppermute x0 -> x30, starting transfers between devices: none -> 49.8 us  [swap(): return lax.ppermute(block, ('row', 'col'), pairs)]
    ppermute x0 -> x30, waiting for transfers between devices: none -> 32.9 us  [swap(): return lax.ppermute(block, ('row', 'col'), pairs)]
    select_n x1 -> x41, other arithmetic: 1.87 us -> 10.5 us  [the longest x14 4.05 us: scatter_gather(): give = jnp.where(mine, low, high)]
    ppermute x4, starting transfers between devices: 17 us -> 14.6 us  [with_halo(): lax.ppermute(lax.slice_in_dim(block, block.shape[dim] - width, None, axis...]
    another operation x1 -> x0, other arithmetic: 2.36 us -> none  [masked_stack(): jnp.stack([jnp.where(me == owner[k], own_operator, jnp.zeros_like(own_ope...]
    dot_general x6 -> x18, matrix products: 6.77 us -> 5.77 us  [local(): jnp.dot(rows, part[k], preferred_element_type=jnp.float32)]
  transfers between devices with their start and end apart: 9 -> 38, of which waited for: 3 -> 18; matrix products, arithmetic and copies ran while one was open for 0% -> 7% of each run, Pallas kernels for 0% -> 0%
where the time goes in v2:
time: 133 us; the launch traced here: 131 us
  starting transfers between devices  74.5 us (56%)
  waiting for transfers between devices  36.1 us (27%)
  other arithmetic  12 us (9%)
  matrix products  5.77 us (4%)
  local copies, waits for them, and re-layouts  1.97 us (1%)
    ppermute x30, starting transfers between devices, swap(): return lax.ppermute(block, ('row', 'col'), pairs)  49.8 us
    ppermute x30, waiting for transfers between devices, swap(): return lax.ppermute(block, ('row', 'col'), pairs)  32.9 us
    ppermute x4, starting transfers between devices, with_halo(): lax.ppermute(lax.slice_in_dim(block, block.shape[dim] - width, None, axis...  14.6 us
    ppermute x4, starting transfers between devices, with_halo(): lax.ppermute(lax.slice_in_dim(block, 0, width, axis=dim), axis, backward)  10.1 us
    dot_general x18, matrix products, local(): jnp.dot(rows, part[k], preferred_element_type=jnp.float32)  5.77 us
    select_n x14, other arithmetic, scatter_gather(): give = jnp.where(mine, low, high)  4.05 us
    select_n x12, other arithmetic, scatter_gather(): block = jnp.where(have[:, None, None], keep, got)  3.93 us
    ppermute x4, waiting for transfers between devices, with_halo(): lax.ppermute(lax.slice_in_dim(block, 0, width, axis=dim), axis, backward)  3.17 us
  transfers between devices with their start and end apart: 38, of which 18 were waited for; matrix products, arithmetic and copies ran while one was open for 7% of the time, Pallas kernels for 0%

profile of v2, /device:TPU:9, one launch (start us, length us, event | category | flops | bytes accessed | tf_op | source)
XLA Modules:
  0.0 131.0 jit_solution(95569952969850353)
XLA Ops:
  0.0 2.3 %broadcast_select_fusion.2 = (bf16[2,512,256]{2,1,0:T(8,128)(2,1)}, bf16[2,512,256]{2,1,0:T(8,128)(2,1)S(1)}) fusion(pred[]{:T(512)S(6)} %eq.42, bf16[1,1024,1024]{2,1,0:T(8,128)(2,1)} %bitcast.76), kind=kLoop, calls=%fused_computation.59 | loop fusion | flops 2359296 | bytes 3145729 | tf_op jit(solution)/shard_map/jit(_where)/select_n | solution.py:60
  8.3 6.6 %collective-permute-done.21 = bf16[2,256,256]{2,1,0:T(8,128)(2,1)S(1)} collective-permute-done((bf16[2,256,256]{2,1,0:T(8,128)(2,1)S(1)}, bf16[2,256,256]{2,1,0:T(8,128)(2,1)S(1)}, u32[]{:S(2)}, u32[]{:S(2)}) %collective-permute-start.21) | collective-permute-done | bytes 262176 | tf_op jit(solution)/shard_map/ppermute | solution.py:49
  22.7 2.4 %collective-permute-start.24 = (bf16[2,32,256]{2,1,0:T(8,128)(2,1)S(1)}, bf16[2,32,256]{2,1,0:T(8,128)(2,1)S(1)}, u32[]{:S(2)}, u32[]{:S(2)}) collective-permute-start(bf16[2,32,256]{2,1,0:T(8,128)(2,1)S(1)} %broadcast_select_fusion.14), channel_id=1, source_target_pairs={{0,4},{1,5},{2,6},{3,7},{4,0},{5,1},{6,2},{7,3},{8,12},{9,13},{10,... | collective-permute-start | bytes 98312 | tf_op jit(solution)/shard_map/ppermute | solution.py:49
  26.5 2.7 %collective-permute-start.25 = (bf16[2,32,256]{2,1,0:T(8,128)(2,1)S(1)}, bf16[2,32,256]{2,1,0:T(8,128)(2,1)S(1)}, u32[]{:S(2)}, u32[]{:S(2)}) collective-permute-start(bf16[2,32,256]{2,1,0:T(8,128)(2,1)S(1)} %select_select_fusion.14), channel_id=1, source_target_pairs={{0,4},{1,5},{2,6},{3,7},{4,0},{5,1},{6,2},{7,3},{8,12},{9,13},{10,... | collective-permute-start | bytes 98312 | tf_op jit(solution)/shard_map/ppermute | solution.py:49
  29.2 3.6 %collective-permute-done.25 = bf16[2,32,256]{2,1,0:T(8,128)(2,1)S(1)} collective-permute-done((bf16[2,32,256]{2,1,0:T(8,128)(2,1)S(1)}, bf16[2,32,256]{2,1,0:T(8,128)(2,1)S(1)}, u32[]{:S(2)}, u32[]{:S(2)}) %collective-permute-start.25) | collective-permute-done | bytes 32800 | tf_op jit(solution)/shard_map/ppermute | solution.py:49
  35.8 2.4 %collective-permute-done.12 = bf16[2,128,384]{2,1,0:T(8,128)(2,1)S(1)} collective-permute-done((bf16[2,128,384]{2,1,0:T(8,128)(2,1)S(1)}, bf16[2,128,384]{2,1,0:T(8,128)(2,1)S(1)}, u32[]{:S(2)}, u32[]{:S(2)}) %collective-permute-start.12) | collective-permute-done | bytes 196640 | tf_op jit(solution)/shard_map/ppermute | solution.py:49
  42.0 2.9 %collective-permute-start.14 = (bf16[2,32,384]{2,1,0:T(8,128)(2,1)S(1)}, bf16[2,32,384]{2,1,0:T(8,128)(2,1)S(1)}, u32[]{:S(2)}, u32[]{:S(2)}) collective-permute-start(bf16[2,32,384]{2,1,0:T(8,128)(2,1)S(1)} %broadcast_select_fusion.12), channel_id=1, source_target_pairs={{0,4},{1,5},{2,6},{3,7},{4,0},{5,1},{6,2},{7,3},{8,12},{9,13},{10,... | collective-permute-start | bytes 147464 | tf_op jit(solution)/shard_map/ppermute | solution.py:49
  45.4 2.0 %collective-permute-start.4 = (bf16[2,32,384]{2,1,0:T(8,128)(2,1)S(1)}, bf16[2,32,384]{2,1,0:T(8,128)(2,1)S(1)}, u32[]{:S(2)}, u32[]{:S(2)}) collective-permute-start(bf16[2,32,384]{2,1,0:T(8,128)(2,1)S(1)} %broadcast_select_fusion.13), channel_id=1, source_target_pairs={{0,4},{1,5},{2,6},{3,7},{4,0},{5,1},{6,2},{7,3},{8,12},{9,13},{10,... | collective-permute-start | bytes 147464 | tf_op jit(solution)/shard_map/ppermute | solution.py:49
  49.4 2.5 %collective-permute-start.5 = (bf16[2,32,384]{2,1,0:T(8,128)(2,1)S(1)}, bf16[2,32,384]{2,1,0:T(8,128)(2,1)S(1)}, u32[]{:S(2)}, u32[]{:S(2)}) collective-permute-start(bf16[2,32,384]{2,1,0:T(8,128)(2,1)S(1)} %get-tuple-element.29), channel_id=1, source_target_pairs={{0,4},{1,5},{2,6},{3,7},{4,0},{5,1},{6,2},{7,3},{8,12},{9,13},{10,... | collective-permute-start | bytes 147464 | tf_op jit(solution)/shard_map/ppermute | solution.py:49
  56.2 2.6 %collective-permute-done.6 = bf16[2,64,384]{2,1,0:T(8,128)(2,1)S(1)} collective-permute-done((bf16[2,64,384]{2,1,0:T(8,128)(2,1)S(1)}, bf16[2,64,384]{2,1,0:T(8,128)(2,1)S(1)}, u32[]{:S(2)}, u32[]{:S(2)}) %collective-permute-start.6) | collective-permute-done | bytes 98336 | tf_op jit(solution)/shard_map/ppermute | solution.py:49
  59.1 12.6 %collective-permute-start.29 = (bf16[2,512,256]{2,1,0:T(8,128)(2,1)S(1)}, bf16[2,512,256]{2,1,0:T(8,128)(2,1)S(1)}, u32[]{:S(2)}, u32[]{:S(2)}) collective-permute-start(bf16[2,512,256]{2,1,0:T(8,128)(2,1)S(1)} %maximum_select_fusion.5), channel_id=1, source_target_pairs={{0,8},{1,9},{2,10},{3,11},{4,12},{5,13},{6,14},{7,15},{8,0},{9,1},... | collective-permute-start | bytes 1572872 | tf_op jit(solution)/shard_map/ppermute | solution.py:49
  73.4 2.7 %collective-permute-done.16 = bf16[2,64,384]{2,1,0:T(8,128)(2,1)S(1)} collective-permute-done((bf16[2,64,384]{2,1,0:T(8,128)(2,1)S(1)}, bf16[2,64,384]{2,1,0:T(8,128)(2,1)S(1)}, u32[]{:S(2)}, u32[]{:S(2)}) %collective-permute-start.16) | collective-permute-done | bytes 98336 | tf_op jit(solution)/shard_map/ppermute | solution.py:49
  77.5 4.0 %collective-permute-done.17 = bf16[2,128,384]{2,1,0:T(8,128)(2,1)S(1)} collective-permute-done((bf16[2,128,384]{2,1,0:T(8,128)(2,1)S(1)}, bf16[2,128,384]{2,1,0:T(8,128)(2,1)S(1)}, u32[]{:S(2)}, u32[]{:S(2)}) %collective-permute-start.17) | collective-permute-done | bytes 196640 | tf_op jit(solution)/shard_map/ppermute | solution.py:49
  82.6 3.1 %collective-permute-start.9 = (bf16[2,512,384]{2,1,0:T(8,128)(2,1)S(1)}, bf16[2,512,384]{2,1,0:T(8,128)(2,1)S(1)}, u32[]{:S(2)}, u32[]{:S(2)}) collective-permute-start(bf16[2,512,384]{2,1,0:T(8,128)(2,1)S(1)} %maximum_select_fusion.3), channel_id=1, source_target_pairs={{0,8},{1,9},{2,10},{3,11},{4,12},{5,13},{6,14},{7,15},{8,0},{9,1},... | collective-permute-start | bytes 2359304 | tf_op jit(solution)/shard_map/ppermute | solution.py:49
  86.4 3.7 %collective-permute-done.18 = bf16[2,256,384]{2,1,0:T(8,128)(2,1)S(1)} collective-permute-done((bf16[2,256,384]{2,1,0:T(8,128)(2,1)S(1)}, bf16[2,256,384]{2,1,0:T(8,128)(2,1)S(1)}, u32[]{:S(2)}, u32[]{:S(2)}) %collective-permute-start.18) | collective-permute-done | bytes 393248 | tf_op jit(solution)/shard_map/ppermute | solution.py:49
  90.4 3.1 %collective-permute-start.19 = (bf16[2,512,384]{2,1,0:T(8,128)(2,1)S(1)}, bf16[2,512,384]{2,1,0:T(8,128)(2,1)S(1)}, u32[]{:S(2)}, u32[]{:S(2)}) collective-permute-start(bf16[2,512,384]{2,1,0:T(8,128)(2,1)S(1)} %maximum_select_fusion.4), channel_id=1, source_target_pairs={{0,8},{1,9},{2,10},{3,11},{4,12},{5,13},{6,14},{7,15},{8,0},{9,1},... | collective-permute-start | bytes 2359304 | tf_op jit(solution)/shard_map/ppermute | solution.py:49
  98.1 3.4 %collective-permute-start.32 = (bf16[1,4,16,256]{3,2,1,0:T(8,128)(2,1)S(1)}, bf16[1,4,16,256]{3,2,1,0:T(8,128)(2,1)S(1)}, u32[]{:S(2)}, u32[]{:S(2)}) collective-permute-start(bf16[1,4,16,256]{3,2,1,0:T(8,128)(2,1)S(1)} %get-tuple-element.25), channel_id=1, source_target_pairs={{0,8},{8,16},{16,24},{1,9},{9,17},{17,25},{2,10},{10,18},{18,26},{... | collective-permute-start | bytes 98312 | tf_op jit(solution)/shard_map/ppermute | solution.py:15
  101.6 1.9 %collective-permute-start.33 = (bf16[1,4,16,256]{3,2,1,0:T(8,128)(2,1)S(1)}, bf16[1,4,16,256]{3,2,1,0:T(8,128)(2,1)S(1)}, u32[]{:S(2)}, u32[]{:S(2)}) collective-permute-start(bf16[1,4,16,256]{3,2,1,0:T(8,128)(2,1)S(1)} %get-tuple-element.26), channel_id=1, source_target_pairs={{8,0},{16,8},{24,16},{9,1},{17,9},{25,17},{10,2},{18,10},{26,18},{... | collective-permute-start | bytes 98312 | tf_op jit(solution)/shard_map/ppermute | solution.py:18
  103.5 2.2 %collective-permute-start.30 = (bf16[2,1,16,256]{3,2,1,0:T(8,128)(2,1)S(1)}, bf16[2,1,16,256]{3,2,1,0:T(8,128)(2,1)S(1)}, u32[]{:S(2)}, u32[]{:S(2)}) collective-permute-start(bf16[2,1,16,256]{3,2,1,0:T(8,128)(2,1)S(1)} %get-tuple-element.21), channel_id=1, source_target_pairs={{0,1},{1,2},{2,3},{3,4},{4,5},{5,6},{6,7},{8,9},{9,10},{10,11},{11... | collective-permute-start | bytes 49160 | tf_op jit(solution)/shard_map/ppermute | solution.py:15
  105.7 3.9 %collective-permute-start.31 = (bf16[2,1,16,256]{3,2,1,0:T(8,128)(2,1)S(1)}, bf16[2,1,16,256]{3,2,1,0:T(8,128)(2,1)S(1)}, u32[]{:S(2)}, u32[]{:S(2)}) collective-permute-start(bf16[2,1,16,256]{3,2,1,0:T(8,128)(2,1)S(1)} %get-tuple-element.22), channel_id=1, source_target_pairs={{1,0},{2,1},{3,2},{4,3},{5,4},{6,5},{7,6},{9,8},{10,9},{11,10},{12... | collective-permute-start | bytes 49160 | tf_op jit(solution)/shard_map/ppermute | solution.py:18
  112.9 4.5 %collective-permute-start.36 = (bf16[1,4,16,256]{3,2,1,0:T(8,128)(2,1)S(1)}, bf16[1,4,16,256]{3,2,1,0:T(8,128)(2,1)S(1)}, u32[]{:S(2)}, u32[]{:S(2)}) collective-permute-start(bf16[1,4,16,256]{3,2,1,0:T(8,128)(2,1)S(1)} %get-tuple-element.17), channel_id=1, source_target_pairs={{0,8},{8,16},{16,24},{1,9},{9,17},{17,25},{2,10},{10,18},{18,26},{... | collective-permute-start | bytes 98312 | tf_op jit(solution)/shard_map/ppermute | solution.py:15
  119.3 4.4 %collective-permute-start.34 = (bf16[2,1,16,256]{3,2,1,0:T(8,128)(2,1)S(1)}, bf16[2,1,16,256]{3,2,1,0:T(8,128)(2,1)S(1)}, u32[]{:S(2)}, u32[]{:S(2)}) collective-permute-start(bf16[2,1,16,256]{3,2,1,0:T(8,128)(2,1)S(1)} %get-tuple-element.13), channel_id=1, source_target_pairs={{0,1},{1,2},{2,3},{3,4},{4,5},{5,6},{6,7},{8,9},{9,10},{10,11},{11... | collective-permute-start | bytes 49160 | tf_op jit(solution)/shard_map/ppermute | solution.py:15
  123.7 2.4 %collective-permute-start.35 = (bf16[2,1,16,256]{3,2,1,0:T(8,128)(2,1)S(1)}, bf16[2,1,16,256]{3,2,1,0:T(8,128)(2,1)S(1)}, u32[]{:S(2)}, u32[]{:S(2)}) collective-permute-start(bf16[2,1,16,256]{3,2,1,0:T(8,128)(2,1)S(1)} %get-tuple-element.14), channel_id=1, source_target_pairs={{1,0},{2,1},{3,2},{4,3},{5,4},{6,5},{7,6},{9,8},{10,9},{11,10},{12... | collective-permute-start | bytes 49160 | tf_op jit(solution)/shard_map/ppermute | solution.py:18
  126.1 2.1 %collective-permute-done.35 = bf16[2,1,16,256]{3,2,1,0:T(8,128)(2,1)S(1)} collective-permute-done((bf16[2,1,16,256]{3,2,1,0:T(8,128)(2,1)S(1)}, bf16[2,1,16,256]{3,2,1,0:T(8,128)(2,1)S(1)}, u32[]{:S(2)}, u32[]{:S(2)}) %collective-permute-start.35) | collective-permute-done | bytes 16416 | tf_op jit(solution)/shard_map/ppermute | solution.py:18
  (159 shorter events, 46.4 us)
Async XLA Ops:
  4.5 11.9 %collective-permute-start = (bf16[2,512,384]{2,1,0:T(8,128)(2,1)}, bf16[2,512,384]{2,1,0:T(8,128)(2,1)}, u32[]{:S(2)}, u32[]{:S(2)}) collective-permute-start(bf16[2,512,384]{2,1,0:T(8,128)(2,1)} %get-tuple-element.11), channel_id=1, source_target_pairs={{0,8},{1,9},{2,10},{3,11},{4,12},{5,13},{6,14},{7,15},{8,0},{9,1},... | collective-permute-start | bytes 2359304 | tf_op jit(solution)/shard_map/ppermute | solution.py:49
  4.5 11.9 %collective-permute-start.10 = (bf16[2,512,384]{2,1,0:T(8,128)(2,1)}, bf16[2,512,384]{2,1,0:T(8,128)(2,1)}, u32[]{:S(2)}, u32[]{:S(2)}) collective-permute-start(bf16[2,512,384]{2,1,0:T(8,128)(2,1)} %get-tuple-element.12), channel_id=1, source_target_pairs={{0,8},{1,9},{2,10},{3,11},{4,12},{5,13},{6,14},{7,15},{8,0},{9,1},... | collective-permute-start | bytes 2359304 | tf_op jit(solution)/shard_map/ppermute | solution.py:49
  7.0 8.0 %collective-permute-start.21 = (bf16[2,256,256]{2,1,0:T(8,128)(2,1)S(1)}, bf16[2,256,256]{2,1,0:T(8,128)(2,1)S(1)}, u32[]{:S(2)}, u32[]{:S(2)}) collective-permute-start(bf16[2,256,256]{2,1,0:T(8,128)(2,1)S(1)} %broadcast_select_fusion.5), channel_id=1, source_target_pairs={{0,16},{1,17},{2,18},{3,19},{4,20},{5,21},{6,22},{7,23},{8,24},{9,... | collective-permute-start | bytes 786440 | tf_op jit(solution)/shard_map/ppermute | solution.py:49
  19.9 13.5 %collective-permute-start.1 = (bf16[2,256,384]{2,1,0:T(8,128)(2,1)S(1)}, bf16[2,256,384]{2,1,0:T(8,128)(2,1)S(1)}, u32[]{:S(2)}, u32[]{:S(2)}) collective-permute-start(bf16[2,256,384]{2,1,0:T(8,128)(2,1)S(1)} %broadcast_select_fusion.3), channel_id=1, source_target_pairs={{0,1},{1,0},{2,3},{3,2},{4,5},{5,4},{6,7},{7,6},{8,9},{9,8},{10,11... | collective-permute-start | bytes 1179656 | tf_op jit(solution)/shard_map/ppermute | solution.py:49
  25.1 8.3 %collective-permute-start.11 = (bf16[2,256,384]{2,1,0:T(8,128)(2,1)S(1)}, bf16[2,256,384]{2,1,0:T(8,128)(2,1)S(1)}, u32[]{:S(2)}, u32[]{:S(2)}) collective-permute-start(bf16[2,256,384]{2,1,0:T(8,128)(2,1)S(1)} %broadcast_select_fusion.4), channel_id=1, source_target_pairs={{0,2},{1,3},{2,0},{3,1},{4,6},{5,7},{6,4},{7,5},{8,10},{9,11},{10,... | collective-permute-start | bytes 1179656 | tf_op jit(solution)/shard_map/ppermute | solution.py:49
  26.5 6.2 %collective-permute-start.25 = (bf16[2,32,256]{2,1,0:T(8,128)(2,1)S(1)}, bf16[2,32,256]{2,1,0:T(8,128)(2,1)S(1)}, u32[]{:S(2)}, u32[]{:S(2)}) collective-permute-start(bf16[2,32,256]{2,1,0:T(8,128)(2,1)S(1)} %select_select_fusion.14), channel_id=1, source_target_pairs={{0,4},{1,5},{2,6},{3,7},{4,0},{5,1},{6,2},{7,3},{8,12},{9,13},{10,... | collective-permute-start | bytes 98312 | tf_op jit(solution)/shard_map/ppermute | solution.py:49
  32.8 14.6 %collective-permute-start.26 = (bf16[2,64,256]{2,1,0:T(8,128)(2,1)S(1)}, bf16[2,64,256]{2,1,0:T(8,128)(2,1)S(1)}, u32[]{:S(2)}, u32[]{:S(2)}) collective-permute-start(bf16[2,64,256]{2,1,0:T(8,128)(2,1)S(1)} %maximum_select_fusion.14), channel_id=1, source_target_pairs={{0,2},{1,3},{2,0},{3,1},{4,6},{5,7},{6,4},{7,5},{8,10},{9,11},{10,... | collective-permute-start | bytes 196616 | tf_op jit(solution)/shard_map/ppermute | solution.py:49
  35.0 5.4 %collective-permute-start.2 = (bf16[2,128,384]{2,1,0:T(8,128)(2,1)S(1)}, bf16[2,128,384]{2,1,0:T(8,128)(2,1)S(1)}, u32[]{:S(2)}, u32[]{:S(2)}) collective-permute-start(bf16[2,128,384]{2,1,0:T(8,128)(2,1)S(1)} %broadcast_select_fusion.6), channel_id=1, source_target_pairs={{0,2},{1,3},{2,0},{3,1},{4,6},{5,7},{6,4},{7,5},{8,10},{9,11},{10,... | collective-permute-start | bytes 589832 | tf_op jit(solution)/shard_map/ppermute | solution.py:49
  42.0 6.6 %collective-permute-start.14 = (bf16[2,32,384]{2,1,0:T(8,128)(2,1)S(1)}, bf16[2,32,384]{2,1,0:T(8,128)(2,1)S(1)}, u32[]{:S(2)}, u32[]{:S(2)}) collective-permute-start(bf16[2,32,384]{2,1,0:T(8,128)(2,1)S(1)} %broadcast_select_fusion.12), channel_id=1, source_target_pairs={{0,4},{1,5},{2,6},{3,7},{4,0},{5,1},{6,2},{7,3},{8,12},{9,13},{10,... | collective-permute-start | bytes 147464 | tf_op jit(solution)/shard_map/ppermute | solution.py:49
  52.0 6.8 %collective-permute-start.28 = (bf16[2,256,256]{2,1,0:T(8,128)(2,1)S(1)}, bf16[2,256,256]{2,1,0:T(8,128)(2,1)S(1)}, u32[]{:S(2)}, u32[]{:S(2)}) collective-permute-start(bf16[2,256,256]{2,1,0:T(8,128)(2,1)S(1)} %maximum_select_fusion.8), channel_id=1, source_target_pairs={{0,16},{1,17},{2,18},{3,19},{4,20},{5,21},{6,22},{7,23},{8,24},{9,... | collective-permute-start | bytes 786440 | tf_op jit(solution)/shard_map/ppermute | solution.py:49
  53.6 5.1 %collective-permute-start.6 = (bf16[2,64,384]{2,1,0:T(8,128)(2,1)S(1)}, bf16[2,64,384]{2,1,0:T(8,128)(2,1)S(1)}, u32[]{:S(2)}, u32[]{:S(2)}) collective-permute-start(bf16[2,64,384]{2,1,0:T(8,128)(2,1)S(1)} %maximum_select_fusion.12), channel_id=1, source_target_pairs={{0,16},{1,17},{2,18},{3,19},{4,20},{5,21},{6,22},{7,23},{8,24},{9,... | collective-permute-start | bytes 294920 | tf_op jit(solution)/shard_map/ppermute | solution.py:49
  54.3 17.4 %collective-permute-start.15 = (bf16[2,32,384]{2,1,0:T(8,128)(2,1)S(1)}, bf16[2,32,384]{2,1,0:T(8,128)(2,1)S(1)}, u32[]{:S(2)}, u32[]{:S(2)}) collective-permute-start(bf16[2,32,384]{2,1,0:T(8,128)(2,1)S(1)} %get-tuple-element.30), channel_id=1, source_target_pairs={{0,4},{1,5},{2,6},{3,7},{4,0},{5,1},{6,2},{7,3},{8,12},{9,13},{10,... | collective-permute-start | bytes 147464 | tf_op jit(solution)/shard_map/ppermute | solution.py:49
  58.8 14.2 %collective-permute-start.7 = (bf16[2,128,384]{2,1,0:T(8,128)(2,1)S(1)}, bf16[2,128,384]{2,1,0:T(8,128)(2,1)S(1)}, u32[]{:S(2)}, u32[]{:S(2)}) collective-permute-start(bf16[2,128,384]{2,1,0:T(8,128)(2,1)S(1)} %maximum_select_fusion.9), channel_id=1, source_target_pairs={{0,2},{1,3},{2,0},{3,1},{4,6},{5,7},{6,4},{7,5},{8,10},{9,11},{10,... | collective-permute-start | bytes 589832 | tf_op jit(solution)/shard_map/ppermute | solution.py:49
  59.1 26.7 %collective-permute-start.29 = (bf16[2,512,256]{2,1,0:T(8,128)(2,1)S(1)}, bf16[2,512,256]{2,1,0:T(8,128)(2,1)S(1)}, u32[]{:S(2)}, u32[]{:S(2)}) collective-permute-start(bf16[2,512,256]{2,1,0:T(8,128)(2,1)S(1)} %maximum_select_fusion.5), channel_id=1, source_target_pairs={{0,8},{1,9},{2,10},{3,11},{4,12},{5,13},{6,14},{7,15},{8,0},{9,1},... | collective-permute-start | bytes 1572872 | tf_op jit(solution)/shard_map/ppermute | solution.py:49
  73.1 9.2 %collective-permute-start.8 = (bf16[2,256,384]{2,1,0:T(8,128)(2,1)S(1)}, bf16[2,256,384]{2,1,0:T(8,128)(2,1)S(1)}, u32[]{:S(2)}, u32[]{:S(2)}) collective-permute-start(bf16[2,256,384]{2,1,0:T(8,128)(2,1)S(1)} %maximum_select_fusion.6), channel_id=1, source_target_pairs={{0,1},{1,0},{2,3},{3,2},{4,5},{5,4},{6,7},{7,6},{8,9},{9,8},{10,11... | collective-permute-start | bytes 1179656 | tf_op jit(solution)/shard_map/ppermute | solution.py:49
  76.2 5.2 %collective-permute-start.17 = (bf16[2,128,384]{2,1,0:T(8,128)(2,1)S(1)}, bf16[2,128,384]{2,1,0:T(8,128)(2,1)S(1)}, u32[]{:S(2)}, u32[]{:S(2)}) collective-permute-start(bf16[2,128,384]{2,1,0:T(8,128)(2,1)S(1)} %maximum_select_fusion.10), channel_id=1, source_target_pairs={{0,16},{1,17},{2,18},{3,19},{4,20},{5,21},{6,22},{7,23},{8,24},{9,... | collective-permute-start | bytes 589832 | tf_op jit(solution)/shard_map/ppermute | solution.py:49
  81.6 8.5 %collective-permute-start.18 = (bf16[2,256,384]{2,1,0:T(8,128)(2,1)S(1)}, bf16[2,256,384]{2,1,0:T(8,128)(2,1)S(1)}, u32[]{:S(2)}, u32[]{:S(2)}) collective-permute-start(bf16[2,256,384]{2,1,0:T(8,128)(2,1)S(1)} %maximum_select_fusion.7), channel_id=1, source_target_pairs={{0,2},{1,3},{2,0},{3,1},{4,6},{5,7},{6,4},{7,5},{8,10},{9,11},{10,... | collective-permute-start | bytes 1179656 | tf_op jit(solution)/shard_map/ppermute | solution.py:49
  82.6 11.2 %collective-permute-start.9 = (bf16[2,512,384]{2,1,0:T(8,128)(2,1)S(1)}, bf16[2,512,384]{2,1,0:T(8,128)(2,1)S(1)}, u32[]{:S(2)}, u32[]{:S(2)}) collective-permute-start(bf16[2,512,384]{2,1,0:T(8,128)(2,1)S(1)} %maximum_select_fusion.3), channel_id=1, source_target_pairs={{0,8},{1,9},{2,10},{3,11},{4,12},{5,13},{6,14},{7,15},{8,0},{9,1},... | collective-permute-start | bytes 2359304 | tf_op jit(solution)/shard_map/ppermute | solution.py:49
  98.1 12.7 %collective-permute-start.32 = (bf16[1,4,16,256]{3,2,1,0:T(8,128)(2,1)S(1)}, bf16[1,4,16,256]{3,2,1,0:T(8,128)(2,1)S(1)}, u32[]{:S(2)}, u32[]{:S(2)}) collective-permute-start(bf16[1,4,16,256]{3,2,1,0:T(8,128)(2,1)S(1)} %get-tuple-element.25), channel_id=1, source_target_pairs={{0,8},{8,16},{16,24},{1,9},{9,17},{17,25},{2,10},{10,18},{18,26},{... | collective-permute-start | bytes 98312 | tf_op jit(solution)/shard_map/ppermute | solution.py:15
  101.6 9.2 %collective-permute-start.33 = (bf16[1,4,16,256]{3,2,1,0:T(8,128)(2,1)S(1)}, bf16[1,4,16,256]{3,2,1,0:T(8,128)(2,1)S(1)}, u32[]{:S(2)}, u32[]{:S(2)}) collective-permute-start(bf16[1,4,16,256]{3,2,1,0:T(8,128)(2,1)S(1)} %get-tuple-element.26), channel_id=1, source_target_pairs={{8,0},{16,8},{24,16},{9,1},{17,9},{25,17},{10,2},{18,10},{26,18},{... | collective-permute-start | bytes 98312 | tf_op jit(solution)/shard_map/ppermute | solution.py:18
  103.5 6.2 %collective-permute-start.30 = (bf16[2,1,16,256]{3,2,1,0:T(8,128)(2,1)S(1)}, bf16[2,1,16,256]{3,2,1,0:T(8,128)(2,1)S(1)}, u32[]{:S(2)}, u32[]{:S(2)}) collective-permute-start(bf16[2,1,16,256]{3,2,1,0:T(8,128)(2,1)S(1)} %get-tuple-element.21), channel_id=1, source_target_pairs={{0,1},{1,2},{2,3},{3,4},{4,5},{5,6},{6,7},{8,9},{9,10},{10,11},{11... | collective-permute-start | bytes 49160 | tf_op jit(solution)/shard_map/ppermute | solution.py:15
  112.9 15.4 %collective-permute-start.36 = (bf16[1,4,16,256]{3,2,1,0:T(8,128)(2,1)S(1)}, bf16[1,4,16,256]{3,2,1,0:T(8,128)(2,1)S(1)}, u32[]{:S(2)}, u32[]{:S(2)}) collective-permute-start(bf16[1,4,16,256]{3,2,1,0:T(8,128)(2,1)S(1)} %get-tuple-element.17), channel_id=1, source_target_pairs={{0,8},{8,16},{16,24},{1,9},{9,17},{17,25},{2,10},{10,18},{18,26},{... | collective-permute-start | bytes 98312 | tf_op jit(solution)/shard_map/ppermute | solution.py:15
  117.4 10.8 %collective-permute-start.37 = (bf16[1,4,16,256]{3,2,1,0:T(8,128)(2,1)S(1)}, bf16[1,4,16,256]{3,2,1,0:T(8,128)(2,1)S(1)}, u32[]{:S(2)}, u32[]{:S(2)}) collective-permute-start(bf16[1,4,16,256]{3,2,1,0:T(8,128)(2,1)S(1)} %get-tuple-element.18), channel_id=1, source_target_pairs={{8,0},{16,8},{24,16},{9,1},{17,9},{25,17},{10,2},{18,10},{26,18},{... | collective-permute-start | bytes 98312 | tf_op jit(solution)/shard_map/ppermute | solution.py:18
  119.3 6.8 %collective-permute-start.34 = (bf16[2,1,16,256]{3,2,1,0:T(8,128)(2,1)S(1)}, bf16[2,1,16,256]{3,2,1,0:T(8,128)(2,1)S(1)}, u32[]{:S(2)}, u32[]{:S(2)}) collective-permute-start(bf16[2,1,16,256]{3,2,1,0:T(8,128)(2,1)S(1)} %get-tuple-element.13), channel_id=1, source_target_pairs={{0,1},{1,2},{2,3},{3,4},{4,5},{5,6},{6,7},{8,9},{9,10},{10,11},{11... | collective-permute-start | bytes 49160 | tf_op jit(solution)/shard_map/ppermute | solution.py:15
  (25 other events, 219.0 us)

commit v3 on v2

--- a/solution.py
+++ b/solution.py
@@ -100,33 +100,98 @@
     return parts
 
 
+def sweep(traces, kinds, ids, parts, port_cell, excite):
+    count, port_count, order = traces.shape
+    rows = traces.reshape(count * port_count, order)
+    products = [
+        jnp.concatenate(
+            [jnp.dot(rows, part[k], preferred_element_type=jnp.float32) for part in parts], axis=-1
+        ).reshape(count, port_count, order)
+        for k in range(TYPES)
+    ]
+    chosen = products[0]
+    for k in range(1, TYPES):
+        chosen = jnp.where((kinds == k)[:, None, None], products[k], chosen)
+    port_hits = (ids[:, None] == port_cell[None, :]).astype(jnp.float32)
+    source = port_hits[..., None] * excite[None]
+    return (chosen + source).astype(jnp.bfloat16)
+
+
+def shift(block, axis, step):
+    count = lax.axis_size(axis)
+    if step > 0:
+        pairs = [(i, i + 1) for i in range(count - 1)]
+    else:
+        pairs = [(i + 1, i) for i in range(count - 1)]
+    return lax.ppermute(block, axis, pairs)
+
+
 def local(incoming, cell_type, bank, owner, port_cell, excite):
     cell_rows, cell_cols, port_count, order = incoming.shape
     col_count = lax.axis_size("col")
+    row_count = lax.axis_size("row")
+    row_at = lax.axis_index("row")
+    col_at = lax.axis_index("col")
+    width = cell_cols * col_count
+    face = order // 4
+    tagged = jnp.concatenate(
+        [incoming, jnp.broadcast_to(cell_type.astype(incoming.dtype)[:, :, None, None], (cell_rows, cell_cols, port_count, 128))],
+        axis=-1,
+    )
+    from_west = shift(tagged[:, -1], "col", 1)
+    from_east = shift(tagged[:, 0], "col", -1)
+    from_north = shift(tagged[-1], "row", 1)
+    from_south = shift(tagged[0], "row", -1)
     parts = broadcast_parts(bank[0, 0], owner)
-    row_ids = lax.axis_index("row") * cell_rows + jnp.arange(cell_rows, dtype=jnp.int32)
-    col_ids = lax.axis_index("col") * cell_cols + jnp.arange(cell_cols, dtype=jnp.int32)
-    flat_ids = row_ids[:, None] * (cell_cols * col_count) + col_ids[None, :]
-    port_hits = (flat_ids[:, :, None] == port_cell[None, None, :]).astype(jnp.float32)
-    source = port_hits[..., None] * excite[None, None]
-    kinds = cell_type[:, :, None, None]
-    traces = incoming
-    outgoing = incoming
-    for sweep_id in range(SWEEPS):
-        rows = traces.reshape(cell_rows * cell_cols * port_count, order)
-        products = [
-            jnp.concatenate(
-                [jnp.dot(rows, part[k], preferred_element_type=jnp.float32) for part in parts], axis=-1
-            ).reshape(cell_rows, cell_cols, port_count, order)
-            for k in range(TYPES)
+    row_ids = row_at * cell_rows + jnp.arange(cell_rows, dtype=jnp.int32)
+    col_ids = col_at * cell_cols + jnp.arange(cell_cols, dtype=jnp.int32)
+    flat_ids = (row_ids[:, None] * width + col_ids[None, :]).reshape(-1)
+    ghost = jnp.concatenate([from_west, from_east, from_north, from_south], axis=0)
+    ghost_ids = jnp.concatenate(
+        [
+            row_ids * width + col_at * cell_cols - 1,
+            row_ids * width + (col_at + 1) * cell_cols,
+            (row_at * cell_rows - 1) * width + col_ids,
+            ((row_at + 1) * cell_rows) * width + col_ids,
         ]
-        chosen = products[0]
-        for k in range(1, TYPES):
-            chosen = jnp.where(kinds == k, products[k], chosen)
-        outgoing = (chosen + source).astype(jnp.bfloat16)
+    )
+    cell_count = cell_rows * cell_cols
+    all_traces = jnp.concatenate([incoming.reshape(cell_count, port_count, order), ghost[:, :, :order]], axis=0)
+    all_kinds = jnp.concatenate([cell_type.reshape(-1), ghost[:, 0, order].astype(jnp.int32)])
+    all_ids = jnp.concatenate([flat_ids, ghost_ids])
+    first = sweep(all_traces, all_kinds, all_ids, parts, port_cell, excite)
+    outgoing = first[:cell_count].reshape(cell_rows, cell_cols, port_count, order)
+    ghost_out = first[cell_count:]
+    zero = jnp.zeros_like(ghost_out[:cell_rows, :, :face])
+    west_in = jnp.where(col_at > 0, ghost_out[:cell_rows, :, face : 2 * face], zero)
+    east_in = jnp.where(col_at < col_count - 1, ghost_out[cell_rows : 2 * cell_rows, :, :face], zero)
+    zero = jnp.zeros_like(ghost_out[:cell_cols, :, :face])
+    at = 2 * cell_rows
+    north_in = jnp.where(row_at > 0, ghost_out[at : at + cell_cols, :, 3 * face :], zero)
+    south_in = jnp.where(
+        row_at < row_count - 1, ghost_out[at + cell_cols : at + 2 * cell_cols, :, 2 * face : 3 * face], zero
+    )
+    traces = assemble(outgoing, west_in, east_in, north_in, south_in)
+    kinds = cell_type.reshape(-1)
+    for sweep_id in range(1, SWEEPS):
+        outgoing = sweep(traces.reshape(cell_count, port_count, order), kinds, flat_ids, parts, port_cell, excite)
+        outgoing = outgoing.reshape(cell_rows, cell_cols, port_count, order)
         if sweep_id + 1 < SWEEPS:
             traces = pass_traces(outgoing)
     return outgoing
+
+
+def assemble(outgoing, west_in, east_in, north_in, south_in):
+    face_len = outgoing.shape[-1] // 4
+    west_face = outgoing[..., :face_len]
+    east_face = outgoing[..., face_len : 2 * face_len]
+    north_face = outgoing[..., 2 * face_len : 3 * face_len]
+    south_face = outgoing[..., 3 * face_len :]
+    new_west = jnp.concatenate([west_in[:, None], east_face[:, :-1]], axis=1)
+    new_east = jnp.concatenate([west_face[:, 1:], east_in[:, None]], axis=1)
+    new_north = jnp.concatenate([north_in[None], south_face[:-1]], axis=0)
+    new_south = jnp.concatenate([north_face[1:], south_in[None]], axis=0)
+    return jnp.concatenate([new_west, new_east, new_north, new_south], axis=-1)
 
 
 def solution(mesh):

time: 133 us -> 139 us (1.045)
  other arithmetic: 12 us -> 18.3 us
  local copies, waits for them, and re-layouts: 1.97 us -> 5.35 us
  waiting for transfers between devices: 36.1 us -> 33.3 us
    ppermute x0 -> x4, starting transfers between devices: none -> 11.4 us  [shift(): return lax.ppermute(block, axis, pairs)]
    ppermute x4 -> x2, starting transfers between devices: 14.6 us -> 6.39 us  [with_halo(): lax.ppermute(lax.slice_in_dim(block, block.shape[dim] - width, None, axis...]
    ppermute x4 -> x2, starting transfers between devices: 10.1 us -> 6.04 us  [with_halo(): lax.ppermute(lax.slice_in_dim(block, 0, width, axis=dim), axis, backward)]
    squeeze x0 -> x2, other arithmetic: none -> 3.27 us  [the longest x1 1.71 us: local(): from_south = shift(tagged[0], 'row', -1)]
    ppermute x30, waiting for transfers between devices: 32.9 us -> 30 us  [swap(): return lax.ppermute(block, ('row', 'col'), pairs)]
    unnamed x22 -> x41, local copies, waits for them, and re-layouts: 1.53 us -> 3.72 us
    convert_element_type x4 -> x6, other arithmetic: 1.17 us -> 3.27 us  [the longest x2 1.33 us: sweep(): port_hits = (ids[:, None] == port_cell[None, :]).astype(jnp.float32)]
    ppermute x4 -> x2, waiting for transfers between devices: 3.17 us -> 3.26 us  [with_halo(): lax.ppermute(lax.slice_in_dim(block, 0, width, axis=dim), axis, backward)]
  transfers between devices with their start and end apart: 38 -> 38, of which waited for: 18 -> 16; matrix products, arithmetic and copies ran while one was open for 7% -> 14% of each run, Pallas kernels for 0% -> 0%
where the time goes in v3:
time: 139 us; the launch traced here: 138 us
  starting transfers between devices  74.4 us (54%)
  waiting for transfers between devices  33.3 us (24%)
  other arithmetic  18.3 us (13%)
  matrix products  6.01 us (4%)
  local copies, waits for them, and re-layouts  5.35 us (4%)
    ppermute x30, starting transfers between devices, swap(): return lax.ppermute(block, ('row', 'col'), pairs)  50.6 us
    ppermute x30, waiting for transfers between devices, swap(): return lax.ppermute(block, ('row', 'col'), pairs)  30 us
    ppermute x4, starting transfers between devices, shift(): return lax.ppermute(block, axis, pairs)  11.4 us
    ppermute x2, starting transfers between devices, with_halo(): lax.ppermute(lax.slice_in_dim(block, block.shape[dim] - width, None, axis...  6.39 us
    ppermute x2, starting transfers between devices, with_halo(): lax.ppermute(lax.slice_in_dim(block, 0, width, axis=dim), axis, backward)  6.04 us
    dot_general x18, matrix products, sweep(): jnp.dot(rows, part[k], preferred_element_type=jnp.float32)  6.01 us
    select_n x14, other arithmetic, scatter_gather(): give = jnp.where(mine, low, high)  3.81 us
    unnamed x41, local copies, waits for them, and re-layouts  3.72 us
  transfers between devices with their start and end apart: 38, of which 16 were waited for; matrix products, arithmetic and copies ran while one was open for 14% of the time, Pallas kernels for 0%

profile of v3, /device:TPU:9, one launch (start us, length us, event | category | flops | bytes accessed | tf_op | source)
XLA Modules:
  0.0 138.2 jit_solution(5017334877104515996)
XLA Ops:
  2.3 3.0 %collective-permute-start.1 = (bf16[2,16,1152]{2,1,0:T(8,128)(2,1)}, bf16[2,16,1152]{2,1,0:T(8,128)(2,1)}, u32[]{:S(2)}, u32[]{:S(2)}) collective-permute-start(bf16[2,16,1152]{2,1,0:T(8,128)(2,1)} %get-tuple-element.19), channel_id=1, source_target_pairs={{1,0},{2,1},{3,2},{4,3},{5,4},{6,5},{7,6},{9,8},{10,9},{11,10},{12... | collective-permute-start | bytes 221192 | tf_op jit(solution)/shard_map/ppermute | solution.py:126
  5.3 2.3 %collective-permute-start = (bf16[2,16,1152]{2,1,0:T(8,128)(2,1)}, bf16[2,16,1152]{2,1,0:T(8,128)(2,1)}, u32[]{:S(2)}, u32[]{:S(2)}) collective-permute-start(bf16[2,16,1152]{2,1,0:T(8,128)(2,1)} %get-tuple-element.20), channel_id=1, source_target_pairs={{0,1},{1,2},{2,3},{3,4},{4,5},{5,6},{6,7},{8,9},{9,10},{10,11},{11... | collective-permute-start | bytes 221192 | tf_op jit(solution)/shard_map/ppermute | solution.py:126
  9.3 3.1 %collective-permute-start.3 = (bf16[4,16,1152]{2,1,0:T(8,128)(2,1)}, bf16[4,16,1152]{2,1,0:T(8,128)(2,1)S(1)}, u32[]{:S(2)}, u32[]{:S(2)}) collective-permute-start(bf16[4,16,1152]{2,1,0:T(8,128)(2,1)} %get-tuple-element.17), channel_id=1, source_target_pairs={{8,0},{16,8},{24,16},{9,1},{17,9},{25,17},{10,2},{18,10},{26,18},{... | collective-permute-start | bytes 442376 | tf_op jit(solution)/shard_map/ppermute | solution.py:126
  12.5 3.0 %collective-permute-start.2 = (bf16[4,16,1152]{2,1,0:T(8,128)(2,1)}, bf16[4,16,1152]{2,1,0:T(8,128)(2,1)}, u32[]{:S(2)}, u32[]{:S(2)}) collective-permute-start(bf16[4,16,1152]{2,1,0:T(8,128)(2,1)} %get-tuple-element.18), channel_id=1, source_target_pairs={{0,8},{8,16},{16,24},{1,9},{9,17},{17,25},{2,10},{10,18},{18,26},{... | collective-permute-start | bytes 442376 | tf_op jit(solution)/shard_map/ppermute | solution.py:126
  15.6 2.3 %broadcast_select_fusion.2 = (bf16[2,512,256]{2,1,0:T(8,128)(2,1)}, bf16[2,512,256]{2,1,0:T(8,128)(2,1)S(1)}) fusion(pred[]{:T(512)S(6)} %eq.62, bf16[1,1024,1024]{2,1,0:T(8,128)(2,1)} %bitcast.82), kind=kLoop, calls=%fused_computation.57 | loop fusion | flops 2359296 | bytes 3145729 | tf_op jit(solution)/shard_map/jit(_where)/select_n | solution.py:60
  29.0 5.0 %collective-permute-done.25 = bf16[2,256,256]{2,1,0:T(8,128)(2,1)S(1)} collective-permute-done((bf16[2,256,256]{2,1,0:T(8,128)(2,1)S(1)}, bf16[2,256,256]{2,1,0:T(8,128)(2,1)S(1)}, u32[]{:S(2)}, u32[]{:S(2)}) %collective-permute-start.25) | collective-permute-done | bytes 262176 | tf_op jit(solution)/shard_map/ppermute | solution.py:49
  39.1 2.9 %collective-permute-done.27 = bf16[2,64,256]{2,1,0:T(8,128)(2,1)S(1)} collective-permute-done((bf16[2,64,256]{2,1,0:T(8,128)(2,1)S(1)}, bf16[2,64,256]{2,1,0:T(8,128)(2,1)S(1)}, u32[]{:S(2)}, u32[]{:S(2)}) %collective-permute-start.27) | collective-permute-done | bytes 65568 | tf_op jit(solution)/shard_map/ppermute | solution.py:49
  42.1 2.3 %collective-permute-start.28 = (bf16[2,32,256]{2,1,0:T(8,128)(2,1)S(1)}, bf16[2,32,256]{2,1,0:T(8,128)(2,1)S(1)}, u32[]{:S(2)}, u32[]{:S(2)}) collective-permute-start(bf16[2,32,256]{2,1,0:T(8,128)(2,1)S(1)} %broadcast_select_fusion.14), channel_id=1, source_target_pairs={{0,4},{1,5},{2,6},{3,7},{4,0},{5,1},{6,2},{7,3},{8,12},{9,13},{10,... | collective-permute-start | bytes 98312 | tf_op jit(solution)/shard_map/ppermute | solution.py:49
  46.3 2.3 %collective-permute-start.29 = (bf16[2,32,256]{2,1,0:T(8,128)(2,1)S(1)}, bf16[2,32,256]{2,1,0:T(8,128)(2,1)S(1)}, u32[]{:S(2)}, u32[]{:S(2)}) collective-permute-start(bf16[2,32,256]{2,1,0:T(8,128)(2,1)S(1)} %select_select_fusion.14), channel_id=1, source_target_pairs={{0,4},{1,5},{2,6},{3,7},{4,0},{5,1},{6,2},{7,3},{8,12},{9,13},{10,... | collective-permute-start | bytes 98312 | tf_op jit(solution)/shard_map/ppermute | solution.py:49
  48.6 3.1 %collective-permute-done.29 = bf16[2,32,256]{2,1,0:T(8,128)(2,1)S(1)} collective-permute-done((bf16[2,32,256]{2,1,0:T(8,128)(2,1)S(1)}, bf16[2,32,256]{2,1,0:T(8,128)(2,1)S(1)}, u32[]{:S(2)}, u32[]{:S(2)}) %collective-permute-start.29) | collective-permute-done | bytes 32800 | tf_op jit(solution)/shard_map/ppermute | solution.py:49
  52.1 2.5 %collective-permute-start.16 = (bf16[2,128,384]{2,1,0:T(8,128)(2,1)S(1)}, bf16[2,128,384]{2,1,0:T(8,128)(2,1)S(1)}, u32[]{:S(2)}, u32[]{:S(2)}) collective-permute-start(bf16[2,128,384]{2,1,0:T(8,128)(2,1)S(1)} %broadcast_select_fusion.7), channel_id=1, source_target_pairs={{0,16},{1,17},{2,18},{3,19},{4,20},{5,21},{6,22},{7,23},{8,24},{9,... | collective-permute-start | bytes 589832 | tf_op jit(solution)/shard_map/ppermute | solution.py:49
  61.7 2.9 %collective-permute-start.18 = (bf16[2,32,384]{2,1,0:T(8,128)(2,1)S(1)}, bf16[2,32,384]{2,1,0:T(8,128)(2,1)S(1)}, u32[]{:S(2)}, u32[]{:S(2)}) collective-permute-start(bf16[2,32,384]{2,1,0:T(8,128)(2,1)S(1)} %broadcast_select_fusion.12), channel_id=1, source_target_pairs={{0,4},{1,5},{2,6},{3,7},{4,0},{5,1},{6,2},{7,3},{8,12},{9,13},{10,... | collective-permute-start | bytes 147464 | tf_op jit(solution)/shard_map/ppermute | solution.py:49
  64.7 3.0 %collective-permute-start.8 = (bf16[2,32,384]{2,1,0:T(8,128)(2,1)S(1)}, bf16[2,32,384]{2,1,0:T(8,128)(2,1)S(1)}, u32[]{:S(2)}, u32[]{:S(2)}) collective-permute-start(bf16[2,32,384]{2,1,0:T(8,128)(2,1)S(1)} %broadcast_select_fusion.13), channel_id=1, source_target_pairs={{0,4},{1,5},{2,6},{3,7},{4,0},{5,1},{6,2},{7,3},{8,12},{9,13},{10,... | collective-permute-start | bytes 147464 | tf_op jit(solution)/shard_map/ppermute | solution.py:49
  69.3 2.4 %collective-permute-start.9 = (bf16[2,32,384]{2,1,0:T(8,128)(2,1)S(1)}, bf16[2,32,384]{2,1,0:T(8,128)(2,1)S(1)}, u32[]{:S(2)}, u32[]{:S(2)}) collective-permute-start(bf16[2,32,384]{2,1,0:T(8,128)(2,1)S(1)} %get-tuple-element.33), channel_id=1, source_target_pairs={{0,4},{1,5},{2,6},{3,7},{4,0},{5,1},{6,2},{7,3},{8,12},{9,13},{10,... | collective-permute-start | bytes 147464 | tf_op jit(solution)/shard_map/ppermute | solution.py:49
  76.1 2.5 %collective-permute-done.10 = bf16[2,64,384]{2,1,0:T(8,128)(2,1)S(1)} collective-permute-done((bf16[2,64,384]{2,1,0:T(8,128)(2,1)S(1)}, bf16[2,64,384]{2,1,0:T(8,128)(2,1)S(1)}, u32[]{:S(2)}, u32[]{:S(2)}) %collective-permute-start.10) | collective-permute-done | bytes 98336 | tf_op jit(solution)/shard_map/ppermute | solution.py:49
  78.9 11.9 %collective-permute-start.33 = (bf16[2,512,256]{2,1,0:T(8,128)(2,1)S(1)}, bf16[2,512,256]{2,1,0:T(8,128)(2,1)S(1)}, u32[]{:S(2)}, u32[]{:S(2)}) collective-permute-start(bf16[2,512,256]{2,1,0:T(8,128)(2,1)S(1)} %maximum_select_fusion.5), channel_id=1, source_target_pairs={{0,8},{1,9},{2,10},{3,11},{4,12},{5,13},{6,14},{7,15},{8,0},{9,1},... | collective-permute-start | bytes 1572872 | tf_op jit(solution)/shard_map/ppermute | solution.py:49
  92.5 2.3 %collective-permute-done.20 = bf16[2,64,384]{2,1,0:T(8,128)(2,1)S(1)} collective-permute-done((bf16[2,64,384]{2,1,0:T(8,128)(2,1)S(1)}, bf16[2,64,384]{2,1,0:T(8,128)(2,1)S(1)}, u32[]{:S(2)}, u32[]{:S(2)}) %collective-permute-start.20) | collective-permute-done | bytes 98336 | tf_op jit(solution)/shard_map/ppermute | solution.py:49
  97.2 3.4 %collective-permute-done.21 = bf16[2,128,384]{2,1,0:T(8,128)(2,1)S(1)} collective-permute-done((bf16[2,128,384]{2,1,0:T(8,128)(2,1)S(1)}, bf16[2,128,384]{2,1,0:T(8,128)(2,1)S(1)}, u32[]{:S(2)}, u32[]{:S(2)}) %collective-permute-start.21) | collective-permute-done | bytes 196640 | tf_op jit(solution)/shard_map/ppermute | solution.py:49
  101.4 3.9 %collective-permute-start.13 = (bf16[2,512,384]{2,1,0:T(8,128)(2,1)S(1)}, bf16[2,512,384]{2,1,0:T(8,128)(2,1)S(1)}, u32[]{:S(2)}, u32[]{:S(2)}) collective-permute-start(bf16[2,512,384]{2,1,0:T(8,128)(2,1)S(1)} %maximum_select_fusion.3), channel_id=1, source_target_pairs={{0,8},{1,9},{2,10},{3,11},{4,12},{5,13},{6,14},{7,15},{8,0},{9,1},... | collective-permute-start | bytes 2359304 | tf_op jit(solution)/shard_map/ppermute | solution.py:49
  105.9 3.3 %collective-permute-done.22 = bf16[2,256,384]{2,1,0:T(8,128)(2,1)S(1)} collective-permute-done((bf16[2,256,384]{2,1,0:T(8,128)(2,1)S(1)}, bf16[2,256,384]{2,1,0:T(8,128)(2,1)S(1)}, u32[]{:S(2)}, u32[]{:S(2)}) %collective-permute-start.22) | collective-permute-done | bytes 393248 | tf_op jit(solution)/shard_map/ppermute | solution.py:49
  109.5 3.3 %collective-permute-start.23 = (bf16[2,512,384]{2,1,0:T(8,128)(2,1)S(1)}, bf16[2,512,384]{2,1,0:T(8,128)(2,1)S(1)}, u32[]{:S(2)}, u32[]{:S(2)}) collective-permute-start(bf16[2,512,384]{2,1,0:T(8,128)(2,1)S(1)} %maximum_select_fusion.4), channel_id=1, source_target_pairs={{0,8},{1,9},{2,10},{3,11},{4,12},{5,13},{6,14},{7,15},{8,0},{9,1},... | collective-permute-start | bytes 2359304 | tf_op jit(solution)/shard_map/ppermute | solution.py:49
  121.9 4.1 %collective-permute-start.35 = (bf16[2,1,16,256]{3,2,1,0:T(8,128)(2,1)S(1)}, bf16[2,1,16,256]{3,2,1,0:T(8,128)(2,1)S(1)}, u32[]{:S(2)}, u32[]{:S(2)}) collective-permute-start(bf16[2,1,16,256]{3,2,1,0:T(8,128)(2,1)S(1)} %get-tuple-element.22), channel_id=1, source_target_pairs={{1,0},{2,1},{3,2},{4,3},{5,4},{6,5},{7,6},{9,8},{10,9},{11,10},{12... | collective-permute-start | bytes 49160 | tf_op jit(solution)/shard_map/ppermute | solution.py:18
  126.0 4.3 %collective-permute-start.36 = (bf16[1,4,16,256]{3,2,1,0:T(8,128)(2,1)S(1)}, bf16[1,4,16,256]{3,2,1,0:T(8,128)(2,1)S(1)}, u32[]{:S(2)}, u32[]{:S(2)}) collective-permute-start(bf16[1,4,16,256]{3,2,1,0:T(8,128)(2,1)S(1)} %get-tuple-element.25), channel_id=1, source_target_pairs={{0,8},{8,16},{16,24},{1,9},{9,17},{17,25},{2,10},{10,18},{18,26},{... | collective-permute-start | bytes 98312 | tf_op jit(solution)/shard_map/ppermute | solution.py:15
  132.3 3.3 %collective-permute-done.37 = bf16[1,4,16,256]{3,2,1,0:T(8,128)(2,1)S(1)} collective-permute-done((bf16[1,4,16,256]{3,2,1,0:T(8,128)(2,1)S(1)}, bf16[1,4,16,256]{3,2,1,0:T(8,128)(2,1)S(1)}, u32[]{:S(2)}, u32[]{:S(2)}) %collective-permute-start.37) | collective-permute-done | bytes 32800 | tf_op jit(solution)/shard_map/ppermute | solution.py:18
  (193 shorter events, 55.0 us)
Async XLA Ops:
  2.3 24.2 %collective-permute-start.1 = (bf16[2,16,1152]{2,1,0:T(8,128)(2,1)}, bf16[2,16,1152]{2,1,0:T(8,128)(2,1)}, u32[]{:S(2)}, u32[]{:S(2)}) collective-permute-start(bf16[2,16,1152]{2,1,0:T(8,128)(2,1)} %get-tuple-element.19), channel_id=1, source_target_pairs={{1,0},{2,1},{3,2},{4,3},{5,4},{6,5},{7,6},{9,8},{10,9},{11,10},{12... | collective-permute-start | bytes 221192 | tf_op jit(solution)/shard_map/ppermute | solution.py:126
  5.3 18.5 %collective-permute-start = (bf16[2,16,1152]{2,1,0:T(8,128)(2,1)}, bf16[2,16,1152]{2,1,0:T(8,128)(2,1)}, u32[]{:S(2)}, u32[]{:S(2)}) collective-permute-start(bf16[2,16,1152]{2,1,0:T(8,128)(2,1)} %get-tuple-element.20), channel_id=1, source_target_pairs={{0,1},{1,2},{2,3},{3,4},{4,5},{5,6},{6,7},{8,9},{9,10},{10,11},{11... | collective-permute-start | bytes 221192 | tf_op jit(solution)/shard_map/ppermute | solution.py:126
  9.3 39.2 %collective-permute-start.3 = (bf16[4,16,1152]{2,1,0:T(8,128)(2,1)}, bf16[4,16,1152]{2,1,0:T(8,128)(2,1)S(1)}, u32[]{:S(2)}, u32[]{:S(2)}) collective-permute-start(bf16[4,16,1152]{2,1,0:T(8,128)(2,1)} %get-tuple-element.17), channel_id=1, source_target_pairs={{8,0},{16,8},{24,16},{9,1},{17,9},{25,17},{10,2},{18,10},{26,18},{... | collective-permute-start | bytes 442376 | tf_op jit(solution)/shard_map/ppermute | solution.py:126
  12.5 15.7 %collective-permute-start.2 = (bf16[4,16,1152]{2,1,0:T(8,128)(2,1)}, bf16[4,16,1152]{2,1,0:T(8,128)(2,1)}, u32[]{:S(2)}, u32[]{:S(2)}) collective-permute-start(bf16[4,16,1152]{2,1,0:T(8,128)(2,1)} %get-tuple-element.18), channel_id=1, source_target_pairs={{0,8},{8,16},{16,24},{1,9},{9,17},{17,25},{2,10},{10,18},{18,26},{... | collective-permute-start | bytes 442376 | tf_op jit(solution)/shard_map/ppermute | solution.py:126
  17.9 7.3 %collective-permute-start.24 = (bf16[2,512,256]{2,1,0:T(8,128)(2,1)}, bf16[2,512,256]{2,1,0:T(8,128)(2,1)}, u32[]{:S(2)}, u32[]{:S(2)}) collective-permute-start(bf16[2,512,256]{2,1,0:T(8,128)(2,1)} %get-tuple-element.7), channel_id=1, source_target_pairs={{0,8},{1,9},{2,10},{3,11},{4,12},{5,13},{6,14},{7,15},{8,0},{9,1},... | collective-permute-start | bytes 1572872 | tf_op jit(solution)/shard_map/ppermute | solution.py:49
  23.8 12.5 %collective-permute-start.4 = (bf16[2,512,384]{2,1,0:T(8,128)(2,1)}, bf16[2,512,384]{2,1,0:T(8,128)(2,1)S(1)}, u32[]{:S(2)}, u32[]{:S(2)}) collective-permute-start(bf16[2,512,384]{2,1,0:T(8,128)(2,1)} %get-tuple-element.11), channel_id=1, source_target_pairs={{0,8},{1,9},{2,10},{3,11},{4,12},{5,13},{6,14},{7,15},{8,0},{9,1},... | collective-permute-start | bytes 2359304 | tf_op jit(solution)/shard_map/ppermute | solution.py:49
  25.2 11.1 %collective-permute-start.14 = (bf16[2,512,384]{2,1,0:T(8,128)(2,1)S(1)}, bf16[2,512,384]{2,1,0:T(8,128)(2,1)S(1)}, u32[]{:S(2)}, u32[]{:S(2)}) collective-permute-start(bf16[2,512,384]{2,1,0:T(8,128)(2,1)S(1)} %get-tuple-element.12), channel_id=1, source_target_pairs={{0,8},{1,9},{2,10},{3,11},{4,12},{5,13},{6,14},{7,15},{8,0},{9,1},... | collective-permute-start | bytes 2359304 | tf_op jit(solution)/shard_map/ppermute | solution.py:49
  26.6 7.5 %collective-permute-start.25 = (bf16[2,256,256]{2,1,0:T(8,128)(2,1)S(1)}, bf16[2,256,256]{2,1,0:T(8,128)(2,1)S(1)}, u32[]{:S(2)}, u32[]{:S(2)}) collective-permute-start(bf16[2,256,256]{2,1,0:T(8,128)(2,1)S(1)} %broadcast_select_fusion.5), channel_id=1, source_target_pairs={{0,16},{1,17},{2,18},{3,19},{4,20},{5,21},{6,22},{7,23},{8,24},{9,... | collective-permute-start | bytes 786440 | tf_op jit(solution)/shard_map/ppermute | solution.py:49
  44.5 7.3 %collective-permute-start.15 = (bf16[2,256,384]{2,1,0:T(8,128)(2,1)S(1)}, bf16[2,256,384]{2,1,0:T(8,128)(2,1)S(1)}, u32[]{:S(2)}, u32[]{:S(2)}) collective-permute-start(bf16[2,256,384]{2,1,0:T(8,128)(2,1)S(1)} %broadcast_select_fusion.4), channel_id=1, source_target_pairs={{0,2},{1,3},{2,0},{3,1},{4,6},{5,7},{6,4},{7,5},{8,10},{9,11},{10,... | collective-permute-start | bytes 1179656 | tf_op jit(solution)/shard_map/ppermute | solution.py:49
  44.7 7.1 %collective-permute-start.5 = (bf16[2,256,384]{2,1,0:T(8,128)(2,1)S(1)}, bf16[2,256,384]{2,1,0:T(8,128)(2,1)S(1)}, u32[]{:S(2)}, u32[]{:S(2)}) collective-permute-start(bf16[2,256,384]{2,1,0:T(8,128)(2,1)S(1)} %broadcast_select_fusion.3), channel_id=1, source_target_pairs={{0,1},{1,0},{2,3},{3,2},{4,5},{5,4},{6,7},{7,6},{8,9},{9,8},{10,11... | collective-permute-start | bytes 1179656 | tf_op jit(solution)/shard_map/ppermute | solution.py:49
  51.7 16.0 %collective-permute-start.30 = (bf16[2,64,256]{2,1,0:T(8,128)(2,1)S(1)}, bf16[2,64,256]{2,1,0:T(8,128)(2,1)S(1)}, u32[]{:S(2)}, u32[]{:S(2)}) collective-permute-start(bf16[2,64,256]{2,1,0:T(8,128)(2,1)S(1)} %maximum_select_fusion.14), channel_id=1, source_target_pairs={{0,2},{1,3},{2,0},{3,1},{4,6},{5,7},{6,4},{7,5},{8,10},{9,11},{10,... | collective-permute-start | bytes 196616 | tf_op jit(solution)/shard_map/ppermute | solution.py:49
  52.1 5.6 %collective-permute-start.16 = (bf16[2,128,384]{2,1,0:T(8,128)(2,1)S(1)}, bf16[2,128,384]{2,1,0:T(8,128)(2,1)S(1)}, u32[]{:S(2)}, u32[]{:S(2)}) collective-permute-start(bf16[2,128,384]{2,1,0:T(8,128)(2,1)S(1)} %broadcast_select_fusion.7), channel_id=1, source_target_pairs={{0,16},{1,17},{2,18},{3,19},{4,20},{5,21},{6,22},{7,23},{8,24},{9,... | collective-permute-start | bytes 589832 | tf_op jit(solution)/shard_map/ppermute | solution.py:49
  61.7 6.2 %collective-permute-start.18 = (bf16[2,32,384]{2,1,0:T(8,128)(2,1)S(1)}, bf16[2,32,384]{2,1,0:T(8,128)(2,1)S(1)}, u32[]{:S(2)}, u32[]{:S(2)}) collective-permute-start(bf16[2,32,384]{2,1,0:T(8,128)(2,1)S(1)} %broadcast_select_fusion.12), channel_id=1, source_target_pairs={{0,4},{1,5},{2,6},{3,7},{4,0},{5,1},{6,2},{7,3},{8,12},{9,13},{10,... | collective-permute-start | bytes 147464 | tf_op jit(solution)/shard_map/ppermute | solution.py:49
  71.9 6.8 %collective-permute-start.32 = (bf16[2,256,256]{2,1,0:T(8,128)(2,1)S(1)}, bf16[2,256,256]{2,1,0:T(8,128)(2,1)S(1)}, u32[]{:S(2)}, u32[]{:S(2)}) collective-permute-start(bf16[2,256,256]{2,1,0:T(8,128)(2,1)S(1)} %maximum_select_fusion.8), channel_id=1, source_target_pairs={{0,16},{1,17},{2,18},{3,19},{4,20},{5,21},{6,22},{7,23},{8,24},{9,... | collective-permute-start | bytes 786440 | tf_op jit(solution)/shard_map/ppermute | solution.py:49
  74.3 16.4 %collective-permute-start.19 = (bf16[2,32,384]{2,1,0:T(8,128)(2,1)S(1)}, bf16[2,32,384]{2,1,0:T(8,128)(2,1)S(1)}, u32[]{:S(2)}, u32[]{:S(2)}) collective-permute-start(bf16[2,32,384]{2,1,0:T(8,128)(2,1)S(1)} %get-tuple-element.34), channel_id=1, source_target_pairs={{0,4},{1,5},{2,6},{3,7},{4,0},{5,1},{6,2},{7,3},{8,12},{9,13},{10,... | collective-permute-start | bytes 147464 | tf_op jit(solution)/shard_map/ppermute | solution.py:49
  78.6 12.7 %collective-permute-start.11 = (bf16[2,128,384]{2,1,0:T(8,128)(2,1)S(1)}, bf16[2,128,384]{2,1,0:T(8,128)(2,1)S(1)}, u32[]{:S(2)}, u32[]{:S(2)}) collective-permute-start(bf16[2,128,384]{2,1,0:T(8,128)(2,1)S(1)} %maximum_select_fusion.9), channel_id=1, source_target_pairs={{0,2},{1,3},{2,0},{3,1},{4,6},{5,7},{6,4},{7,5},{8,10},{9,11},{10,... | collective-permute-start | bytes 589832 | tf_op jit(solution)/shard_map/ppermute | solution.py:49
  78.9 26.4 %collective-permute-start.33 = (bf16[2,512,256]{2,1,0:T(8,128)(2,1)S(1)}, bf16[2,512,256]{2,1,0:T(8,128)(2,1)S(1)}, u32[]{:S(2)}, u32[]{:S(2)}) collective-permute-start(bf16[2,512,256]{2,1,0:T(8,128)(2,1)S(1)} %maximum_select_fusion.5), channel_id=1, source_target_pairs={{0,8},{1,9},{2,10},{3,11},{4,12},{5,13},{6,14},{7,15},{8,0},{9,1},... | collective-permute-start | bytes 1572872 | tf_op jit(solution)/shard_map/ppermute | solution.py:49
  91.4 9.8 %collective-permute-start.12 = (bf16[2,256,384]{2,1,0:T(8,128)(2,1)S(1)}, bf16[2,256,384]{2,1,0:T(8,128)(2,1)S(1)}, u32[]{:S(2)}, u32[]{:S(2)}) collective-permute-start(bf16[2,256,384]{2,1,0:T(8,128)(2,1)S(1)} %maximum_select_fusion.6), channel_id=1, source_target_pairs={{0,1},{1,0},{2,3},{3,2},{4,5},{5,4},{6,7},{7,6},{8,9},{9,8},{10,11... | collective-permute-start | bytes 1179656 | tf_op jit(solution)/shard_map/ppermute | solution.py:49
  94.9 5.8 %collective-permute-start.21 = (bf16[2,128,384]{2,1,0:T(8,128)(2,1)S(1)}, bf16[2,128,384]{2,1,0:T(8,128)(2,1)S(1)}, u32[]{:S(2)}, u32[]{:S(2)}) collective-permute-start(bf16[2,128,384]{2,1,0:T(8,128)(2,1)S(1)} %maximum_select_fusion.10), channel_id=1, source_target_pairs={{0,16},{1,17},{2,18},{3,19},{4,20},{5,21},{6,22},{7,23},{8,24},{9,... | collective-permute-start | bytes 589832 | tf_op jit(solution)/shard_map/ppermute | solution.py:49
  100.8 8.4 %collective-permute-start.22 = (bf16[2,256,384]{2,1,0:T(8,128)(2,1)S(1)}, bf16[2,256,384]{2,1,0:T(8,128)(2,1)S(1)}, u32[]{:S(2)}, u32[]{:S(2)}) collective-permute-start(bf16[2,256,384]{2,1,0:T(8,128)(2,1)S(1)} %maximum_select_fusion.7), channel_id=1, source_target_pairs={{0,2},{1,3},{2,0},{3,1},{4,6},{5,7},{6,4},{7,5},{8,10},{9,11},{10,... | collective-permute-start | bytes 1179656 | tf_op jit(solution)/shard_map/ppermute | solution.py:49
  101.4 11.7 %collective-permute-start.13 = (bf16[2,512,384]{2,1,0:T(8,128)(2,1)S(1)}, bf16[2,512,384]{2,1,0:T(8,128)(2,1)S(1)}, u32[]{:S(2)}, u32[]{:S(2)}) collective-permute-start(bf16[2,512,384]{2,1,0:T(8,128)(2,1)S(1)} %maximum_select_fusion.3), channel_id=1, source_target_pairs={{0,8},{1,9},{2,10},{3,11},{4,12},{5,13},{6,14},{7,15},{8,0},{9,1},... | collective-permute-start | bytes 2359304 | tf_op jit(solution)/shard_map/ppermute | solution.py:49
  119.8 12.5 %collective-permute-start.34 = (bf16[2,1,16,256]{3,2,1,0:T(8,128)(2,1)S(1)}, bf16[2,1,16,256]{3,2,1,0:T(8,128)(2,1)S(1)}, u32[]{:S(2)}, u32[]{:S(2)}) collective-permute-start(bf16[2,1,16,256]{3,2,1,0:T(8,128)(2,1)S(1)} %get-tuple-element.21), channel_id=1, source_target_pairs={{0,1},{1,2},{2,3},{3,4},{4,5},{5,6},{6,7},{8,9},{9,10},{10,11},{11... | collective-permute-start | bytes 49160 | tf_op jit(solution)/shard_map/ppermute | solution.py:15
  121.9 10.4 %collective-permute-start.35 = (bf16[2,1,16,256]{3,2,1,0:T(8,128)(2,1)S(1)}, bf16[2,1,16,256]{3,2,1,0:T(8,128)(2,1)S(1)}, u32[]{:S(2)}, u32[]{:S(2)}) collective-permute-start(bf16[2,1,16,256]{3,2,1,0:T(8,128)(2,1)S(1)} %get-tuple-element.22), channel_id=1, source_target_pairs={{1,0},{2,1},{3,2},{4,3},{5,4},{6,5},{7,6},{9,8},{10,9},{11,10},{12... | collective-permute-start | bytes 49160 | tf_op jit(solution)/shard_map/ppermute | solution.py:18
  126.0 6.3 %collective-permute-start.36 = (bf16[1,4,16,256]{3,2,1,0:T(8,128)(2,1)S(1)}, bf16[1,4,16,256]{3,2,1,0:T(8,128)(2,1)S(1)}, u32[]{:S(2)}, u32[]{:S(2)}) collective-permute-start(bf16[1,4,16,256]{3,2,1,0:T(8,128)(2,1)S(1)} %get-tuple-element.25), channel_id=1, source_target_pairs={{0,8},{8,16},{16,24},{1,9},{9,17},{17,25},{2,10},{10,18},{18,26},{... | collective-permute-start | bytes 98312 | tf_op jit(solution)/shard_map/ppermute | solution.py:15
  (33 other events, 201.9 us)

commit v4 on v3

--- a/solution.py
+++ b/solution.py
@@ -49,7 +49,7 @@
     return lax.ppermute(block, ("row", "col"), pairs)
 
 
-def scatter_gather(block, owner, order, col_bits, me):
+def scatter_gather(block, owner, order, col_bits, me, tie):
     done_mask = 0
     full = (1 << len(order)) - 1
     for bit in order:
@@ -63,16 +63,17 @@
         have = ((me ^ owner) & outside) == 0
         block = jnp.where(have[:, None, None], keep, got)
         done_mask |= 1 << bit
+    block, tie = lax.optimization_barrier((block, tie))
     for bit in reversed(order):
         mine = ((me >> bit) & 1) == 1
         got = swap(block, bit, col_bits)
         block = jnp.where(
             mine, jnp.concatenate([got, block], axis=1), jnp.concatenate([block, got], axis=1)
         )
-    return block
-
-
-def broadcast_parts(own_operator, owner):
+    return block, tie
+
+
+def broadcast_parts(own_operator, owner, tie):
     col_bits = device_bits("col")
     row_bits = device_bits("row")
     me = lax.axis_index("row") * lax.axis_size("col") + lax.axis_index("col")
@@ -80,7 +81,7 @@
     order_len = None if col_bits is None or row_bits is None else col_bits + row_bits
     if order_len is None or row_bits < 1 or col_bits < 1 or (own_operator.shape[0] >> order_len) < 8:
         mask = (me == owner)[:, None, None]
-        return [lax.psum(jnp.where(mask, stacked, jnp.zeros_like(stacked)), ("row", "col"))]
+        return [lax.psum(jnp.where(mask, stacked, jnp.zeros_like(stacked)), ("row", "col"))], tie
     core = col_bits
     middle = list(range(col_bits - 1)) + list(range(col_bits + 1, col_bits + row_bits))
     last = [col_bits - 1]
@@ -95,9 +96,10 @@
         rotated = middle[s:] + middle[:s]
         order = [core] + rotated + last
         piece = stacked[:, :, offset : offset + cols]
-        parts.append(scatter_gather(piece, owner, order, col_bits, me))
+        gathered, tie = scatter_gather(piece, owner, order, col_bits, me, tie)
+        parts.append(gathered)
         offset += cols
-    return parts
+    return parts, tie
 
 
 def sweep(traces, kinds, ids, parts, port_cell, excite):
@@ -138,11 +140,11 @@
         [incoming, jnp.broadcast_to(cell_type.astype(incoming.dtype)[:, :, None, None], (cell_rows, cell_cols, port_count, 128))],
         axis=-1,
     )
+    parts, tagged = broadcast_parts(bank[0, 0], owner, tagged)
     from_west = shift(tagged[:, -1], "col", 1)
     from_east = shift(tagged[:, 0], "col", -1)
     from_north = shift(tagged[-1], "row", 1)
     from_south = shift(tagged[0], "row", -1)
-    parts = broadcast_parts(bank[0, 0], owner)
     row_ids = row_at * cell_rows + jnp.arange(cell_rows, dtype=jnp.int32)
     col_ids = col_at * cell_cols + jnp.arange(cell_cols, dtype=jnp.int32)
     flat_ids = (row_ids[:, None] * width + col_ids[None, :]).reshape(-1)

time: 139 us -> 122 us (0.88)
  starting transfers between devices: 74.4 us -> 67.8 us
  other arithmetic: 18.3 us -> 13.3 us
  local copies, waits for them, and re-layouts: 5.35 us -> 2.03 us
  waiting for transfers between devices: 33.3 us -> 31.8 us
    ppermute x30, starting transfers between devices: 50.6 us -> 36.5 us  [swap(): return lax.ppermute(block, ('row', 'col'), pairs)]
    ppermute x4, starting transfers between devices: 11.4 us -> 20.8 us  [shift(): return lax.ppermute(block, axis, pairs)]
    squeeze x2 -> x0, other arithmetic: 3.27 us -> none  [the longest x1 1.71 us: local(): from_south = shift(tagged[0], 'row', -1)]
    ppermute x2, starting transfers between devices: 6.39 us -> 3.85 us  [with_halo(): lax.ppermute(lax.slice_in_dim(block, block.shape[dim] - width, None, axis...]
    unnamed x41 -> x17, local copies, waits for them, and re-layouts: 3.72 us -> 1.55 us
    select_n x12, other arithmetic: 2.65 us -> 4.09 us  [scatter_gather(): block = jnp.where(have[:, None, None], keep, got)]
  transfers between devices with their start and end apart: 38 -> 38, of which waited for: 16 -> 15; matrix products, arithmetic and copies ran while one was open for 14% -> 9% of each run, Pallas kernels for 0% -> 0%
where the time goes in v4:
time: 122 us
  starting transfers between devices  67.8 us (56%)
  waiting for transfers between devices  31.8 us (26%)
  other arithmetic  13.3 us (11%)
  matrix products  5.97 us (5%)
  local copies, waits for them, and re-layouts  2.03 us (2%)
    ppermute x30, starting transfers between devices, swap(): return lax.ppermute(block, ('row', 'col'), pairs)  36.5 us
    ppermute x30, waiting for transfers between devices, swap(): return lax.ppermute(block, ('row', 'col'), pairs)  29 us
    ppermute x4, starting transfers between devices, shift(): return lax.ppermute(block, axis, pairs)  20.8 us
    ppermute x2, starting transfers between devices, with_halo(): lax.ppermute(lax.slice_in_dim(block, 0, width, axis=dim), axis, backward)  6.66 us
    dot_general x18, matrix products, sweep(): jnp.dot(rows, part[k], preferred_element_type=jnp.float32)  5.97 us
    select_n x14, other arithmetic, scatter_gather(): give = jnp.where(mine, low, high)  4.2 us
    select_n x12, other arithmetic, scatter_gather(): block = jnp.where(have[:, None, None], keep, got)  4.09 us
    ppermute x2, starting transfers between devices, with_halo(): lax.ppermute(lax.slice_in_dim(block, block.shape[dim] - width, None, axis...  3.85 us
  transfers between devices with their start and end apart: 38, of which 15 were waited for; matrix products, arithmetic and copies ran while one was open for 9% of the time, Pallas kernels for 0%

profile of v4, /device:TPU:9, one launch (start us, length us, event | category | flops | bytes accessed | tf_op | source)
XLA Modules:
  0.0 121.6 jit_solution(5135258252058446233)
XLA Ops:
  0.0 2.5 %broadcast_select_fusion.2 = (bf16[2,512,256]{2,1,0:T(8,128)(2,1)}, bf16[2,512,256]{2,1,0:T(8,128)(2,1)S(1)}, bf16[2,512,256]{2,1,0:T(8,128)(2,1)}) fusion(pred[]{:T(512)S(6)} %eq.139, bf16[1,1024,1024]{2,1,0:T(8,128)(2,1)} %bitcast.78), kind=kLoop, calls=%fused_computation.47 | loop fusion | flops 2359296 | bytes 3670017 | tf_op jit(solution)/shard_map/jit(_where)/select_n | solution.py:60
  9.1 6.2 %collective-permute-done.1 = bf16[2,256,256]{2,1,0:T(8,128)(2,1)S(1)} collective-permute-done((bf16[2,256,256]{2,1,0:T(8,128)(2,1)S(1)}, bf16[2,256,256]{2,1,0:T(8,128)(2,1)S(1)}, u32[]{:S(2)}, u32[]{:S(2)}) %collective-permute-start.1) | collective-permute-done | bytes 262176 | tf_op jit(solution)/shard_map/ppermute | solution.py:49
  16.8 1.9 %select_select_fusion = (bf16[2,512,384]{2,1,0:T(8,128)(2,1)S(1)}, bf16[2,512,384]{2,1,0:T(8,128)(2,1)S(1)}) fusion(bf16[2,512,384]{2,1,0:T(8,128)(2,1)} %collective-permute-done.10, pred[2]{0:T(512)(128)(4,1)S(1)} %get-tuple-element.51, pred[]{:T(512)S(6)} %eq.139, bf16[1,1024,1024]{2,1,0:T(8,128)(2,1)S(1)} %bitcast.80, ...), kind=kLoop, calls=%fused_computation.16 | loop fusion | flops 7864320 | bytes 5242883 | tf_op jit(solution)/shard_map/jit(_where)/select_n | solution.py:64
  22.8 2.4 %collective-permute-start.4 = (bf16[2,32,256]{2,1,0:T(8,128)(2,1)S(1)}, bf16[2,32,256]{2,1,0:T(8,128)(2,1)S(1)}, u32[]{:S(2)}, u32[]{:S(2)}) collective-permute-start(bf16[2,32,256]{2,1,0:T(8,128)(2,1)S(1)} %broadcast_select_fusion.14), channel_id=1, source_target_pairs={{0,4},{1,5},{2,6},{3,7},{4,0},{5,1},{6,2},{7,3},{8,12},{9,13},{10,... | collective-permute-start | bytes 98312 | tf_op jit(solution)/shard_map/ppermute | solution.py:49
  25.1 4.6 %collective-permute-done.6 = bf16[2,256,384]{2,1,0:T(8,128)(2,1)S(1)} collective-permute-done((bf16[2,256,384]{2,1,0:T(8,128)(2,1)S(1)}, bf16[2,256,384]{2,1,0:T(8,128)(2,1)S(1)}, u32[]{:S(2)}, u32[]{:S(2)}) %collective-permute-start.6) | collective-permute-done | bytes 393248 | tf_op jit(solution)/shard_map/ppermute | solution.py:49
  32.7 1.9 %collective-permute-done.7 = bf16[2,128,384]{2,1,0:T(8,128)(2,1)S(1)} collective-permute-done((bf16[2,128,384]{2,1,0:T(8,128)(2,1)S(1)}, bf16[2,128,384]{2,1,0:T(8,128)(2,1)S(1)}, u32[]{:S(2)}, u32[]{:S(2)}) %collective-permute-start.7) | collective-permute-done | bytes 196640 | tf_op jit(solution)/shard_map/ppermute | solution.py:49
  38.7 2.3 %collective-permute-start.9 = (bf16[2,32,384]{2,1,0:T(8,128)(2,1)S(1)}, bf16[2,32,384]{2,1,0:T(8,128)(2,1)S(1)}, u32[]{:S(2)}, u32[]{:S(2)}) collective-permute-start(bf16[2,32,384]{2,1,0:T(8,128)(2,1)S(1)} %broadcast_select_fusion.13), channel_id=1, source_target_pairs={{0,4},{1,5},{2,6},{3,7},{4,0},{5,1},{6,2},{7,3},{8,12},{9,13},{10,... | collective-permute-start | bytes 147464 | tf_op jit(solution)/shard_map/ppermute | solution.py:49
  42.6 2.5 %collective-permute-done.14 = bf16[2,32,384]{2,1,0:T(8,128)(2,1)S(1)} collective-permute-done((bf16[2,32,384]{2,1,0:T(8,128)(2,1)S(1)}, bf16[2,32,384]{2,1,0:T(8,128)(2,1)S(1)}, u32[]{:S(2)}, u32[]{:S(2)}) %collective-permute-start.14) | collective-permute-done | bytes 49184 | tf_op jit(solution)/shard_map/ppermute | solution.py:49
  48.9 3.7 %collective-permute-start.16 = (bf16[2,16,1152]{2,1,0:T(8,128)(2,1)S(1)}, bf16[2,16,1152]{2,1,0:T(8,128)(2,1)S(1)}, u32[]{:S(2)}, u32[]{:S(2)}) collective-permute-start(bf16[2,16,1152]{2,1,0:T(8,128)(2,1)S(1)} %get-tuple-element.32), channel_id=1, source_target_pairs={{1,0},{2,1},{3,2},{4,3},{5,4},{6,5},{7,6},{9,8},{10,9},{11,10},{12... | collective-permute-start | bytes 221192 | tf_op jit(solution)/shard_map/ppermute | solution.py:128
  52.6 1.9 %collective-permute-start.15 = (bf16[2,16,1152]{2,1,0:T(8,128)(2,1)S(1)}, bf16[2,16,1152]{2,1,0:T(8,128)(2,1)S(1)}, u32[]{:S(2)}, u32[]{:S(2)}) collective-permute-start(bf16[2,16,1152]{2,1,0:T(8,128)(2,1)S(1)} %get-tuple-element.33), channel_id=1, source_target_pairs={{0,1},{1,2},{2,3},{3,4},{4,5},{5,6},{6,7},{8,9},{9,10},{10,11},{11... | collective-permute-start | bytes 221192 | tf_op jit(solution)/shard_map/ppermute | solution.py:128
  54.5 12.2 %collective-permute-start.18 = (bf16[4,16,1152]{2,1,0:T(8,128)(2,1)S(1)}, bf16[4,16,1152]{2,1,0:T(8,128)(2,1)S(1)}, u32[]{:S(2)}, u32[]{:S(2)}) collective-permute-start(bf16[4,16,1152]{2,1,0:T(8,128)(2,1)S(1)} %get-tuple-element.30), channel_id=1, source_target_pairs={{8,0},{16,8},{24,16},{9,1},{17,9},{25,17},{10,2},{18,10},{26,18},{... | collective-permute-start | bytes 442376 | tf_op jit(solution)/shard_map/ppermute | solution.py:128
  66.8 2.9 %collective-permute-start.17 = (bf16[4,16,1152]{2,1,0:T(8,128)(2,1)S(1)}, bf16[4,16,1152]{2,1,0:T(8,128)(2,1)S(1)}, u32[]{:S(2)}, u32[]{:S(2)}) collective-permute-start(bf16[4,16,1152]{2,1,0:T(8,128)(2,1)S(1)} %get-tuple-element.31), channel_id=1, source_target_pairs={{0,8},{8,16},{16,24},{1,9},{9,17},{17,25},{2,10},{10,18},{18,26},{... | collective-permute-start | bytes 442376 | tf_op jit(solution)/shard_map/ppermute | solution.py:128
  70.0 2.5 %collective-permute-start.25 = (bf16[2,64,384]{2,1,0:T(8,128)(2,1)S(1)}, bf16[2,64,384]{2,1,0:T(8,128)(2,1)S(1)}, u32[]{:S(2)}, u32[]{:S(2)}) collective-permute-start(bf16[2,64,384]{2,1,0:T(8,128)(2,1)S(1)} %maximum_select_fusion.13), channel_id=1, source_target_pairs={{0,1},{1,0},{2,3},{3,2},{4,5},{5,4},{6,7},{7,6},{8,9},{9,8},{10,11... | collective-permute-start | bytes 294920 | tf_op jit(solution)/shard_map/ppermute | solution.py:49
  73.9 2.0 %collective-permute-start.31 = (bf16[2,128,256]{2,1,0:T(8,128)(2,1)S(1)}, bf16[2,128,256]{2,1,0:T(8,128)(2,1)S(1)}, u32[]{:S(2)}, u32[]{:S(2)}) collective-permute-start(bf16[2,128,256]{2,1,0:T(8,128)(2,1)S(1)} %maximum_select_fusion.11), channel_id=1, source_target_pairs={{0,1},{1,0},{2,3},{3,2},{4,5},{5,4},{6,7},{7,6},{8,9},{9,8},{10,11... | collective-permute-start | bytes 393224 | tf_op jit(solution)/shard_map/ppermute | solution.py:49
  76.6 1.8 %collective-permute-start.21 = (bf16[2,128,384]{2,1,0:T(8,128)(2,1)S(1)}, bf16[2,128,384]{2,1,0:T(8,128)(2,1)S(1)}, u32[]{:S(2)}, u32[]{:S(2)}) collective-permute-start(bf16[2,128,384]{2,1,0:T(8,128)(2,1)S(1)} %maximum_select_fusion.9), channel_id=1, source_target_pairs={{0,2},{1,3},{2,0},{3,1},{4,6},{5,7},{6,4},{7,5},{8,10},{9,11},{10,... | collective-permute-start | bytes 589832 | tf_op jit(solution)/shard_map/ppermute | solution.py:49
  79.9 2.3 %collective-permute-done.21 = bf16[2,128,384]{2,1,0:T(8,128)(2,1)S(1)} collective-permute-done((bf16[2,128,384]{2,1,0:T(8,128)(2,1)S(1)}, bf16[2,128,384]{2,1,0:T(8,128)(2,1)S(1)}, u32[]{:S(2)}, u32[]{:S(2)}) %collective-permute-start.21) | collective-permute-done | bytes 196640 | tf_op jit(solution)/shard_map/ppermute | solution.py:49
  82.3 3.0 %collective-permute-start.22 = (bf16[2,256,384]{2,1,0:T(8,128)(2,1)S(1)}, bf16[2,256,384]{2,1,0:T(8,128)(2,1)S(1)}, u32[]{:S(2)}, u32[]{:S(2)}) collective-permute-start(bf16[2,256,384]{2,1,0:T(8,128)(2,1)S(1)} %maximum_select_fusion.6), channel_id=1, source_target_pairs={{0,1},{1,0},{2,3},{3,2},{4,5},{5,4},{6,7},{7,6},{8,9},{9,8},{10,11... | collective-permute-start | bytes 1179656 | tf_op jit(solution)/shard_map/ppermute | solution.py:49
  89.8 4.9 %collective-permute-done.27 = bf16[2,256,384]{2,1,0:T(8,128)(2,1)S(1)} collective-permute-done((bf16[2,256,384]{2,1,0:T(8,128)(2,1)S(1)}, bf16[2,256,384]{2,1,0:T(8,128)(2,1)S(1)}, u32[]{:S(2)}, u32[]{:S(2)}) %collective-permute-start.27) | collective-permute-done | bytes 393248 | tf_op jit(solution)/shard_map/ppermute | solution.py:49
  95.0 2.5 %collective-permute-start.28 = (bf16[2,512,384]{2,1,0:T(8,128)(2,1)S(1)}, bf16[2,512,384]{2,1,0:T(8,128)(2,1)S(1)}, u32[]{:S(2)}, u32[]{:S(2)}) collective-permute-start(bf16[2,512,384]{2,1,0:T(8,128)(2,1)S(1)} %maximum_select_fusion.4), channel_id=1, source_target_pairs={{0,8},{1,9},{2,10},{3,11},{4,12},{5,13},{6,14},{7,15},{8,0},{9,1},... | collective-permute-start | bytes 2359304 | tf_op jit(solution)/shard_map/ppermute | solution.py:49
  105.6 1.9 %collective-permute-start.34 = (bf16[2,1,16,256]{3,2,1,0:T(8,128)(2,1)S(1)}, bf16[2,1,16,256]{3,2,1,0:T(8,128)(2,1)S(1)}, u32[]{:S(2)}, u32[]{:S(2)}) collective-permute-start(bf16[2,1,16,256]{3,2,1,0:T(8,128)(2,1)S(1)} %get-tuple-element.34), channel_id=1, source_target_pairs={{0,1},{1,2},{2,3},{3,4},{4,5},{5,6},{6,7},{8,9},{9,10},{10,11},{11... | collective-permute-start | bytes 49160 | tf_op jit(solution)/shard_map/ppermute | solution.py:15
  107.5 4.3 %collective-permute-start.35 = (bf16[2,1,16,256]{3,2,1,0:T(8,128)(2,1)S(1)}, bf16[2,1,16,256]{3,2,1,0:T(8,128)(2,1)S(1)}, u32[]{:S(2)}, u32[]{:S(2)}) collective-permute-start(bf16[2,1,16,256]{3,2,1,0:T(8,128)(2,1)S(1)} %get-tuple-element.35), channel_id=1, source_target_pairs={{1,0},{2,1},{3,2},{4,3},{5,4},{6,5},{7,6},{9,8},{10,9},{11,10},{12... | collective-permute-start | bytes 49160 | tf_op jit(solution)/shard_map/ppermute | solution.py:18
  111.8 1.9 %collective-permute-start.36 = (bf16[1,4,16,256]{3,2,1,0:T(8,128)(2,1)S(1)}, bf16[1,4,16,256]{3,2,1,0:T(8,128)(2,1)S(1)}, u32[]{:S(2)}, u32[]{:S(2)}) collective-permute-start(bf16[1,4,16,256]{3,2,1,0:T(8,128)(2,1)S(1)} %get-tuple-element.38), channel_id=1, source_target_pairs={{0,8},{8,16},{16,24},{1,9},{9,17},{17,25},{2,10},{10,18},{18,26},{... | collective-permute-start | bytes 98312 | tf_op jit(solution)/shard_map/ppermute | solution.py:15
  113.7 2.4 %collective-permute-start.37 = (bf16[1,4,16,256]{3,2,1,0:T(8,128)(2,1)S(1)}, bf16[1,4,16,256]{3,2,1,0:T(8,128)(2,1)S(1)}, u32[]{:S(2)}, u32[]{:S(2)}) collective-permute-start(bf16[1,4,16,256]{3,2,1,0:T(8,128)(2,1)S(1)} %get-tuple-element.39), channel_id=1, source_target_pairs={{8,0},{16,8},{24,16},{9,1},{17,9},{25,17},{10,2},{18,10},{26,18},{... | collective-permute-start | bytes 98312 | tf_op jit(solution)/shard_map/ppermute | solution.py:18
  116.2 2.8 %collective-permute-done.37 = bf16[1,4,16,256]{3,2,1,0:T(8,128)(2,1)S(1)} collective-permute-done((bf16[1,4,16,256]{3,2,1,0:T(8,128)(2,1)S(1)}, bf16[1,4,16,256]{3,2,1,0:T(8,128)(2,1)S(1)}, u32[]{:S(2)}, u32[]{:S(2)}) %collective-permute-start.37) | collective-permute-done | bytes 32800 | tf_op jit(solution)/shard_map/ppermute | solution.py:18
  (170 shorter events, 43.5 us)
Async XLA Ops:
  4.6 12.2 %collective-permute-start.10 = (bf16[2,512,384]{2,1,0:T(8,128)(2,1)}, bf16[2,512,384]{2,1,0:T(8,128)(2,1)}, u32[]{:S(2)}, u32[]{:S(2)}) collective-permute-start(bf16[2,512,384]{2,1,0:T(8,128)(2,1)} %get-tuple-element.24), channel_id=1, source_target_pairs={{0,8},{1,9},{2,10},{3,11},{4,12},{5,13},{6,14},{7,15},{8,0},{9,1},... | collective-permute-start | bytes 2359304 | tf_op jit(solution)/shard_map/ppermute | solution.py:49
  4.6 12.2 %collective-permute-start.5 = (bf16[2,512,384]{2,1,0:T(8,128)(2,1)}, bf16[2,512,384]{2,1,0:T(8,128)(2,1)}, u32[]{:S(2)}, u32[]{:S(2)}) collective-permute-start(bf16[2,512,384]{2,1,0:T(8,128)(2,1)} %get-tuple-element.25), channel_id=1, source_target_pairs={{0,8},{1,9},{2,10},{3,11},{4,12},{5,13},{6,14},{7,15},{8,0},{9,1},... | collective-permute-start | bytes 2359304 | tf_op jit(solution)/shard_map/ppermute | solution.py:49
  7.6 7.8 %collective-permute-start.1 = (bf16[2,256,256]{2,1,0:T(8,128)(2,1)S(1)}, bf16[2,256,256]{2,1,0:T(8,128)(2,1)S(1)}, u32[]{:S(2)}, u32[]{:S(2)}) collective-permute-start(bf16[2,256,256]{2,1,0:T(8,128)(2,1)S(1)} %broadcast_select_fusion.5), channel_id=1, source_target_pairs={{0,16},{1,17},{2,18},{3,19},{4,20},{5,21},{6,22},{7,23},{8,24},{9,... | collective-permute-start | bytes 786440 | tf_op jit(solution)/shard_map/ppermute | solution.py:49
  20.4 9.4 %collective-permute-start.6 = (bf16[2,256,384]{2,1,0:T(8,128)(2,1)S(1)}, bf16[2,256,384]{2,1,0:T(8,128)(2,1)S(1)}, u32[]{:S(2)}, u32[]{:S(2)}) collective-permute-start(bf16[2,256,384]{2,1,0:T(8,128)(2,1)S(1)} %broadcast_select_fusion.4), channel_id=1, source_target_pairs={{0,2},{1,3},{2,0},{3,1},{4,6},{5,7},{6,4},{7,5},{8,10},{9,11},{10,... | collective-permute-start | bytes 1179656 | tf_op jit(solution)/shard_map/ppermute | solution.py:49
  21.1 8.6 %collective-permute-start.11 = (bf16[2,256,384]{2,1,0:T(8,128)(2,1)S(1)}, bf16[2,256,384]{2,1,0:T(8,128)(2,1)S(1)}, u32[]{:S(2)}, u32[]{:S(2)}) collective-permute-start(bf16[2,256,384]{2,1,0:T(8,128)(2,1)S(1)} %broadcast_select_fusion.3), channel_id=1, source_target_pairs={{0,1},{1,0},{2,3},{3,2},{4,5},{5,4},{6,7},{7,6},{8,9},{9,8},{10,11... | collective-permute-start | bytes 1179656 | tf_op jit(solution)/shard_map/ppermute | solution.py:49
  22.8 19.6 %collective-permute-start.4 = (bf16[2,32,256]{2,1,0:T(8,128)(2,1)S(1)}, bf16[2,32,256]{2,1,0:T(8,128)(2,1)S(1)}, u32[]{:S(2)}, u32[]{:S(2)}) collective-permute-start(bf16[2,32,256]{2,1,0:T(8,128)(2,1)S(1)} %broadcast_select_fusion.14), channel_id=1, source_target_pairs={{0,4},{1,5},{2,6},{3,7},{4,0},{5,1},{6,2},{7,3},{8,12},{9,13},{10,... | collective-permute-start | bytes 98312 | tf_op jit(solution)/shard_map/ppermute | solution.py:49
  45.2 9.3 %collective-permute-start.29 = (bf16[2,32,256]{2,1,0:T(8,128)(2,1)S(1)}, bf16[2,32,256]{2,1,0:T(8,128)(2,1)S(1)}, u32[]{:S(2)}, u32[]{:S(2)}) collective-permute-start(bf16[2,32,256]{2,1,0:T(8,128)(2,1)S(1)} %select_select_fusion.14), channel_id=1, source_target_pairs={{0,4},{1,5},{2,6},{3,7},{4,0},{5,1},{6,2},{7,3},{8,12},{9,13},{10,... | collective-permute-start | bytes 98312 | tf_op jit(solution)/shard_map/ppermute | solution.py:49
  46.4 20.3 %collective-permute-start.24 = (bf16[2,32,384]{2,1,0:T(8,128)(2,1)S(1)}, bf16[2,32,384]{2,1,0:T(8,128)(2,1)S(1)}, u32[]{:S(2)}, u32[]{:S(2)}) collective-permute-start(bf16[2,32,384]{2,1,0:T(8,128)(2,1)S(1)} %get-tuple-element.15), channel_id=1, source_target_pairs={{0,4},{1,5},{2,6},{3,7},{4,0},{5,1},{6,2},{7,3},{8,12},{9,13},{10,... | collective-permute-start | bytes 147464 | tf_op jit(solution)/shard_map/ppermute | solution.py:49
  47.7 22.0 %collective-permute-start.19 = (bf16[2,32,384]{2,1,0:T(8,128)(2,1)S(1)}, bf16[2,32,384]{2,1,0:T(8,128)(2,1)S(1)}, u32[]{:S(2)}, u32[]{:S(2)}) collective-permute-start(bf16[2,32,384]{2,1,0:T(8,128)(2,1)S(1)} %get-tuple-element.14), channel_id=1, source_target_pairs={{0,4},{1,5},{2,6},{3,7},{4,0},{5,1},{6,2},{7,3},{8,12},{9,13},{10,... | collective-permute-start | bytes 147464 | tf_op jit(solution)/shard_map/ppermute | solution.py:49
  48.9 21.1 %collective-permute-start.16 = (bf16[2,16,1152]{2,1,0:T(8,128)(2,1)S(1)}, bf16[2,16,1152]{2,1,0:T(8,128)(2,1)S(1)}, u32[]{:S(2)}, u32[]{:S(2)}) collective-permute-start(bf16[2,16,1152]{2,1,0:T(8,128)(2,1)S(1)} %get-tuple-element.32), channel_id=1, source_target_pairs={{1,0},{2,1},{3,2},{4,3},{5,4},{6,5},{7,6},{9,8},{10,9},{11,10},{12... | collective-permute-start | bytes 221192 | tf_op jit(solution)/shard_map/ppermute | solution.py:128
  52.6 17.3 %collective-permute-start.15 = (bf16[2,16,1152]{2,1,0:T(8,128)(2,1)S(1)}, bf16[2,16,1152]{2,1,0:T(8,128)(2,1)S(1)}, u32[]{:S(2)}, u32[]{:S(2)}) collective-permute-start(bf16[2,16,1152]{2,1,0:T(8,128)(2,1)S(1)} %get-tuple-element.33), channel_id=1, source_target_pairs={{0,1},{1,2},{2,3},{3,4},{4,5},{5,6},{6,7},{8,9},{9,10},{10,11},{11... | collective-permute-start | bytes 221192 | tf_op jit(solution)/shard_map/ppermute | solution.py:128
  54.5 25.4 %collective-permute-start.18 = (bf16[4,16,1152]{2,1,0:T(8,128)(2,1)S(1)}, bf16[4,16,1152]{2,1,0:T(8,128)(2,1)S(1)}, u32[]{:S(2)}, u32[]{:S(2)}) collective-permute-start(bf16[4,16,1152]{2,1,0:T(8,128)(2,1)S(1)} %get-tuple-element.30), channel_id=1, source_target_pairs={{8,0},{16,8},{24,16},{9,1},{17,9},{25,17},{10,2},{18,10},{26,18},{... | collective-permute-start | bytes 442376 | tf_op jit(solution)/shard_map/ppermute | solution.py:128
  66.8 11.6 %collective-permute-start.17 = (bf16[4,16,1152]{2,1,0:T(8,128)(2,1)S(1)}, bf16[4,16,1152]{2,1,0:T(8,128)(2,1)S(1)}, u32[]{:S(2)}, u32[]{:S(2)}) collective-permute-start(bf16[4,16,1152]{2,1,0:T(8,128)(2,1)S(1)} %get-tuple-element.31), channel_id=1, source_target_pairs={{0,8},{8,16},{16,24},{1,9},{9,17},{17,25},{2,10},{10,18},{18,26},{... | collective-permute-start | bytes 442376 | tf_op jit(solution)/shard_map/ppermute | solution.py:128
  69.9 6.7 %collective-permute-start.20 = (bf16[2,64,384]{2,1,0:T(8,128)(2,1)S(1)}, bf16[2,64,384]{2,1,0:T(8,128)(2,1)S(1)}, u32[]{:S(2)}, u32[]{:S(2)}) collective-permute-start(bf16[2,64,384]{2,1,0:T(8,128)(2,1)S(1)} %maximum_select_fusion.12), channel_id=1, source_target_pairs={{0,16},{1,17},{2,18},{3,19},{4,20},{5,21},{6,22},{7,23},{8,24},{9,... | collective-permute-start | bytes 294920 | tf_op jit(solution)/shard_map/ppermute | solution.py:49
  70.0 6.0 %collective-permute-start.25 = (bf16[2,64,384]{2,1,0:T(8,128)(2,1)S(1)}, bf16[2,64,384]{2,1,0:T(8,128)(2,1)S(1)}, u32[]{:S(2)}, u32[]{:S(2)}) collective-permute-start(bf16[2,64,384]{2,1,0:T(8,128)(2,1)S(1)} %maximum_select_fusion.13), channel_id=1, source_target_pairs={{0,1},{1,0},{2,3},{3,2},{4,5},{5,4},{6,7},{7,6},{8,9},{9,8},{10,11... | collective-permute-start | bytes 294920 | tf_op jit(solution)/shard_map/ppermute | solution.py:49
  73.9 5.8 %collective-permute-start.31 = (bf16[2,128,256]{2,1,0:T(8,128)(2,1)S(1)}, bf16[2,128,256]{2,1,0:T(8,128)(2,1)S(1)}, u32[]{:S(2)}, u32[]{:S(2)}) collective-permute-start(bf16[2,128,256]{2,1,0:T(8,128)(2,1)S(1)} %maximum_select_fusion.11), channel_id=1, source_target_pairs={{0,1},{1,0},{2,3},{3,2},{4,5},{5,4},{6,7},{7,6},{8,9},{9,8},{10,11... | collective-permute-start | bytes 393224 | tf_op jit(solution)/shard_map/ppermute | solution.py:49
  76.0 9.3 %collective-permute-start.26 = (bf16[2,128,384]{2,1,0:T(8,128)(2,1)S(1)}, bf16[2,128,384]{2,1,0:T(8,128)(2,1)S(1)}, u32[]{:S(2)}, u32[]{:S(2)}) collective-permute-start(bf16[2,128,384]{2,1,0:T(8,128)(2,1)S(1)} %maximum_select_fusion.10), channel_id=1, source_target_pairs={{0,16},{1,17},{2,18},{3,19},{4,20},{5,21},{6,22},{7,23},{8,24},{9,... | collective-permute-start | bytes 589832 | tf_op jit(solution)/shard_map/ppermute | solution.py:49
  76.6 5.6 %collective-permute-start.21 = (bf16[2,128,384]{2,1,0:T(8,128)(2,1)S(1)}, bf16[2,128,384]{2,1,0:T(8,128)(2,1)S(1)}, u32[]{:S(2)}, u32[]{:S(2)}) collective-permute-start(bf16[2,128,384]{2,1,0:T(8,128)(2,1)S(1)} %maximum_select_fusion.9), channel_id=1, source_target_pairs={{0,2},{1,3},{2,0},{3,1},{4,6},{5,7},{6,4},{7,5},{8,10},{9,11},{10,... | collective-permute-start | bytes 589832 | tf_op jit(solution)/shard_map/ppermute | solution.py:49
  79.8 8.0 %collective-permute-start.32 = (bf16[2,256,256]{2,1,0:T(8,128)(2,1)S(1)}, bf16[2,256,256]{2,1,0:T(8,128)(2,1)S(1)}, u32[]{:S(2)}, u32[]{:S(2)}) collective-permute-start(bf16[2,256,256]{2,1,0:T(8,128)(2,1)S(1)} %maximum_select_fusion.8), channel_id=1, source_target_pairs={{0,16},{1,17},{2,18},{3,19},{4,20},{5,21},{6,22},{7,23},{8,24},{9,... | collective-permute-start | bytes 786440 | tf_op jit(solution)/shard_map/ppermute | solution.py:49
  82.3 15.1 %collective-permute-start.22 = (bf16[2,256,384]{2,1,0:T(8,128)(2,1)S(1)}, bf16[2,256,384]{2,1,0:T(8,128)(2,1)S(1)}, u32[]{:S(2)}, u32[]{:S(2)}) collective-permute-start(bf16[2,256,384]{2,1,0:T(8,128)(2,1)S(1)} %maximum_select_fusion.6), channel_id=1, source_target_pairs={{0,1},{1,0},{2,3},{3,2},{4,5},{5,4},{6,7},{7,6},{8,9},{9,8},{10,11... | collective-permute-start | bytes 1179656 | tf_op jit(solution)/shard_map/ppermute | solution.py:49
  85.5 9.2 %collective-permute-start.27 = (bf16[2,256,384]{2,1,0:T(8,128)(2,1)S(1)}, bf16[2,256,384]{2,1,0:T(8,128)(2,1)S(1)}, u32[]{:S(2)}, u32[]{:S(2)}) collective-permute-start(bf16[2,256,384]{2,1,0:T(8,128)(2,1)S(1)} %maximum_select_fusion.7), channel_id=1, source_target_pairs={{0,2},{1,3},{2,0},{3,1},{4,6},{5,7},{6,4},{7,5},{8,10},{9,11},{10,... | collective-permute-start | bytes 1179656 | tf_op jit(solution)/shard_map/ppermute | solution.py:49
  88.0 9.8 %collective-permute-start.33 = (bf16[2,512,256]{2,1,0:T(8,128)(2,1)S(1)}, bf16[2,512,256]{2,1,0:T(8,128)(2,1)S(1)}, u32[]{:S(2)}, u32[]{:S(2)}) collective-permute-start(bf16[2,512,256]{2,1,0:T(8,128)(2,1)S(1)} %maximum_select_fusion.5), channel_id=1, source_target_pairs={{0,8},{1,9},{2,10},{3,11},{4,12},{5,13},{6,14},{7,15},{8,0},{9,1},... | collective-permute-start | bytes 1572872 | tf_op jit(solution)/shard_map/ppermute | solution.py:49
  105.6 10.6 %collective-permute-start.34 = (bf16[2,1,16,256]{3,2,1,0:T(8,128)(2,1)S(1)}, bf16[2,1,16,256]{3,2,1,0:T(8,128)(2,1)S(1)}, u32[]{:S(2)}, u32[]{:S(2)}) collective-permute-start(bf16[2,1,16,256]{3,2,1,0:T(8,128)(2,1)S(1)} %get-tuple-element.34), channel_id=1, source_target_pairs={{0,1},{1,2},{2,3},{3,4},{4,5},{5,6},{6,7},{8,9},{9,10},{10,11},{11... | collective-permute-start | bytes 49160 | tf_op jit(solution)/shard_map/ppermute | solution.py:15
  107.5 8.6 %collective-permute-start.35 = (bf16[2,1,16,256]{3,2,1,0:T(8,128)(2,1)S(1)}, bf16[2,1,16,256]{3,2,1,0:T(8,128)(2,1)S(1)}, u32[]{:S(2)}, u32[]{:S(2)}) collective-permute-start(bf16[2,1,16,256]{3,2,1,0:T(8,128)(2,1)S(1)} %get-tuple-element.35), channel_id=1, source_target_pairs={{1,0},{2,1},{3,2},{4,3},{5,4},{6,5},{7,6},{9,8},{10,9},{11,10},{12... | collective-permute-start | bytes 49160 | tf_op jit(solution)/shard_map/ppermute | solution.py:18
  (21 other events, 76.7 us)

commit v5 on v4

--- a/solution.py
+++ b/solution.py
@@ -52,7 +52,17 @@
 def scatter_gather(block, owner, order, col_bits, me, tie):
     done_mask = 0
     full = (1 << len(order)) - 1
-    for bit in order:
+    for step, bit in enumerate(order):
+        if step == 0:
+            half = block.shape[0] // 2
+            mine = ((me >> bit) & 1) == 1
+            keep = jnp.where(mine, block[half:], block[:half])
+            give = jnp.where(mine, block[:half], block[half:])
+            got = swap(give, bit, col_bits)
+            have = ((me ^ owner) & full) == 0
+            block = jnp.where(have[:, None, None], keep[None], got[None])
+            done_mask |= 1 << bit
+            continue
         half = block.shape[1] // 2
         mine = ((me >> bit) & 1) == 1
         low, high = block[:, :half], block[:, half:]
@@ -95,7 +105,7 @@
         cols = sizes[s] * 128
         rotated = middle[s:] + middle[:s]
         order = [core] + rotated + last
-        piece = stacked[:, :, offset : offset + cols]
+        piece = own_operator[:, offset : offset + cols]
         gathered, tie = scatter_gather(piece, owner, order, col_bits, me, tie)
         parts.append(gathered)
         offset += cols

time: 122 us -> 119 us (0.975)
  other arithmetic: 13.3 us -> 9.28 us
  waiting for transfers between devices: 31.8 us -> 35.1 us
  starting transfers between devices: 67.8 us -> 66 us
    select_n x14 -> x12, other arithmetic: 4.2 us -> 0.28 us  [scatter_gather(): give = jnp.where(mine, low, high)]
    select_n x12 -> x10, other arithmetic: 4.09 us -> 1 us  [scatter_gather(): block = jnp.where(have[:, None, None], keep, got)]
    select_n x0 -> x4, other arithmetic: none -> 2.95 us  [the longest x2 2.59 us: scatter_gather(): keep = jnp.where(mine, block[half:], block[:half])]
    ppermute x30, waiting for transfers between devices: 29 us -> 31.9 us  [swap(): return lax.ppermute(block, ('row', 'col'), pairs)]
    ppermute x30, starting transfers between devices: 36.5 us -> 35.1 us  [swap(): return lax.ppermute(block, ('row', 'col'), pairs)]
  transfers between devices with their start and end apart: 38 -> 38, of which waited for: 15 -> 15; matrix products, arithmetic and copies ran while one was open for 9% -> 7% of each run, Pallas kernels for 0% -> 0%
where the time goes in v5:
time: 119 us; the launch traced here: 118 us
  starting transfers between devices  66 us (55%)
  waiting for transfers between devices  35.1 us (29%)
  other arithmetic  9.28 us (8%)
  matrix products  5.97 us (5%)
  local copies, waits for them, and re-layouts  1.22 us (1%)
    ppermute x30, starting transfers between devices, swap(): return lax.ppermute(block, ('row', 'col'), pairs)  35.1 us
    ppermute x30, waiting for transfers between devices, swap(): return lax.ppermute(block, ('row', 'col'), pairs)  31.9 us
    ppermute x4, starting transfers between devices, shift(): return lax.ppermute(block, axis, pairs)  20.5 us
    dot_general x18, matrix products, sweep(): jnp.dot(rows, part[k], preferred_element_type=jnp.float32)  5.97 us
    ppermute x2, starting transfers between devices, with_halo(): lax.ppermute(lax.slice_in_dim(block, 0, width, axis=dim), axis, backward)  5.74 us
    ppermute x2, starting transfers between devices, with_halo(): lax.ppermute(lax.slice_in_dim(block, block.shape[dim] - width, None, axis...  4.77 us
    ppermute x2, waiting for transfers between devices, with_halo(): lax.ppermute(lax.slice_in_dim(block, 0, width, axis=dim), axis, backward)  3.23 us
    select_n x2, other arithmetic, scatter_gather(): keep = jnp.where(mine, block[half:], block[:half])  2.59 us
  transfers between devices with their start and end apart: 38, of which 15 were waited for; matrix products, arithmetic and copies ran while one was open for 7% of the time, Pallas kernels for 0%

profile of v5, /device:TPU:9, one launch (start us, length us, event | category | flops | bytes accessed | tf_op | source)
XLA Modules:
  0.0 118.5 jit_solution(305536312847561922)
XLA Ops:
  1.9 1.5 %broadcast_select_fusion.5 = (bf16[512,384]{1,0:T(8,128)(2,1)S(1)}, bf16[512,384]{1,0:T(8,128)(2,1)S(1)}, bf16[512,384]{1,0:T(8,128)(2,1)S(1)}, bf16[512,384]{1,0:T(8,128)(2,1)S(1)}) fusion(pred[]{:T(512)S(6)} %eq.139, bf16[1024,1024]{1,0:T(8,128)(2,1)} %bitcast.103), kind=kLoop, calls=%fused_computation.51 | loop fusion | flops 786432 | bytes 3145729 | tf_op jit(solution)/shard_map/jit(_where)/select_n | solution.py:59
  6.4 6.4 %collective-permute-done.1 = bf16[2,256,256]{2,1,0:T(8,128)(2,1)S(1)} collective-permute-done((bf16[2,256,256]{2,1,0:T(8,128)(2,1)S(1)}, bf16[2,256,256]{2,1,0:T(8,128)(2,1)S(1)}, u32[]{:S(2)}, u32[]{:S(2)}) %collective-permute-start.1) | collective-permute-done | bytes 262176 | tf_op jit(solution)/shard_map/ppermute | solution.py:49
  14.2 2.9 %collective-permute-done.2 = bf16[2,128,256]{2,1,0:T(8,128)(2,1)S(1)} collective-permute-done((bf16[2,128,256]{2,1,0:T(8,128)(2,1)S(1)}, bf16[2,128,256]{2,1,0:T(8,128)(2,1)S(1)}, u32[]{:S(2)}, u32[]{:S(2)}) %collective-permute-start.2) | collective-permute-done | bytes 131104 | tf_op jit(solution)/shard_map/ppermute | solution.py:49
  20.5 2.4 %collective-permute-start.4 = (bf16[2,32,256]{2,1,0:T(8,128)(2,1)S(1)}, bf16[2,32,256]{2,1,0:T(8,128)(2,1)S(1)}, u32[]{:S(2)}, u32[]{:S(2)}) collective-permute-start(bf16[2,32,256]{2,1,0:T(8,128)(2,1)S(1)} %broadcast_select_fusion.20), channel_id=1, source_target_pairs={{0,4},{1,5},{2,6},{3,7},{4,0},{5,1},{6,2},{7,3},{8,12},{9,13},{10,... | collective-permute-start | bytes 98312 | tf_op jit(solution)/shard_map/ppermute | solution.py:49
  22.9 4.7 %collective-permute-done.6 = bf16[2,256,384]{2,1,0:T(8,128)(2,1)S(1)} collective-permute-done((bf16[2,256,384]{2,1,0:T(8,128)(2,1)S(1)}, bf16[2,256,384]{2,1,0:T(8,128)(2,1)S(1)}, u32[]{:S(2)}, u32[]{:S(2)}) %collective-permute-start.6) | collective-permute-done | bytes 393248 | tf_op jit(solution)/shard_map/ppermute | solution.py:49
  29.2 2.1 %collective-permute-start.12 = (bf16[2,128,384]{2,1,0:T(8,128)(2,1)S(1)}, bf16[2,128,384]{2,1,0:T(8,128)(2,1)S(1)}, u32[]{:S(2)}, u32[]{:S(2)}) collective-permute-start(bf16[2,128,384]{2,1,0:T(8,128)(2,1)S(1)} %broadcast_select_fusion.12), channel_id=1, source_target_pairs={{0,2},{1,3},{2,0},{3,1},{4,6},{5,7},{6,4},{7,5},{8,10},{9,11},{10,... | collective-permute-start | bytes 589832 | tf_op jit(solution)/shard_map/ppermute | solution.py:49
  36.5 2.7 %collective-permute-start.9 = (bf16[2,32,384]{2,1,0:T(8,128)(2,1)S(1)}, bf16[2,32,384]{2,1,0:T(8,128)(2,1)S(1)}, u32[]{:S(2)}, u32[]{:S(2)}) collective-permute-start(bf16[2,32,384]{2,1,0:T(8,128)(2,1)S(1)} %broadcast_select_fusion.19), channel_id=1, source_target_pairs={{0,4},{1,5},{2,6},{3,7},{4,0},{5,1},{6,2},{7,3},{8,12},{9,13},{10,... | collective-permute-start | bytes 147464 | tf_op jit(solution)/shard_map/ppermute | solution.py:49
  40.7 2.6 %collective-permute-done.14 = bf16[2,32,384]{2,1,0:T(8,128)(2,1)S(1)} collective-permute-done((bf16[2,32,384]{2,1,0:T(8,128)(2,1)S(1)}, bf16[2,32,384]{2,1,0:T(8,128)(2,1)S(1)}, u32[]{:S(2)}, u32[]{:S(2)}) %collective-permute-start.14) | collective-permute-done | bytes 49184 | tf_op jit(solution)/shard_map/ppermute | solution.py:49
  47.1 3.7 %collective-permute-start.16 = (bf16[2,16,1152]{2,1,0:T(8,128)(2,1)S(1)}, bf16[2,16,1152]{2,1,0:T(8,128)(2,1)S(1)}, u32[]{:S(2)}, u32[]{:S(2)}) collective-permute-start(bf16[2,16,1152]{2,1,0:T(8,128)(2,1)S(1)} %get-tuple-element.31), channel_id=1, source_target_pairs={{1,0},{2,1},{3,2},{4,3},{5,4},{6,5},{7,6},{9,8},{10,9},{11,10},{12... | collective-permute-start | bytes 221192 | tf_op jit(solution)/shard_map/ppermute | solution.py:138
  50.8 1.9 %collective-permute-start.15 = (bf16[2,16,1152]{2,1,0:T(8,128)(2,1)S(1)}, bf16[2,16,1152]{2,1,0:T(8,128)(2,1)S(1)}, u32[]{:S(2)}, u32[]{:S(2)}) collective-permute-start(bf16[2,16,1152]{2,1,0:T(8,128)(2,1)S(1)} %get-tuple-element.32), channel_id=1, source_target_pairs={{0,1},{1,2},{2,3},{3,4},{4,5},{5,6},{6,7},{8,9},{9,10},{10,11},{11... | collective-permute-start | bytes 221192 | tf_op jit(solution)/shard_map/ppermute | solution.py:138
  52.7 11.8 %collective-permute-start.18 = (bf16[4,16,1152]{2,1,0:T(8,128)(2,1)S(1)}, bf16[4,16,1152]{2,1,0:T(8,128)(2,1)S(1)}, u32[]{:S(2)}, u32[]{:S(2)}) collective-permute-start(bf16[4,16,1152]{2,1,0:T(8,128)(2,1)S(1)} %get-tuple-element.29), channel_id=1, source_target_pairs={{8,0},{16,8},{24,16},{9,1},{17,9},{25,17},{10,2},{18,10},{26,18},{... | collective-permute-start | bytes 442376 | tf_op jit(solution)/shard_map/ppermute | solution.py:138
  64.5 3.1 %collective-permute-start.17 = (bf16[4,16,1152]{2,1,0:T(8,128)(2,1)S(1)}, bf16[4,16,1152]{2,1,0:T(8,128)(2,1)S(1)}, u32[]{:S(2)}, u32[]{:S(2)}) collective-permute-start(bf16[4,16,1152]{2,1,0:T(8,128)(2,1)S(1)} %get-tuple-element.30), channel_id=1, source_target_pairs={{0,8},{8,16},{16,24},{1,9},{9,17},{17,25},{2,10},{10,18},{18,26},{... | collective-permute-start | bytes 442376 | tf_op jit(solution)/shard_map/ppermute | solution.py:138
  67.9 2.0 %collective-permute-start.25 = (bf16[2,64,384]{2,1,0:T(8,128)(2,1)S(1)}, bf16[2,64,384]{2,1,0:T(8,128)(2,1)S(1)}, u32[]{:S(2)}, u32[]{:S(2)}) collective-permute-start(bf16[2,64,384]{2,1,0:T(8,128)(2,1)S(1)} %maximum_select_fusion.13), channel_id=1, source_target_pairs={{0,1},{1,0},{2,3},{3,2},{4,5},{5,4},{6,7},{7,6},{8,9},{9,8},{10,11... | collective-permute-start | bytes 294920 | tf_op jit(solution)/shard_map/ppermute | solution.py:49
  70.0 1.7 %collective-permute-done.30 = bf16[2,64,256]{2,1,0:T(8,128)(2,1)S(1)} collective-permute-done((bf16[2,64,256]{2,1,0:T(8,128)(2,1)S(1)}, bf16[2,64,256]{2,1,0:T(8,128)(2,1)S(1)}, u32[]{:S(2)}, u32[]{:S(2)}) %collective-permute-start.30) | collective-permute-done | bytes 65568 | tf_op jit(solution)/shard_map/ppermute | solution.py:49
  71.7 2.2 %collective-permute-start.31 = (bf16[2,128,256]{2,1,0:T(8,128)(2,1)S(1)}, bf16[2,128,256]{2,1,0:T(8,128)(2,1)S(1)}, u32[]{:S(2)}, u32[]{:S(2)}) collective-permute-start(bf16[2,128,256]{2,1,0:T(8,128)(2,1)S(1)} %maximum_select_fusion.11), channel_id=1, source_target_pairs={{0,1},{1,0},{2,3},{3,2},{4,5},{5,4},{6,7},{7,6},{8,9},{9,8},{10,11... | collective-permute-start | bytes 393224 | tf_op jit(solution)/shard_map/ppermute | solution.py:49
  77.7 2.8 %collective-permute-done.21 = bf16[2,128,384]{2,1,0:T(8,128)(2,1)S(1)} collective-permute-done((bf16[2,128,384]{2,1,0:T(8,128)(2,1)S(1)}, bf16[2,128,384]{2,1,0:T(8,128)(2,1)S(1)}, u32[]{:S(2)}, u32[]{:S(2)}) %collective-permute-start.21) | collective-permute-done | bytes 196640 | tf_op jit(solution)/shard_map/ppermute | solution.py:49
  82.7 3.0 %collective-permute-done.32 = bf16[2,256,256]{2,1,0:T(8,128)(2,1)S(1)} collective-permute-done((bf16[2,256,256]{2,1,0:T(8,128)(2,1)S(1)}, bf16[2,256,256]{2,1,0:T(8,128)(2,1)S(1)}, u32[]{:S(2)}, u32[]{:S(2)}) %collective-permute-start.32) | collective-permute-done | bytes 262176 | tf_op jit(solution)/shard_map/ppermute | solution.py:49
  87.7 2.5 %collective-permute-done.27 = bf16[2,256,384]{2,1,0:T(8,128)(2,1)S(1)} collective-permute-done((bf16[2,256,384]{2,1,0:T(8,128)(2,1)S(1)}, bf16[2,256,384]{2,1,0:T(8,128)(2,1)S(1)}, u32[]{:S(2)}, u32[]{:S(2)}) %collective-permute-start.27) | collective-permute-done | bytes 393248 | tf_op jit(solution)/shard_map/ppermute | solution.py:49
  90.5 3.3 %collective-permute-start.28 = (bf16[2,512,384]{2,1,0:T(8,128)(2,1)S(1)}, bf16[2,512,384]{2,1,0:T(8,128)(2,1)S(1)}, u32[]{:S(2)}, u32[]{:S(2)}) collective-permute-start(bf16[2,512,384]{2,1,0:T(8,128)(2,1)S(1)} %maximum_select_fusion.4), channel_id=1, source_target_pairs={{0,8},{1,9},{2,10},{3,11},{4,12},{5,13},{6,14},{7,15},{8,0},{9,1},... | collective-permute-start | bytes 2359304 | tf_op jit(solution)/shard_map/ppermute | solution.py:49
  102.0 2.4 %collective-permute-start.34 = (bf16[2,1,16,256]{3,2,1,0:T(8,128)(2,1)S(1)}, bf16[2,1,16,256]{3,2,1,0:T(8,128)(2,1)S(1)}, u32[]{:S(2)}, u32[]{:S(2)}) collective-permute-start(bf16[2,1,16,256]{3,2,1,0:T(8,128)(2,1)S(1)} %get-tuple-element.33), channel_id=1, source_target_pairs={{0,1},{1,2},{2,3},{3,4},{4,5},{5,6},{6,7},{8,9},{9,10},{10,11},{11... | collective-permute-start | bytes 49160 | tf_op jit(solution)/shard_map/ppermute | solution.py:15
  104.4 3.8 %collective-permute-start.35 = (bf16[2,1,16,256]{3,2,1,0:T(8,128)(2,1)S(1)}, bf16[2,1,16,256]{3,2,1,0:T(8,128)(2,1)S(1)}, u32[]{:S(2)}, u32[]{:S(2)}) collective-permute-start(bf16[2,1,16,256]{3,2,1,0:T(8,128)(2,1)S(1)} %get-tuple-element.34), channel_id=1, source_target_pairs={{1,0},{2,1},{3,2},{4,3},{5,4},{6,5},{7,6},{9,8},{10,9},{11,10},{12... | collective-permute-start | bytes 49160 | tf_op jit(solution)/shard_map/ppermute | solution.py:18
  108.2 2.4 %collective-permute-start.36 = (bf16[1,4,16,256]{3,2,1,0:T(8,128)(2,1)S(1)}, bf16[1,4,16,256]{3,2,1,0:T(8,128)(2,1)S(1)}, u32[]{:S(2)}, u32[]{:S(2)}) collective-permute-start(bf16[1,4,16,256]{3,2,1,0:T(8,128)(2,1)S(1)} %get-tuple-element.37), channel_id=1, source_target_pairs={{0,8},{8,16},{16,24},{1,9},{9,17},{17,25},{2,10},{10,18},{18,26},{... | collective-permute-start | bytes 98312 | tf_op jit(solution)/shard_map/ppermute | solution.py:15
  110.6 2.0 %collective-permute-start.37 = (bf16[1,4,16,256]{3,2,1,0:T(8,128)(2,1)S(1)}, bf16[1,4,16,256]{3,2,1,0:T(8,128)(2,1)S(1)}, u32[]{:S(2)}, u32[]{:S(2)}) collective-permute-start(bf16[1,4,16,256]{3,2,1,0:T(8,128)(2,1)S(1)} %get-tuple-element.38), channel_id=1, source_target_pairs={{8,0},{16,8},{24,16},{9,1},{17,9},{25,17},{10,2},{18,10},{26,18},{... | collective-permute-start | bytes 98312 | tf_op jit(solution)/shard_map/ppermute | solution.py:18
  112.6 3.2 %collective-permute-done.37 = bf16[1,4,16,256]{3,2,1,0:T(8,128)(2,1)S(1)} collective-permute-done((bf16[1,4,16,256]{3,2,1,0:T(8,128)(2,1)S(1)}, bf16[1,4,16,256]{3,2,1,0:T(8,128)(2,1)S(1)}, u32[]{:S(2)}, u32[]{:S(2)}) %collective-permute-start.37) | collective-permute-done | bytes 32800 | tf_op jit(solution)/shard_map/ppermute | solution.py:18
  (166 shorter events, 40.6 us)
Async XLA Ops:
  4.8 8.0 %collective-permute-start.1 = (bf16[2,256,256]{2,1,0:T(8,128)(2,1)S(1)}, bf16[2,256,256]{2,1,0:T(8,128)(2,1)S(1)}, u32[]{:S(2)}, u32[]{:S(2)}) collective-permute-start(bf16[2,256,256]{2,1,0:T(8,128)(2,1)S(1)} %broadcast_select_fusion.11), channel_id=1, source_target_pairs={{0,16},{1,17},{2,18},{3,19},{4,20},{5,21},{6,22},{7,23},{8,24},{9,... | collective-permute-start | bytes 786440 | tf_op jit(solution)/shard_map/ppermute | solution.py:49
  17.7 9.9 %collective-permute-start.6 = (bf16[2,256,384]{2,1,0:T(8,128)(2,1)S(1)}, bf16[2,256,384]{2,1,0:T(8,128)(2,1)S(1)}, u32[]{:S(2)}, u32[]{:S(2)}) collective-permute-start(bf16[2,256,384]{2,1,0:T(8,128)(2,1)S(1)} %broadcast_select_fusion.8), channel_id=1, source_target_pairs={{0,2},{1,3},{2,0},{3,1},{4,6},{5,7},{6,4},{7,5},{8,10},{9,11},{10,... | collective-permute-start | bytes 1179656 | tf_op jit(solution)/shard_map/ppermute | solution.py:49
  18.9 8.7 %collective-permute-start.11 = (bf16[2,256,384]{2,1,0:T(8,128)(2,1)S(1)}, bf16[2,256,384]{2,1,0:T(8,128)(2,1)S(1)}, u32[]{:S(2)}, u32[]{:S(2)}) collective-permute-start(bf16[2,256,384]{2,1,0:T(8,128)(2,1)S(1)} %broadcast_select_fusion.3), channel_id=1, source_target_pairs={{0,1},{1,0},{2,3},{3,2},{4,5},{5,4},{6,7},{7,6},{8,9},{9,8},{10,11... | collective-permute-start | bytes 1179656 | tf_op jit(solution)/shard_map/ppermute | solution.py:49
  20.5 20.1 %collective-permute-start.4 = (bf16[2,32,256]{2,1,0:T(8,128)(2,1)S(1)}, bf16[2,32,256]{2,1,0:T(8,128)(2,1)S(1)}, u32[]{:S(2)}, u32[]{:S(2)}) collective-permute-start(bf16[2,32,256]{2,1,0:T(8,128)(2,1)S(1)} %broadcast_select_fusion.20), channel_id=1, source_target_pairs={{0,4},{1,5},{2,6},{3,7},{4,0},{5,1},{6,2},{7,3},{8,12},{9,13},{10,... | collective-permute-start | bytes 98312 | tf_op jit(solution)/shard_map/ppermute | solution.py:49
  29.2 5.4 %collective-permute-start.12 = (bf16[2,128,384]{2,1,0:T(8,128)(2,1)S(1)}, bf16[2,128,384]{2,1,0:T(8,128)(2,1)S(1)}, u32[]{:S(2)}, u32[]{:S(2)}) collective-permute-start(bf16[2,128,384]{2,1,0:T(8,128)(2,1)S(1)} %broadcast_select_fusion.12), channel_id=1, source_target_pairs={{0,2},{1,3},{2,0},{3,1},{4,6},{5,7},{6,4},{7,5},{8,10},{9,11},{10,... | collective-permute-start | bytes 589832 | tf_op jit(solution)/shard_map/ppermute | solution.py:49
  43.4 9.3 %collective-permute-start.29 = (bf16[2,32,256]{2,1,0:T(8,128)(2,1)S(1)}, bf16[2,32,256]{2,1,0:T(8,128)(2,1)S(1)}, u32[]{:S(2)}, u32[]{:S(2)}) collective-permute-start(bf16[2,32,256]{2,1,0:T(8,128)(2,1)S(1)} %select_select_fusion.11), channel_id=1, source_target_pairs={{0,4},{1,5},{2,6},{3,7},{4,0},{5,1},{6,2},{7,3},{8,12},{9,13},{10,... | collective-permute-start | bytes 98312 | tf_op jit(solution)/shard_map/ppermute | solution.py:49
  44.7 19.9 %collective-permute-start.24 = (bf16[2,32,384]{2,1,0:T(8,128)(2,1)S(1)}, bf16[2,32,384]{2,1,0:T(8,128)(2,1)S(1)}, u32[]{:S(2)}, u32[]{:S(2)}) collective-permute-start(bf16[2,32,384]{2,1,0:T(8,128)(2,1)S(1)} %get-tuple-element.15), channel_id=1, source_target_pairs={{0,4},{1,5},{2,6},{3,7},{4,0},{5,1},{6,2},{7,3},{8,12},{9,13},{10,... | collective-permute-start | bytes 147464 | tf_op jit(solution)/shard_map/ppermute | solution.py:49
  46.0 21.7 %collective-permute-start.19 = (bf16[2,32,384]{2,1,0:T(8,128)(2,1)S(1)}, bf16[2,32,384]{2,1,0:T(8,128)(2,1)S(1)}, u32[]{:S(2)}, u32[]{:S(2)}) collective-permute-start(bf16[2,32,384]{2,1,0:T(8,128)(2,1)S(1)} %get-tuple-element.14), channel_id=1, source_target_pairs={{0,4},{1,5},{2,6},{3,7},{4,0},{5,1},{6,2},{7,3},{8,12},{9,13},{10,... | collective-permute-start | bytes 147464 | tf_op jit(solution)/shard_map/ppermute | solution.py:49
  47.1 20.8 %collective-permute-start.16 = (bf16[2,16,1152]{2,1,0:T(8,128)(2,1)S(1)}, bf16[2,16,1152]{2,1,0:T(8,128)(2,1)S(1)}, u32[]{:S(2)}, u32[]{:S(2)}) collective-permute-start(bf16[2,16,1152]{2,1,0:T(8,128)(2,1)S(1)} %get-tuple-element.31), channel_id=1, source_target_pairs={{1,0},{2,1},{3,2},{4,3},{5,4},{6,5},{7,6},{9,8},{10,9},{11,10},{12... | collective-permute-start | bytes 221192 | tf_op jit(solution)/shard_map/ppermute | solution.py:138
  50.8 17.0 %collective-permute-start.15 = (bf16[2,16,1152]{2,1,0:T(8,128)(2,1)S(1)}, bf16[2,16,1152]{2,1,0:T(8,128)(2,1)S(1)}, u32[]{:S(2)}, u32[]{:S(2)}) collective-permute-start(bf16[2,16,1152]{2,1,0:T(8,128)(2,1)S(1)} %get-tuple-element.32), channel_id=1, source_target_pairs={{0,1},{1,2},{2,3},{3,4},{4,5},{5,6},{6,7},{8,9},{9,10},{10,11},{11... | collective-permute-start | bytes 221192 | tf_op jit(solution)/shard_map/ppermute | solution.py:138
  52.7 24.9 %collective-permute-start.18 = (bf16[4,16,1152]{2,1,0:T(8,128)(2,1)S(1)}, bf16[4,16,1152]{2,1,0:T(8,128)(2,1)S(1)}, u32[]{:S(2)}, u32[]{:S(2)}) collective-permute-start(bf16[4,16,1152]{2,1,0:T(8,128)(2,1)S(1)} %get-tuple-element.29), channel_id=1, source_target_pairs={{8,0},{16,8},{24,16},{9,1},{17,9},{25,17},{10,2},{18,10},{26,18},{... | collective-permute-start | bytes 442376 | tf_op jit(solution)/shard_map/ppermute | solution.py:138
  64.5 9.3 %collective-permute-start.17 = (bf16[4,16,1152]{2,1,0:T(8,128)(2,1)S(1)}, bf16[4,16,1152]{2,1,0:T(8,128)(2,1)S(1)}, u32[]{:S(2)}, u32[]{:S(2)}) collective-permute-start(bf16[4,16,1152]{2,1,0:T(8,128)(2,1)S(1)} %get-tuple-element.30), channel_id=1, source_target_pairs={{0,8},{8,16},{16,24},{1,9},{9,17},{17,25},{2,10},{10,18},{18,26},{... | collective-permute-start | bytes 442376 | tf_op jit(solution)/shard_map/ppermute | solution.py:138
  67.8 6.9 %collective-permute-start.20 = (bf16[2,64,384]{2,1,0:T(8,128)(2,1)S(1)}, bf16[2,64,384]{2,1,0:T(8,128)(2,1)S(1)}, u32[]{:S(2)}, u32[]{:S(2)}) collective-permute-start(bf16[2,64,384]{2,1,0:T(8,128)(2,1)S(1)} %maximum_select_fusion.12), channel_id=1, source_target_pairs={{0,16},{1,17},{2,18},{3,19},{4,20},{5,21},{6,22},{7,23},{8,24},{9,... | collective-permute-start | bytes 294920 | tf_op jit(solution)/shard_map/ppermute | solution.py:49
  67.9 6.0 %collective-permute-start.25 = (bf16[2,64,384]{2,1,0:T(8,128)(2,1)S(1)}, bf16[2,64,384]{2,1,0:T(8,128)(2,1)S(1)}, u32[]{:S(2)}, u32[]{:S(2)}) collective-permute-start(bf16[2,64,384]{2,1,0:T(8,128)(2,1)S(1)} %maximum_select_fusion.13), channel_id=1, source_target_pairs={{0,1},{1,0},{2,3},{3,2},{4,5},{5,4},{6,7},{7,6},{8,9},{9,8},{10,11... | collective-permute-start | bytes 294920 | tf_op jit(solution)/shard_map/ppermute | solution.py:49
  71.7 5.8 %collective-permute-start.31 = (bf16[2,128,256]{2,1,0:T(8,128)(2,1)S(1)}, bf16[2,128,256]{2,1,0:T(8,128)(2,1)S(1)}, u32[]{:S(2)}, u32[]{:S(2)}) collective-permute-start(bf16[2,128,256]{2,1,0:T(8,128)(2,1)S(1)} %maximum_select_fusion.11), channel_id=1, source_target_pairs={{0,1},{1,0},{2,3},{3,2},{4,5},{5,4},{6,7},{7,6},{8,9},{9,8},{10,11... | collective-permute-start | bytes 393224 | tf_op jit(solution)/shard_map/ppermute | solution.py:49
  73.9 7.8 %collective-permute-start.26 = (bf16[2,128,384]{2,1,0:T(8,128)(2,1)S(1)}, bf16[2,128,384]{2,1,0:T(8,128)(2,1)S(1)}, u32[]{:S(2)}, u32[]{:S(2)}) collective-permute-start(bf16[2,128,384]{2,1,0:T(8,128)(2,1)S(1)} %maximum_select_fusion.10), channel_id=1, source_target_pairs={{0,16},{1,17},{2,18},{3,19},{4,20},{5,21},{6,22},{7,23},{8,24},{9,... | collective-permute-start | bytes 589832 | tf_op jit(solution)/shard_map/ppermute | solution.py:49
  74.8 5.8 %collective-permute-start.21 = (bf16[2,128,384]{2,1,0:T(8,128)(2,1)S(1)}, bf16[2,128,384]{2,1,0:T(8,128)(2,1)S(1)}, u32[]{:S(2)}, u32[]{:S(2)}) collective-permute-start(bf16[2,128,384]{2,1,0:T(8,128)(2,1)S(1)} %maximum_select_fusion.9), channel_id=1, source_target_pairs={{0,2},{1,3},{2,0},{3,1},{4,6},{5,7},{6,4},{7,5},{8,10},{9,11},{10,... | collective-permute-start | bytes 589832 | tf_op jit(solution)/shard_map/ppermute | solution.py:49
  77.6 8.2 %collective-permute-start.32 = (bf16[2,256,256]{2,1,0:T(8,128)(2,1)S(1)}, bf16[2,256,256]{2,1,0:T(8,128)(2,1)S(1)}, u32[]{:S(2)}, u32[]{:S(2)}) collective-permute-start(bf16[2,256,256]{2,1,0:T(8,128)(2,1)S(1)} %maximum_select_fusion.8), channel_id=1, source_target_pairs={{0,16},{1,17},{2,18},{3,19},{4,20},{5,21},{6,22},{7,23},{8,24},{9,... | collective-permute-start | bytes 786440 | tf_op jit(solution)/shard_map/ppermute | solution.py:49
  80.7 13.1 %collective-permute-start.22 = (bf16[2,256,384]{2,1,0:T(8,128)(2,1)S(1)}, bf16[2,256,384]{2,1,0:T(8,128)(2,1)S(1)}, u32[]{:S(2)}, u32[]{:S(2)}) collective-permute-start(bf16[2,256,384]{2,1,0:T(8,128)(2,1)S(1)} %maximum_select_fusion.6), channel_id=1, source_target_pairs={{0,1},{1,0},{2,3},{3,2},{4,5},{5,4},{6,7},{7,6},{8,9},{9,8},{10,11... | collective-permute-start | bytes 1179656 | tf_op jit(solution)/shard_map/ppermute | solution.py:49
  81.9 8.4 %collective-permute-start.27 = (bf16[2,256,384]{2,1,0:T(8,128)(2,1)S(1)}, bf16[2,256,384]{2,1,0:T(8,128)(2,1)S(1)}, u32[]{:S(2)}, u32[]{:S(2)}) collective-permute-start(bf16[2,256,384]{2,1,0:T(8,128)(2,1)S(1)} %maximum_select_fusion.7), channel_id=1, source_target_pairs={{0,2},{1,3},{2,0},{3,1},{4,6},{5,7},{6,4},{7,5},{8,10},{9,11},{10,... | collective-permute-start | bytes 1179656 | tf_op jit(solution)/shard_map/ppermute | solution.py:49
  86.0 8.2 %collective-permute-start.33 = (bf16[2,512,256]{2,1,0:T(8,128)(2,1)S(1)}, bf16[2,512,256]{2,1,0:T(8,128)(2,1)S(1)}, u32[]{:S(2)}, u32[]{:S(2)}) collective-permute-start(bf16[2,512,256]{2,1,0:T(8,128)(2,1)S(1)} %maximum_select_fusion.5), channel_id=1, source_target_pairs={{0,8},{1,9},{2,10},{3,11},{4,12},{5,13},{6,14},{7,15},{8,0},{9,1},... | collective-permute-start | bytes 1572872 | tf_op jit(solution)/shard_map/ppermute | solution.py:49
  102.0 10.6 %collective-permute-start.34 = (bf16[2,1,16,256]{3,2,1,0:T(8,128)(2,1)S(1)}, bf16[2,1,16,256]{3,2,1,0:T(8,128)(2,1)S(1)}, u32[]{:S(2)}, u32[]{:S(2)}) collective-permute-start(bf16[2,1,16,256]{3,2,1,0:T(8,128)(2,1)S(1)} %get-tuple-element.33), channel_id=1, source_target_pairs={{0,1},{1,2},{2,3},{3,4},{4,5},{5,6},{6,7},{8,9},{9,10},{10,11},{11... | collective-permute-start | bytes 49160 | tf_op jit(solution)/shard_map/ppermute | solution.py:15
  104.4 8.2 %collective-permute-start.35 = (bf16[2,1,16,256]{3,2,1,0:T(8,128)(2,1)S(1)}, bf16[2,1,16,256]{3,2,1,0:T(8,128)(2,1)S(1)}, u32[]{:S(2)}, u32[]{:S(2)}) collective-permute-start(bf16[2,1,16,256]{3,2,1,0:T(8,128)(2,1)S(1)} %get-tuple-element.34), channel_id=1, source_target_pairs={{1,0},{2,1},{3,2},{4,3},{5,4},{6,5},{7,6},{9,8},{10,9},{11,10},{12... | collective-permute-start | bytes 49160 | tf_op jit(solution)/shard_map/ppermute | solution.py:18
  110.6 5.2 %collective-permute-start.37 = (bf16[1,4,16,256]{3,2,1,0:T(8,128)(2,1)S(1)}, bf16[1,4,16,256]{3,2,1,0:T(8,128)(2,1)S(1)}, u32[]{:S(2)}, u32[]{:S(2)}) collective-permute-start(bf16[1,4,16,256]{3,2,1,0:T(8,128)(2,1)S(1)} %get-tuple-element.38), channel_id=1, source_target_pairs={{8,0},{16,8},{24,16},{9,1},{17,9},{25,17},{10,2},{18,10},{26,18},{... | collective-permute-start | bytes 98312 | tf_op jit(solution)/shard_map/ppermute | solution.py:18
  (19 other events, 67.8 us)

commit v6 on v4

--- a/solution.py
+++ b/solution.py
@@ -49,28 +49,41 @@
     return lax.ppermute(block, ("row", "col"), pairs)
 
 
-def scatter_gather(block, owner, order, col_bits, me, tie):
-    done_mask = 0
-    full = (1 << len(order)) - 1
-    for bit in order:
-        half = block.shape[1] // 2
-        mine = ((me >> bit) & 1) == 1
-        low, high = block[:, :half], block[:, half:]
-        keep = jnp.where(mine, high, low)
-        give = jnp.where(mine, low, high)
-        got = swap(give, bit, col_bits)
-        outside = full & ~done_mask
-        have = ((me ^ owner) & outside) == 0
-        block = jnp.where(have[:, None, None], keep, got)
-        done_mask |= 1 << bit
-    block, tie = lax.optimization_barrier((block, tie))
-    for bit in reversed(order):
-        mine = ((me >> bit) & 1) == 1
-        got = swap(block, bit, col_bits)
-        block = jnp.where(
-            mine, jnp.concatenate([got, block], axis=1), jnp.concatenate([block, got], axis=1)
-        )
-    return block, tie
+def scatter_gather(blocks, owner, orders, col_bits, me, tie):
+    stages = len(orders[0])
+    full = (1 << stages) - 1
+    done_mask = [0] * len(blocks)
+    for step in range(stages):
+        gots, keeps = [], []
+        for s, block in enumerate(blocks):
+            bit = orders[s][step]
+            mine = ((me >> bit) & 1) == 1
+            if step == 0:
+                half = block.shape[0] // 2
+                keep = jnp.where(mine, block[half:], block[:half])[None]
+                give = jnp.where(mine, block[:half], block[half:])
+            else:
+                half = block.shape[1] // 2
+                keep = jnp.where(mine, block[:, half:], block[:, :half])
+                give = jnp.where(mine, block[:, :half], block[:, half:])
+            got = swap(give, bit, col_bits)
+            keeps.append(keep)
+            gots.append(got[None] if step == 0 else got)
+        for s in range(len(blocks)):
+            have = ((me ^ owner) & (full & ~done_mask[s])) == 0
+            blocks[s] = jnp.where(have[:, None, None], keeps[s], gots[s])
+            done_mask[s] |= 1 << orders[s][step]
+        blocks = list(lax.optimization_barrier(tuple(blocks)))
+    blocks, tie = lax.optimization_barrier((tuple(blocks), tie))
+    blocks = list(blocks)
+    for step in reversed(range(stages)):
+        gots = [swap(block, orders[s][step], col_bits) for s, block in enumerate(blocks)]
+        for s in range(len(blocks)):
+            mine = ((me >> orders[s][step]) & 1) == 1
+            blocks[s] = jnp.where(
+                mine, jnp.concatenate([gots[s], blocks[s]], axis=1), jnp.concatenate([blocks[s], gots[s]], axis=1)
+            )
+    return blocks, tie
 
 
 def broadcast_parts(own_operator, owner, tie):
@@ -89,16 +102,14 @@
     width = own_operator.shape[1]
     unit = width // 128
     sizes = [unit // streams + (1 if s < unit % streams else 0) for s in range(streams)]
-    parts = []
+    blocks, orders = [], []
     offset = 0
     for s in range(streams):
         cols = sizes[s] * 128
-        rotated = middle[s:] + middle[:s]
-        order = [core] + rotated + last
-        piece = stacked[:, :, offset : offset + cols]
-        gathered, tie = scatter_gather(piece, owner, order, col_bits, me, tie)
-        parts.append(gathered)
+        orders.append([core] + middle[s:] + middle[:s] + last)
+        blocks.append(own_operator[:, offset : offset + cols])
         offset += cols
+    parts, tie = scatter_gather(blocks, owner, orders, col_bits, me, tie)
     return parts, tie
 
 

time: 122 us -> 114 us (0.934)
  starting transfers between devices: 67.8 us -> 62.5 us
  other arithmetic: 13.3 us -> 9.96 us
    ppermute x30, starting transfers between devices: 36.5 us -> 32.5 us  [swap(): return lax.ppermute(block, ('row', 'col'), pairs)]
    select_n x41, other arithmetic: 10.8 us -> 7.46 us  [the longest x2 3.29 us: scatter_gather(): keep = jnp.where(mine, block[half:], block[:half])[None]]
    ppermute x4, starting transfers between devices: 20.8 us -> 19.2 us  [shift(): return lax.ppermute(block, axis, pairs)]
  transfers between devices with their start and end apart: 38 -> 38, of which waited for: 15 -> 19; matrix products, arithmetic and copies ran while one was open for 9% -> 6% of each run, Pallas kernels for 0% -> 0%
where the time goes in v6:
time: 114 us; the launch traced here: 113 us
  starting transfers between devices  62.5 us (55%)
  waiting for transfers between devices  32.8 us (29%)
  other arithmetic  9.96 us (9%)
  matrix products  5.98 us (5%)
  local copies, waits for them, and re-layouts  1.2 us (1%)
    ppermute x30, starting transfers between devices, swap(): return lax.ppermute(block, ('row', 'col'), pairs)  32.5 us
    ppermute x30, waiting for transfers between devices, swap(): return lax.ppermute(block, ('row', 'col'), pairs)  29.5 us
    ppermute x4, starting transfers between devices, shift(): return lax.ppermute(block, axis, pairs)  19.2 us
    dot_general x18, matrix products, sweep(): jnp.dot(rows, part[k], preferred_element_type=jnp.float32)  5.98 us
    ppermute x2, starting transfers between devices, with_halo(): lax.ppermute(lax.slice_in_dim(block, 0, width, axis=dim), axis, backward)  5.84 us
    ppermute x2, starting transfers between devices, with_halo(): lax.ppermute(lax.slice_in_dim(block, block.shape[dim] - width, None, axis...  4.93 us
    select_n x2, other arithmetic, scatter_gather(): keep = jnp.where(mine, block[half:], block[:half])[None]  3.29 us
    ppermute x2, waiting for transfers between devices, with_halo(): lax.ppermute(lax.slice_in_dim(block, 0, width, axis=dim), axis, backward)  3.26 us
  transfers between devices with their start and end apart: 38, of which 19 were waited for; matrix products, arithmetic and copies ran while one was open for 6% of the time, Pallas kernels for 0%

profile of v6, /device:TPU:9, one launch (start us, length us, event | category | flops | bytes accessed | tf_op | source)
XLA Modules:
  0.0 113.2 jit_solution(3947062130265469839)
XLA Ops:
  0.0 1.8 %broadcast_select_fusion.11 = (bf16[512,256]{1,0:T(8,128)(2,1)S(1)}, bf16[512,256]{1,0:T(8,128)(2,1)}) fusion(pred[]{:T(512)S(6)} %eq.139, bf16[1024,1024]{1,0:T(8,128)(2,1)} %bitcast.102), kind=kLoop, calls=%fused_computation.62 | loop fusion | flops 262144 | bytes 1048577 | tf_op jit(solution)/shard_map/jit(_where)/select_n | solution.py:63
  9.6 4.9 %collective-permute-done.5 = bf16[2,256,256]{2,1,0:T(8,128)(2,1)S(1)} collective-permute-done((bf16[2,256,256]{2,1,0:T(8,128)(2,1)S(1)}, bf16[2,256,256]{2,1,0:T(8,128)(2,1)S(1)}, u32[]{:S(2)}, u32[]{:S(2)}) %collective-permute-start.5) | collective-permute-done | bytes 262176 | tf_op jit(solution)/shard_map/ppermute | solution.py:49
  14.6 3.7 %collective-permute-done.4 = bf16[2,256,384]{2,1,0:T(8,128)(2,1)S(1)} collective-permute-done((bf16[2,256,384]{2,1,0:T(8,128)(2,1)S(1)}, bf16[2,256,384]{2,1,0:T(8,128)(2,1)S(1)}, u32[]{:S(2)}, u32[]{:S(2)}) %collective-permute-start.4) | collective-permute-done | bytes 393248 | tf_op jit(solution)/shard_map/ppermute | solution.py:49
  22.6 2.2 %collective-permute-done.7 = bf16[2,128,384]{2,1,0:T(8,128)(2,1)S(1)} collective-permute-done((bf16[2,128,384]{2,1,0:T(8,128)(2,1)S(1)}, bf16[2,128,384]{2,1,0:T(8,128)(2,1)S(1)}, u32[]{:S(2)}, u32[]{:S(2)}) %collective-permute-start.7) | collective-permute-done | bytes 196640 | tf_op jit(solution)/shard_map/ppermute | solution.py:49
  28.5 1.6 %collective-permute-done.10 = bf16[2,64,384]{2,1,0:T(8,128)(2,1)S(1)} collective-permute-done((bf16[2,64,384]{2,1,0:T(8,128)(2,1)S(1)}, bf16[2,64,384]{2,1,0:T(8,128)(2,1)S(1)}, u32[]{:S(2)}, u32[]{:S(2)}) %collective-permute-start.10) | collective-permute-done | bytes 98336 | tf_op jit(solution)/shard_map/ppermute | solution.py:49
  30.5 2.4 %collective-permute-start.14 = (bf16[2,32,256]{2,1,0:T(8,128)(2,1)S(1)}, bf16[2,32,256]{2,1,0:T(8,128)(2,1)S(1)}, u32[]{:S(2)}, u32[]{:S(2)}) collective-permute-start(bf16[2,32,256]{2,1,0:T(8,128)(2,1)S(1)} %broadcast_select_fusion.20), channel_id=1, source_target_pairs={{0,4},{1,5},{2,6},{3,7},{4,0},{5,1},{6,2},{7,3},{8,12},{9,13},{10,... | collective-permute-start | bytes 98312 | tf_op jit(solution)/shard_map/ppermute | solution.py:49
  33.0 2.3 %collective-permute-start.12 = (bf16[2,32,384]{2,1,0:T(8,128)(2,1)S(1)}, bf16[2,32,384]{2,1,0:T(8,128)(2,1)S(1)}, u32[]{:S(2)}, u32[]{:S(2)}) collective-permute-start(bf16[2,32,384]{2,1,0:T(8,128)(2,1)S(1)} %broadcast_select_fusion.19), channel_id=1, source_target_pairs={{0,4},{1,5},{2,6},{3,7},{4,0},{5,1},{6,2},{7,3},{8,12},{9,13},{10,... | collective-permute-start | bytes 147464 | tf_op jit(solution)/shard_map/ppermute | solution.py:49
  37.5 2.3 %collective-permute-start.29 = (bf16[2,32,256]{2,1,0:T(8,128)(2,1)S(1)}, bf16[2,32,256]{2,1,0:T(8,128)(2,1)S(1)}, u32[]{:S(2)}, u32[]{:S(2)}) collective-permute-start(bf16[2,32,256]{2,1,0:T(8,128)(2,1)S(1)} %select_select_fusion.11), channel_id=1, source_target_pairs={{0,4},{1,5},{2,6},{3,7},{4,0},{5,1},{6,2},{7,3},{8,12},{9,13},{10,... | collective-permute-start | bytes 98312 | tf_op jit(solution)/shard_map/ppermute | solution.py:49
  40.0 2.2 %collective-permute-start.24 = (bf16[2,32,384]{2,1,0:T(8,128)(2,1)S(1)}, bf16[2,32,384]{2,1,0:T(8,128)(2,1)S(1)}, u32[]{:S(2)}, u32[]{:S(2)}) collective-permute-start(bf16[2,32,384]{2,1,0:T(8,128)(2,1)S(1)} %get-tuple-element.41), channel_id=1, source_target_pairs={{0,4},{1,5},{2,6},{3,7},{4,0},{5,1},{6,2},{7,3},{8,12},{9,13},{10,... | collective-permute-start | bytes 147464 | tf_op jit(solution)/shard_map/ppermute | solution.py:49
  42.2 2.6 %collective-permute-start.16 = (bf16[2,16,1152]{2,1,0:T(8,128)(2,1)S(1)}, bf16[2,16,1152]{2,1,0:T(8,128)(2,1)S(1)}, u32[]{:S(2)}, u32[]{:S(2)}) collective-permute-start(bf16[2,16,1152]{2,1,0:T(8,128)(2,1)S(1)} %get-tuple-element.57), channel_id=1, source_target_pairs={{1,0},{2,1},{3,2},{4,3},{5,4},{6,5},{7,6},{9,8},{10,9},{11,10},{12... | collective-permute-start | bytes 221192 | tf_op jit(solution)/shard_map/ppermute | solution.py:139
  44.8 2.7 %collective-permute-start.15 = (bf16[2,16,1152]{2,1,0:T(8,128)(2,1)S(1)}, bf16[2,16,1152]{2,1,0:T(8,128)(2,1)S(1)}, u32[]{:S(2)}, u32[]{:S(2)}) collective-permute-start(bf16[2,16,1152]{2,1,0:T(8,128)(2,1)S(1)} %get-tuple-element.58), channel_id=1, source_target_pairs={{0,1},{1,2},{2,3},{3,4},{4,5},{5,6},{6,7},{8,9},{9,10},{10,11},{11... | collective-permute-start | bytes 221192 | tf_op jit(solution)/shard_map/ppermute | solution.py:139
  47.5 10.9 %collective-permute-start.18 = (bf16[4,16,1152]{2,1,0:T(8,128)(2,1)S(1)}, bf16[4,16,1152]{2,1,0:T(8,128)(2,1)S(1)}, u32[]{:S(2)}, u32[]{:S(2)}) collective-permute-start(bf16[4,16,1152]{2,1,0:T(8,128)(2,1)S(1)} %get-tuple-element.55), channel_id=1, source_target_pairs={{8,0},{16,8},{24,16},{9,1},{17,9},{25,17},{10,2},{18,10},{26,18},{... | collective-permute-start | bytes 442376 | tf_op jit(solution)/shard_map/ppermute | solution.py:139
  58.5 3.0 %collective-permute-start.17 = (bf16[4,16,1152]{2,1,0:T(8,128)(2,1)S(1)}, bf16[4,16,1152]{2,1,0:T(8,128)(2,1)S(1)}, u32[]{:S(2)}, u32[]{:S(2)}) collective-permute-start(bf16[4,16,1152]{2,1,0:T(8,128)(2,1)S(1)} %get-tuple-element.56), channel_id=1, source_target_pairs={{0,8},{8,16},{16,24},{1,9},{9,17},{17,25},{2,10},{10,18},{18,26},{... | collective-permute-start | bytes 442376 | tf_op jit(solution)/shard_map/ppermute | solution.py:139
  61.7 2.2 %collective-permute-start.25 = (bf16[2,64,384]{2,1,0:T(8,128)(2,1)S(1)}, bf16[2,64,384]{2,1,0:T(8,128)(2,1)S(1)}, u32[]{:S(2)}, u32[]{:S(2)}) collective-permute-start(bf16[2,64,384]{2,1,0:T(8,128)(2,1)S(1)} %maximum_select_fusion.13), channel_id=1, source_target_pairs={{0,1},{1,0},{2,3},{3,2},{4,5},{5,4},{6,7},{7,6},{8,9},{9,8},{10,11... | collective-permute-start | bytes 294920 | tf_op jit(solution)/shard_map/ppermute | solution.py:49
  65.6 2.2 %collective-permute-start.31 = (bf16[2,128,256]{2,1,0:T(8,128)(2,1)S(1)}, bf16[2,128,256]{2,1,0:T(8,128)(2,1)S(1)}, u32[]{:S(2)}, u32[]{:S(2)}) collective-permute-start(bf16[2,128,256]{2,1,0:T(8,128)(2,1)S(1)} %maximum_select_fusion.11), channel_id=1, source_target_pairs={{0,1},{1,0},{2,3},{3,2},{4,5},{5,4},{6,7},{7,6},{8,9},{9,8},{10,11... | collective-permute-start | bytes 393224 | tf_op jit(solution)/shard_map/ppermute | solution.py:49
  71.8 3.7 %collective-permute-done.26 = bf16[2,128,384]{2,1,0:T(8,128)(2,1)S(1)} collective-permute-done((bf16[2,128,384]{2,1,0:T(8,128)(2,1)S(1)}, bf16[2,128,384]{2,1,0:T(8,128)(2,1)S(1)}, u32[]{:S(2)}, u32[]{:S(2)}) %collective-permute-start.26) | collective-permute-done | bytes 196640 | tf_op jit(solution)/shard_map/ppermute | solution.py:49
  76.7 4.4 %collective-permute-done.32 = bf16[2,256,256]{2,1,0:T(8,128)(2,1)S(1)} collective-permute-done((bf16[2,256,256]{2,1,0:T(8,128)(2,1)S(1)}, bf16[2,256,256]{2,1,0:T(8,128)(2,1)S(1)}, u32[]{:S(2)}, u32[]{:S(2)}) %collective-permute-start.32) | collective-permute-done | bytes 262176 | tf_op jit(solution)/shard_map/ppermute | solution.py:49
  81.4 2.0 %collective-permute-start.33 = (bf16[2,512,256]{2,1,0:T(8,128)(2,1)S(1)}, bf16[2,512,256]{2,1,0:T(8,128)(2,1)S(1)}, u32[]{:S(2)}, u32[]{:S(2)}) collective-permute-start(bf16[2,512,256]{2,1,0:T(8,128)(2,1)S(1)} %maximum_select_fusion.5), channel_id=1, source_target_pairs={{0,8},{1,9},{2,10},{3,11},{4,12},{5,13},{6,14},{7,15},{8,0},{9,1},... | collective-permute-start | bytes 1572872 | tf_op jit(solution)/shard_map/ppermute | solution.py:49
  84.2 4.1 %collective-permute-start.23 = (bf16[2,512,384]{2,1,0:T(8,128)(2,1)S(1)}, bf16[2,512,384]{2,1,0:T(8,128)(2,1)S(1)}, u32[]{:S(2)}, u32[]{:S(2)}) collective-permute-start(bf16[2,512,384]{2,1,0:T(8,128)(2,1)S(1)} %maximum_select_fusion.3), channel_id=1, source_target_pairs={{0,8},{1,9},{2,10},{3,11},{4,12},{5,13},{6,14},{7,15},{8,0},{9,1},... | collective-permute-start | bytes 2359304 | tf_op jit(solution)/shard_map/ppermute | solution.py:49
  96.4 2.3 %collective-permute-start.34 = (bf16[2,1,16,256]{3,2,1,0:T(8,128)(2,1)S(1)}, bf16[2,1,16,256]{3,2,1,0:T(8,128)(2,1)S(1)}, u32[]{:S(2)}, u32[]{:S(2)}) collective-permute-start(bf16[2,1,16,256]{3,2,1,0:T(8,128)(2,1)S(1)} %get-tuple-element.59), channel_id=1, source_target_pairs={{0,1},{1,2},{2,3},{3,4},{4,5},{5,6},{6,7},{8,9},{9,10},{10,11},{11... | collective-permute-start | bytes 49160 | tf_op jit(solution)/shard_map/ppermute | solution.py:15
  98.7 3.9 %collective-permute-start.35 = (bf16[2,1,16,256]{3,2,1,0:T(8,128)(2,1)S(1)}, bf16[2,1,16,256]{3,2,1,0:T(8,128)(2,1)S(1)}, u32[]{:S(2)}, u32[]{:S(2)}) collective-permute-start(bf16[2,1,16,256]{3,2,1,0:T(8,128)(2,1)S(1)} %get-tuple-element.60), channel_id=1, source_target_pairs={{1,0},{2,1},{3,2},{4,3},{5,4},{6,5},{7,6},{9,8},{10,9},{11,10},{12... | collective-permute-start | bytes 49160 | tf_op jit(solution)/shard_map/ppermute | solution.py:18
  102.6 2.7 %collective-permute-start.36 = (bf16[1,4,16,256]{3,2,1,0:T(8,128)(2,1)S(1)}, bf16[1,4,16,256]{3,2,1,0:T(8,128)(2,1)S(1)}, u32[]{:S(2)}, u32[]{:S(2)}) collective-permute-start(bf16[1,4,16,256]{3,2,1,0:T(8,128)(2,1)S(1)} %get-tuple-element.63), channel_id=1, source_target_pairs={{0,8},{8,16},{16,24},{1,9},{9,17},{17,25},{2,10},{10,18},{18,26},{... | collective-permute-start | bytes 98312 | tf_op jit(solution)/shard_map/ppermute | solution.py:15
  105.3 1.9 %collective-permute-start.37 = (bf16[1,4,16,256]{3,2,1,0:T(8,128)(2,1)S(1)}, bf16[1,4,16,256]{3,2,1,0:T(8,128)(2,1)S(1)}, u32[]{:S(2)}, u32[]{:S(2)}) collective-permute-start(bf16[1,4,16,256]{3,2,1,0:T(8,128)(2,1)S(1)} %get-tuple-element.64), channel_id=1, source_target_pairs={{8,0},{16,8},{24,16},{9,1},{17,9},{25,17},{10,2},{18,10},{26,18},{... | collective-permute-start | bytes 98312 | tf_op jit(solution)/shard_map/ppermute | solution.py:18
  107.3 3.3 %collective-permute-done.37 = bf16[1,4,16,256]{3,2,1,0:T(8,128)(2,1)S(1)} collective-permute-done((bf16[1,4,16,256]{3,2,1,0:T(8,128)(2,1)S(1)}, bf16[1,4,16,256]{3,2,1,0:T(8,128)(2,1)S(1)}, u32[]{:S(2)}, u32[]{:S(2)}) %collective-permute-start.37) | collective-permute-done | bytes 32800 | tf_op jit(solution)/shard_map/ppermute | solution.py:18
  (166 shorter events, 37.2 us)
Async XLA Ops:
  6.7 7.8 %collective-permute-start.5 = (bf16[2,256,256]{2,1,0:T(8,128)(2,1)S(1)}, bf16[2,256,256]{2,1,0:T(8,128)(2,1)S(1)}, u32[]{:S(2)}, u32[]{:S(2)}) collective-permute-start(bf16[2,256,256]{2,1,0:T(8,128)(2,1)S(1)} %broadcast_select_fusion.9), channel_id=1, source_target_pairs={{0,16},{1,17},{2,18},{3,19},{4,20},{5,21},{6,22},{7,23},{8,24},{9,... | collective-permute-start | bytes 786440 | tf_op jit(solution)/shard_map/ppermute | solution.py:49
  8.0 10.3 %collective-permute-start.4 = (bf16[2,256,384]{2,1,0:T(8,128)(2,1)S(1)}, bf16[2,256,384]{2,1,0:T(8,128)(2,1)S(1)}, u32[]{:S(2)}, u32[]{:S(2)}) collective-permute-start(bf16[2,256,384]{2,1,0:T(8,128)(2,1)S(1)} %broadcast_select_fusion.3), channel_id=1, source_target_pairs={{0,2},{1,3},{2,0},{3,1},{4,6},{5,7},{6,4},{7,5},{8,10},{9,11},{10,... | collective-permute-start | bytes 1179656 | tf_op jit(solution)/shard_map/ppermute | solution.py:49
  8.3 10.0 %collective-permute-start.3 = (bf16[2,256,384]{2,1,0:T(8,128)(2,1)S(1)}, bf16[2,256,384]{2,1,0:T(8,128)(2,1)S(1)}, u32[]{:S(2)}, u32[]{:S(2)}) collective-permute-start(bf16[2,256,384]{2,1,0:T(8,128)(2,1)S(1)} %broadcast_select_fusion.8), channel_id=1, source_target_pairs={{0,1},{1,0},{2,3},{3,2},{4,5},{5,4},{6,7},{7,6},{8,9},{9,8},{10,11... | collective-permute-start | bytes 1179656 | tf_op jit(solution)/shard_map/ppermute | solution.py:49
  19.9 4.9 %collective-permute-start.7 = (bf16[2,128,384]{2,1,0:T(8,128)(2,1)S(1)}, bf16[2,128,384]{2,1,0:T(8,128)(2,1)S(1)}, u32[]{:S(2)}, u32[]{:S(2)}) collective-permute-start(bf16[2,128,384]{2,1,0:T(8,128)(2,1)S(1)} %broadcast_select_fusion.12), channel_id=1, source_target_pairs={{0,16},{1,17},{2,18},{3,19},{4,20},{5,21},{6,22},{7,23},{8,24},{9,... | collective-permute-start | bytes 589832 | tf_op jit(solution)/shard_map/ppermute | solution.py:49
  20.2 4.9 %collective-permute-start.6 = (bf16[2,128,384]{2,1,0:T(8,128)(2,1)S(1)}, bf16[2,128,384]{2,1,0:T(8,128)(2,1)S(1)}, u32[]{:S(2)}, u32[]{:S(2)}) collective-permute-start(bf16[2,128,384]{2,1,0:T(8,128)(2,1)S(1)} %broadcast_select_fusion.13), channel_id=1, source_target_pairs={{0,2},{1,3},{2,0},{3,1},{4,6},{5,7},{6,4},{7,5},{8,10},{9,11},{10,... | collective-permute-start | bytes 589832 | tf_op jit(solution)/shard_map/ppermute | solution.py:49
  37.5 10.0 %collective-permute-start.29 = (bf16[2,32,256]{2,1,0:T(8,128)(2,1)S(1)}, bf16[2,32,256]{2,1,0:T(8,128)(2,1)S(1)}, u32[]{:S(2)}, u32[]{:S(2)}) collective-permute-start(bf16[2,32,256]{2,1,0:T(8,128)(2,1)S(1)} %select_select_fusion.11), channel_id=1, source_target_pairs={{0,4},{1,5},{2,6},{3,7},{4,0},{5,1},{6,2},{7,3},{8,12},{9,13},{10,... | collective-permute-start | bytes 98312 | tf_op jit(solution)/shard_map/ppermute | solution.py:49
  39.8 18.6 %collective-permute-start.19 = (bf16[2,32,384]{2,1,0:T(8,128)(2,1)S(1)}, bf16[2,32,384]{2,1,0:T(8,128)(2,1)S(1)}, u32[]{:S(2)}, u32[]{:S(2)}) collective-permute-start(bf16[2,32,384]{2,1,0:T(8,128)(2,1)S(1)} %get-tuple-element.40), channel_id=1, source_target_pairs={{0,4},{1,5},{2,6},{3,7},{4,0},{5,1},{6,2},{7,3},{8,12},{9,13},{10,... | collective-permute-start | bytes 147464 | tf_op jit(solution)/shard_map/ppermute | solution.py:49
  40.0 21.5 %collective-permute-start.24 = (bf16[2,32,384]{2,1,0:T(8,128)(2,1)S(1)}, bf16[2,32,384]{2,1,0:T(8,128)(2,1)S(1)}, u32[]{:S(2)}, u32[]{:S(2)}) collective-permute-start(bf16[2,32,384]{2,1,0:T(8,128)(2,1)S(1)} %get-tuple-element.41), channel_id=1, source_target_pairs={{0,4},{1,5},{2,6},{3,7},{4,0},{5,1},{6,2},{7,3},{8,12},{9,13},{10,... | collective-permute-start | bytes 147464 | tf_op jit(solution)/shard_map/ppermute | solution.py:49
  42.2 21.6 %collective-permute-start.16 = (bf16[2,16,1152]{2,1,0:T(8,128)(2,1)S(1)}, bf16[2,16,1152]{2,1,0:T(8,128)(2,1)S(1)}, u32[]{:S(2)}, u32[]{:S(2)}) collective-permute-start(bf16[2,16,1152]{2,1,0:T(8,128)(2,1)S(1)} %get-tuple-element.57), channel_id=1, source_target_pairs={{1,0},{2,1},{3,2},{4,3},{5,4},{6,5},{7,6},{9,8},{10,9},{11,10},{12... | collective-permute-start | bytes 221192 | tf_op jit(solution)/shard_map/ppermute | solution.py:139
  44.8 16.8 %collective-permute-start.15 = (bf16[2,16,1152]{2,1,0:T(8,128)(2,1)S(1)}, bf16[2,16,1152]{2,1,0:T(8,128)(2,1)S(1)}, u32[]{:S(2)}, u32[]{:S(2)}) collective-permute-start(bf16[2,16,1152]{2,1,0:T(8,128)(2,1)S(1)} %get-tuple-element.58), channel_id=1, source_target_pairs={{0,1},{1,2},{2,3},{3,4},{4,5},{5,6},{6,7},{8,9},{9,10},{10,11},{11... | collective-permute-start | bytes 221192 | tf_op jit(solution)/shard_map/ppermute | solution.py:139
  47.5 24.2 %collective-permute-start.18 = (bf16[4,16,1152]{2,1,0:T(8,128)(2,1)S(1)}, bf16[4,16,1152]{2,1,0:T(8,128)(2,1)S(1)}, u32[]{:S(2)}, u32[]{:S(2)}) collective-permute-start(bf16[4,16,1152]{2,1,0:T(8,128)(2,1)S(1)} %get-tuple-element.55), channel_id=1, source_target_pairs={{8,0},{16,8},{24,16},{9,1},{17,9},{25,17},{10,2},{18,10},{26,18},{... | collective-permute-start | bytes 442376 | tf_op jit(solution)/shard_map/ppermute | solution.py:139
  58.5 9.3 %collective-permute-start.17 = (bf16[4,16,1152]{2,1,0:T(8,128)(2,1)S(1)}, bf16[4,16,1152]{2,1,0:T(8,128)(2,1)S(1)}, u32[]{:S(2)}, u32[]{:S(2)}) collective-permute-start(bf16[4,16,1152]{2,1,0:T(8,128)(2,1)S(1)} %get-tuple-element.56), channel_id=1, source_target_pairs={{0,8},{8,16},{16,24},{1,9},{9,17},{17,25},{2,10},{10,18},{18,26},{... | collective-permute-start | bytes 442376 | tf_op jit(solution)/shard_map/ppermute | solution.py:139
  61.7 8.3 %collective-permute-start.25 = (bf16[2,64,384]{2,1,0:T(8,128)(2,1)S(1)}, bf16[2,64,384]{2,1,0:T(8,128)(2,1)S(1)}, u32[]{:S(2)}, u32[]{:S(2)}) collective-permute-start(bf16[2,64,384]{2,1,0:T(8,128)(2,1)S(1)} %maximum_select_fusion.13), channel_id=1, source_target_pairs={{0,1},{1,0},{2,3},{3,2},{4,5},{5,4},{6,7},{7,6},{8,9},{9,8},{10,11... | collective-permute-start | bytes 294920 | tf_op jit(solution)/shard_map/ppermute | solution.py:49
  65.6 5.9 %collective-permute-start.31 = (bf16[2,128,256]{2,1,0:T(8,128)(2,1)S(1)}, bf16[2,128,256]{2,1,0:T(8,128)(2,1)S(1)}, u32[]{:S(2)}, u32[]{:S(2)}) collective-permute-start(bf16[2,128,256]{2,1,0:T(8,128)(2,1)S(1)} %maximum_select_fusion.11), channel_id=1, source_target_pairs={{0,1},{1,0},{2,3},{3,2},{4,5},{5,4},{6,7},{7,6},{8,9},{9,8},{10,11... | collective-permute-start | bytes 393224 | tf_op jit(solution)/shard_map/ppermute | solution.py:49
  68.7 7.5 %collective-permute-start.21 = (bf16[2,128,384]{2,1,0:T(8,128)(2,1)S(1)}, bf16[2,128,384]{2,1,0:T(8,128)(2,1)S(1)}, u32[]{:S(2)}, u32[]{:S(2)}) collective-permute-start(bf16[2,128,384]{2,1,0:T(8,128)(2,1)S(1)} %maximum_select_fusion.9), channel_id=1, source_target_pairs={{0,2},{1,3},{2,0},{3,1},{4,6},{5,7},{6,4},{7,5},{8,10},{9,11},{10,... | collective-permute-start | bytes 589832 | tf_op jit(solution)/shard_map/ppermute | solution.py:49
  70.0 5.5 %collective-permute-start.26 = (bf16[2,128,384]{2,1,0:T(8,128)(2,1)S(1)}, bf16[2,128,384]{2,1,0:T(8,128)(2,1)S(1)}, u32[]{:S(2)}, u32[]{:S(2)}) collective-permute-start(bf16[2,128,384]{2,1,0:T(8,128)(2,1)S(1)} %maximum_select_fusion.10), channel_id=1, source_target_pairs={{0,16},{1,17},{2,18},{3,19},{4,20},{5,21},{6,22},{7,23},{8,24},{9,... | collective-permute-start | bytes 589832 | tf_op jit(solution)/shard_map/ppermute | solution.py:49
  71.6 9.5 %collective-permute-start.32 = (bf16[2,256,256]{2,1,0:T(8,128)(2,1)S(1)}, bf16[2,256,256]{2,1,0:T(8,128)(2,1)S(1)}, u32[]{:S(2)}, u32[]{:S(2)}) collective-permute-start(bf16[2,256,256]{2,1,0:T(8,128)(2,1)S(1)} %maximum_select_fusion.8), channel_id=1, source_target_pairs={{0,16},{1,17},{2,18},{3,19},{4,20},{5,21},{6,22},{7,23},{8,24},{9,... | collective-permute-start | bytes 786440 | tf_op jit(solution)/shard_map/ppermute | solution.py:49
  75.7 12.6 %collective-permute-start.27 = (bf16[2,256,384]{2,1,0:T(8,128)(2,1)S(1)}, bf16[2,256,384]{2,1,0:T(8,128)(2,1)S(1)}, u32[]{:S(2)}, u32[]{:S(2)}) collective-permute-start(bf16[2,256,384]{2,1,0:T(8,128)(2,1)S(1)} %maximum_select_fusion.7), channel_id=1, source_target_pairs={{0,2},{1,3},{2,0},{3,1},{4,6},{5,7},{6,4},{7,5},{8,10},{9,11},{10,... | collective-permute-start | bytes 1179656 | tf_op jit(solution)/shard_map/ppermute | solution.py:49
  76.3 7.5 %collective-permute-start.22 = (bf16[2,256,384]{2,1,0:T(8,128)(2,1)S(1)}, bf16[2,256,384]{2,1,0:T(8,128)(2,1)S(1)}, u32[]{:S(2)}, u32[]{:S(2)}) collective-permute-start(bf16[2,256,384]{2,1,0:T(8,128)(2,1)S(1)} %maximum_select_fusion.6), channel_id=1, source_target_pairs={{0,1},{1,0},{2,3},{3,2},{4,5},{5,4},{6,7},{7,6},{8,9},{9,8},{10,11... | collective-permute-start | bytes 1179656 | tf_op jit(solution)/shard_map/ppermute | solution.py:49
  81.4 7.3 %collective-permute-start.33 = (bf16[2,512,256]{2,1,0:T(8,128)(2,1)S(1)}, bf16[2,512,256]{2,1,0:T(8,128)(2,1)S(1)}, u32[]{:S(2)}, u32[]{:S(2)}) collective-permute-start(bf16[2,512,256]{2,1,0:T(8,128)(2,1)S(1)} %maximum_select_fusion.5), channel_id=1, source_target_pairs={{0,8},{1,9},{2,10},{3,11},{4,12},{5,13},{6,14},{7,15},{8,0},{9,1},... | collective-permute-start | bytes 1572872 | tf_op jit(solution)/shard_map/ppermute | solution.py:49
  84.2 6.0 %collective-permute-start.23 = (bf16[2,512,384]{2,1,0:T(8,128)(2,1)S(1)}, bf16[2,512,384]{2,1,0:T(8,128)(2,1)S(1)}, u32[]{:S(2)}, u32[]{:S(2)}) collective-permute-start(bf16[2,512,384]{2,1,0:T(8,128)(2,1)S(1)} %maximum_select_fusion.3), channel_id=1, source_target_pairs={{0,8},{1,9},{2,10},{3,11},{4,12},{5,13},{6,14},{7,15},{8,0},{9,1},... | collective-permute-start | bytes 2359304 | tf_op jit(solution)/shard_map/ppermute | solution.py:49
  96.4 10.8 %collective-permute-start.34 = (bf16[2,1,16,256]{3,2,1,0:T(8,128)(2,1)S(1)}, bf16[2,1,16,256]{3,2,1,0:T(8,128)(2,1)S(1)}, u32[]{:S(2)}, u32[]{:S(2)}) collective-permute-start(bf16[2,1,16,256]{3,2,1,0:T(8,128)(2,1)S(1)} %get-tuple-element.59), channel_id=1, source_target_pairs={{0,1},{1,2},{2,3},{3,4},{4,5},{5,6},{6,7},{8,9},{9,10},{10,11},{11... | collective-permute-start | bytes 49160 | tf_op jit(solution)/shard_map/ppermute | solution.py:15
  98.7 8.6 %collective-permute-start.35 = (bf16[2,1,16,256]{3,2,1,0:T(8,128)(2,1)S(1)}, bf16[2,1,16,256]{3,2,1,0:T(8,128)(2,1)S(1)}, u32[]{:S(2)}, u32[]{:S(2)}) collective-permute-start(bf16[2,1,16,256]{3,2,1,0:T(8,128)(2,1)S(1)} %get-tuple-element.60), channel_id=1, source_target_pairs={{1,0},{2,1},{3,2},{4,3},{5,4},{6,5},{7,6},{9,8},{10,9},{11,10},{12... | collective-permute-start | bytes 49160 | tf_op jit(solution)/shard_map/ppermute | solution.py:18
  105.3 5.2 %collective-permute-start.37 = (bf16[1,4,16,256]{3,2,1,0:T(8,128)(2,1)S(1)}, bf16[1,4,16,256]{3,2,1,0:T(8,128)(2,1)S(1)}, u32[]{:S(2)}, u32[]{:S(2)}) collective-permute-start(bf16[1,4,16,256]{3,2,1,0:T(8,128)(2,1)S(1)} %get-tuple-element.64), channel_id=1, source_target_pairs={{8,0},{16,8},{24,16},{9,1},{17,9},{25,17},{10,2},{18,10},{26,18},{... | collective-permute-start | bytes 98312 | tf_op jit(solution)/shard_map/ppermute | solution.py:18
  (19 other events, 64.9 us)

commit v7 on v6

--- a/solution.py
+++ b/solution.py
@@ -83,6 +83,8 @@
             blocks[s] = jnp.where(
                 mine, jnp.concatenate([gots[s], blocks[s]], axis=1), jnp.concatenate([blocks[s], gots[s]], axis=1)
             )
+        if step == stages - 1:
+            blocks = list(lax.optimization_barrier(tuple(blocks)))
     return blocks, tie
 
 
@@ -98,7 +100,7 @@
     core = col_bits
     middle = list(range(col_bits - 1)) + list(range(col_bits + 1, col_bits + row_bits))
     last = [col_bits - 1]
-    streams = max(1, min(3, len(middle)))
+    streams = max(1, min(2, len(middle)))
     width = own_operator.shape[1]
     unit = width // 128
     sizes = [unit // streams + (1 if s < unit % streams else 0) for s in range(streams)]

time: 114 us -> 111 us (0.974)
  waiting for transfers between devices: 32.8 us -> 47.6 us
  starting transfers between devices: 62.5 us -> 48.2 us
  other arithmetic: 9.96 us -> 8.02 us
  matrix products: 5.98 us -> 4.44 us
    ppermute x30 -> x20, waiting for transfers between devices: 29.5 us -> 44.5 us  [swap(): return lax.ppermute(block, ('row', 'col'), pairs)]
    ppermute x30 -> x20, starting transfers between devices: 32.5 us -> 19.8 us  [swap(): return lax.ppermute(block, ('row', 'col'), pairs)]
    select_n x2 -> x1, other arithmetic: 3.29 us -> 1.68 us  [scatter_gather(): keep = jnp.where(mine, block[half:], block[:half])[None]]
    dot_general x18 -> x12, matrix products: 5.98 us -> 4.44 us  [sweep(): jnp.dot(rows, part[k], preferred_element_type=jnp.float32)]
    ppermute x4, starting transfers between devices: 19.2 us -> 17.9 us  [shift(): return lax.ppermute(block, axis, pairs)]
    select_n x15 -> x10, other arithmetic: 2.55 us -> 2.84 us  [scatter_gather(): jnp.where(mine, jnp.concatenate([gots[s], blocks[s]], axis=1), jnp.concat...]
  transfers between devices with their start and end apart: 38 -> 28, of which waited for: 19 -> 17; matrix products, arithmetic and copies ran while one was open for 6% -> 4% of each run, Pallas kernels for 0% -> 0%
where the time goes in v7:
time: 111 us; the launch traced here: 110 us
  starting transfers between devices  48.2 us (43%)
  waiting for transfers between devices  47.6 us (43%)
  other arithmetic  8.02 us (7%)
  matrix products  4.44 us (4%)
  local copies, waits for them, and re-layouts  1.14 us (1%)
    ppermute x20, waiting for transfers between devices, swap(): return lax.ppermute(block, ('row', 'col'), pairs)  44.5 us
    ppermute x20, starting transfers between devices, swap(): return lax.ppermute(block, ('row', 'col'), pairs)  19.8 us
    ppermute x4, starting transfers between devices, shift(): return lax.ppermute(block, axis, pairs)  17.9 us
    ppermute x2, starting transfers between devices, with_halo(): lax.ppermute(lax.slice_in_dim(block, 0, width, axis=dim), axis, backward)  5.42 us
    ppermute x2, starting transfers between devices, with_halo(): lax.ppermute(lax.slice_in_dim(block, block.shape[dim] - width, None, axis...  5.09 us
    dot_general x12, matrix products, sweep(): jnp.dot(rows, part[k], preferred_element_type=jnp.float32)  4.44 us
    ppermute x2, waiting for transfers between devices, with_halo(): lax.ppermute(lax.slice_in_dim(block, 0, width, axis=dim), axis, backward)  3.07 us
    select_n x10, other arithmetic, scatter_gather(): jnp.where(mine, jnp.concatenate([gots[s], blocks[s]], axis=1), jnp.concat...  2.84 us
  transfers between devices with their start and end apart: 28, of which 17 were waited for; matrix products, arithmetic and copies ran while one was open for 4% of the time, Pallas kernels for 0%

profile of v7, /device:TPU:9, one launch (start us, length us, event | category | flops | bytes accessed | tf_op | source)
XLA Modules:
  0.0 110.0 jit_solution(10651773206724763081)
XLA Ops:
  0.0 1.7 %broadcast_select_fusion.4 = (bf16[512,512]{1,0:T(8,128)(2,1)S(1)}, bf16[512,512]{1,0:T(8,128)(2,1)S(1)}, bf16[512,512]{1,0:T(8,128)(2,1)S(1)}, bf16[512,512]{1,0:T(8,128)(2,1)S(1)}) fusion(pred[]{:T(512)S(6)} %eq.120, bf16[1024,1024]{1,0:T(8,128)(2,1)} %bitcast.68), kind=kLoop, calls=%fused_computation.40 | loop fusion | flops 1048576 | bytes 4194305 | tf_op jit(solution)/shard_map/jit(_where)/select_n | solution.py:63
  2.6 1.4 %collective-permute-done = bf16[512,512]{1,0:T(8,128)(2,1)S(1)} collective-permute-done((bf16[512,512]{1,0:T(8,128)(2,1)S(1)}, bf16[512,512]{1,0:T(8,128)(2,1)S(1)}, u32[]{:S(2)}, u32[]{:S(2)}) %collective-permute-start) | collective-permute-done | bytes 524320 | tf_op jit(solution)/shard_map/ppermute | solution.py:49
  5.2 1.4 %collective-permute-start.2 = (bf16[2,256,512]{2,1,0:T(8,128)(2,1)S(1)}, bf16[2,256,512]{2,1,0:T(8,128)(2,1)S(1)}, u32[]{:S(2)}, u32[]{:S(2)}) collective-permute-start(bf16[2,256,512]{2,1,0:T(8,128)(2,1)S(1)} %broadcast_select_fusion.7), channel_id=1, source_target_pairs={{0,1},{1,0},{2,3},{3,2},{4,5},{5,4},{6,7},{7,6},{8,9},{9,8},{10,11... | collective-permute-start | bytes 1572872 | tf_op jit(solution)/shard_map/ppermute | solution.py:49
  6.8 11.4 %collective-permute-done.3 = bf16[2,256,512]{2,1,0:T(8,128)(2,1)S(1)} collective-permute-done((bf16[2,256,512]{2,1,0:T(8,128)(2,1)S(1)}, bf16[2,256,512]{2,1,0:T(8,128)(2,1)S(1)}, u32[]{:S(2)}, u32[]{:S(2)}) %collective-permute-start.3) | collective-permute-done | bytes 524320 | tf_op jit(solution)/shard_map/ppermute | solution.py:49
  21.4 4.0 %collective-permute-done.5 = bf16[2,128,512]{2,1,0:T(8,128)(2,1)S(1)} collective-permute-done((bf16[2,128,512]{2,1,0:T(8,128)(2,1)S(1)}, bf16[2,128,512]{2,1,0:T(8,128)(2,1)S(1)}, u32[]{:S(2)}, u32[]{:S(2)}) %collective-permute-start.5) | collective-permute-done | bytes 262176 | tf_op jit(solution)/shard_map/ppermute | solution.py:49
  27.8 2.2 %collective-permute-done.7 = bf16[2,64,512]{2,1,0:T(8,128)(2,1)S(1)} collective-permute-done((bf16[2,64,512]{2,1,0:T(8,128)(2,1)S(1)}, bf16[2,64,512]{2,1,0:T(8,128)(2,1)S(1)}, u32[]{:S(2)}, u32[]{:S(2)}) %collective-permute-start.7) | collective-permute-done | bytes 131104 | tf_op jit(solution)/shard_map/ppermute | solution.py:49
  31.4 2.4 %collective-permute-start.9 = (bf16[2,32,512]{2,1,0:T(8,128)(2,1)S(1)}, bf16[2,32,512]{2,1,0:T(8,128)(2,1)S(1)}, u32[]{:S(2)}, u32[]{:S(2)}) collective-permute-start(bf16[2,32,512]{2,1,0:T(8,128)(2,1)S(1)} %broadcast_select_fusion.12), channel_id=1, source_target_pairs={{0,4},{1,5},{2,6},{3,7},{4,0},{5,1},{6,2},{7,3},{8,12},{9,13},{10,... | collective-permute-start | bytes 196616 | tf_op jit(solution)/shard_map/ppermute | solution.py:49
  33.9 1.6 %collective-permute-done.9 = bf16[2,32,512]{2,1,0:T(8,128)(2,1)S(1)} collective-permute-done((bf16[2,32,512]{2,1,0:T(8,128)(2,1)S(1)}, bf16[2,32,512]{2,1,0:T(8,128)(2,1)S(1)}, u32[]{:S(2)}, u32[]{:S(2)}) %collective-permute-start.9) | collective-permute-done | bytes 65568 | tf_op jit(solution)/shard_map/ppermute | solution.py:49
  35.6 2.3 %collective-permute-done.8 = bf16[2,32,512]{2,1,0:T(8,128)(2,1)S(1)} collective-permute-done((bf16[2,32,512]{2,1,0:T(8,128)(2,1)S(1)}, bf16[2,32,512]{2,1,0:T(8,128)(2,1)S(1)}, u32[]{:S(2)}, u32[]{:S(2)}) %collective-permute-start.8) | collective-permute-done | bytes 65568 | tf_op jit(solution)/shard_map/ppermute | solution.py:49
  38.0 2.1 %collective-permute-start.14 = (bf16[2,32,512]{2,1,0:T(8,128)(2,1)S(1)}, bf16[2,32,512]{2,1,0:T(8,128)(2,1)S(1)}, u32[]{:S(2)}, u32[]{:S(2)}) collective-permute-start(bf16[2,32,512]{2,1,0:T(8,128)(2,1)S(1)} %get-tuple-element.31), channel_id=1, source_target_pairs={{0,4},{1,5},{2,6},{3,7},{4,0},{5,1},{6,2},{7,3},{8,12},{9,13},{10,... | collective-permute-start | bytes 196616 | tf_op jit(solution)/shard_map/ppermute | solution.py:49
  40.5 3.2 %collective-permute-done.14 = bf16[2,32,512]{2,1,0:T(8,128)(2,1)S(1)} collective-permute-done((bf16[2,32,512]{2,1,0:T(8,128)(2,1)S(1)}, bf16[2,32,512]{2,1,0:T(8,128)(2,1)S(1)}, u32[]{:S(2)}, u32[]{:S(2)}) %collective-permute-start.14) | collective-permute-done | bytes 65568 | tf_op jit(solution)/shard_map/ppermute | solution.py:49
  45.1 3.4 %collective-permute-done.20 = bf16[2,64,512]{2,1,0:T(8,128)(2,1)S(1)} collective-permute-done((bf16[2,64,512]{2,1,0:T(8,128)(2,1)S(1)}, bf16[2,64,512]{2,1,0:T(8,128)(2,1)S(1)}, u32[]{:S(2)}, u32[]{:S(2)}) %collective-permute-start.20) | collective-permute-done | bytes 131104 | tf_op jit(solution)/shard_map/ppermute | solution.py:49
  48.9 2.2 %collective-permute-start.10 = (bf16[2,16,1152]{2,1,0:T(8,128)(2,1)S(1)}, bf16[2,16,1152]{2,1,0:T(8,128)(2,1)S(1)}, u32[]{:S(2)}, u32[]{:S(2)}) collective-permute-start(bf16[2,16,1152]{2,1,0:T(8,128)(2,1)S(1)} %get-tuple-element.48), channel_id=1, source_target_pairs={{0,1},{1,2},{2,3},{3,4},{4,5},{5,6},{6,7},{8,9},{9,10},{10,11},{11... | collective-permute-start | bytes 221192 | tf_op jit(solution)/shard_map/ppermute | solution.py:141
  51.1 2.6 %collective-permute-start.17 = (bf16[2,128,512]{2,1,0:T(8,128)(2,1)S(1)}, bf16[2,128,512]{2,1,0:T(8,128)(2,1)S(1)}, u32[]{:S(2)}, u32[]{:S(2)}) collective-permute-start(bf16[2,128,512]{2,1,0:T(8,128)(2,1)S(1)} %maximum_select_fusion.6), channel_id=1, source_target_pairs={{0,2},{1,3},{2,0},{3,1},{4,6},{5,7},{6,4},{7,5},{8,10},{9,11},{10,... | collective-permute-start | bytes 786440 | tf_op jit(solution)/shard_map/ppermute | solution.py:49
  54.0 2.6 %collective-permute-start.22 = (bf16[2,256,512]{2,1,0:T(8,128)(2,1)S(1)}, bf16[2,256,512]{2,1,0:T(8,128)(2,1)S(1)}, u32[]{:S(2)}, u32[]{:S(2)}) collective-permute-start(bf16[2,256,512]{2,1,0:T(8,128)(2,1)S(1)} %maximum_select_fusion.5), channel_id=1, source_target_pairs={{0,2},{1,3},{2,0},{3,1},{4,6},{5,7},{6,4},{7,5},{8,10},{9,11},{10,... | collective-permute-start | bytes 1572872 | tf_op jit(solution)/shard_map/ppermute | solution.py:49
  56.6 1.9 %collective-permute-start.11 = (bf16[2,16,1152]{2,1,0:T(8,128)(2,1)S(1)}, bf16[2,16,1152]{2,1,0:T(8,128)(2,1)S(1)}, u32[]{:S(2)}, u32[]{:S(2)}) collective-permute-start(bf16[2,16,1152]{2,1,0:T(8,128)(2,1)S(1)} %get-tuple-element.47), channel_id=1, source_target_pairs={{1,0},{2,1},{3,2},{4,3},{5,4},{6,5},{7,6},{9,8},{10,9},{11,10},{12... | collective-permute-start | bytes 221192 | tf_op jit(solution)/shard_map/ppermute | solution.py:141
  58.5 11.2 %collective-permute-start.13 = (bf16[4,16,1152]{2,1,0:T(8,128)(2,1)S(1)}, bf16[4,16,1152]{2,1,0:T(8,128)(2,1)S(1)}, u32[]{:S(2)}, u32[]{:S(2)}) collective-permute-start(bf16[4,16,1152]{2,1,0:T(8,128)(2,1)S(1)} %get-tuple-element.45), channel_id=1, source_target_pairs={{8,0},{16,8},{24,16},{9,1},{17,9},{25,17},{10,2},{18,10},{26,18},{... | collective-permute-start | bytes 442376 | tf_op jit(solution)/shard_map/ppermute | solution.py:141
  69.7 2.6 %collective-permute-start.12 = (bf16[4,16,1152]{2,1,0:T(8,128)(2,1)S(1)}, bf16[4,16,1152]{2,1,0:T(8,128)(2,1)S(1)}, u32[]{:S(2)}, u32[]{:S(2)}) collective-permute-start(bf16[4,16,1152]{2,1,0:T(8,128)(2,1)S(1)} %get-tuple-element.46), channel_id=1, source_target_pairs={{0,8},{8,16},{16,24},{1,9},{9,17},{17,25},{2,10},{10,18},{18,26},{... | collective-permute-start | bytes 442376 | tf_op jit(solution)/shard_map/ppermute | solution.py:141
  74.8 11.5 %collective-permute-done.18 = bf16[2,256,512]{2,1,0:T(8,128)(2,1)S(1)} collective-permute-done((bf16[2,256,512]{2,1,0:T(8,128)(2,1)S(1)}, bf16[2,256,512]{2,1,0:T(8,128)(2,1)S(1)}, u32[]{:S(2)}, u32[]{:S(2)}) %collective-permute-start.18) | collective-permute-done | bytes 524320 | tf_op jit(solution)/shard_map/ppermute | solution.py:49
  94.2 2.9 %collective-permute-start.24 = (bf16[2,1,16,256]{3,2,1,0:T(8,128)(2,1)S(1)}, bf16[2,1,16,256]{3,2,1,0:T(8,128)(2,1)S(1)}, u32[]{:S(2)}, u32[]{:S(2)}) collective-permute-start(bf16[2,1,16,256]{3,2,1,0:T(8,128)(2,1)S(1)} %get-tuple-element.49), channel_id=1, source_target_pairs={{0,1},{1,2},{2,3},{3,4},{4,5},{5,6},{6,7},{8,9},{9,10},{10,11},{11... | collective-permute-start | bytes 49160 | tf_op jit(solution)/shard_map/ppermute | solution.py:15
  97.0 3.3 %collective-permute-start.25 = (bf16[2,1,16,256]{3,2,1,0:T(8,128)(2,1)S(1)}, bf16[2,1,16,256]{3,2,1,0:T(8,128)(2,1)S(1)}, u32[]{:S(2)}, u32[]{:S(2)}) collective-permute-start(bf16[2,1,16,256]{3,2,1,0:T(8,128)(2,1)S(1)} %get-tuple-element.50), channel_id=1, source_target_pairs={{1,0},{2,1},{3,2},{4,3},{5,4},{6,5},{7,6},{9,8},{10,9},{11,10},{12... | collective-permute-start | bytes 49160 | tf_op jit(solution)/shard_map/ppermute | solution.py:18
  100.4 2.2 %collective-permute-start.26 = (bf16[1,4,16,256]{3,2,1,0:T(8,128)(2,1)S(1)}, bf16[1,4,16,256]{3,2,1,0:T(8,128)(2,1)S(1)}, u32[]{:S(2)}, u32[]{:S(2)}) collective-permute-start(bf16[1,4,16,256]{3,2,1,0:T(8,128)(2,1)S(1)} %get-tuple-element.53), channel_id=1, source_target_pairs={{0,8},{8,16},{16,24},{1,9},{9,17},{17,25},{2,10},{10,18},{18,26},{... | collective-permute-start | bytes 98312 | tf_op jit(solution)/shard_map/ppermute | solution.py:15
  102.6 2.1 %collective-permute-start.27 = (bf16[1,4,16,256]{3,2,1,0:T(8,128)(2,1)S(1)}, bf16[1,4,16,256]{3,2,1,0:T(8,128)(2,1)S(1)}, u32[]{:S(2)}, u32[]{:S(2)}) collective-permute-start(bf16[1,4,16,256]{3,2,1,0:T(8,128)(2,1)S(1)} %get-tuple-element.54), channel_id=1, source_target_pairs={{8,0},{16,8},{24,16},{9,1},{17,9},{25,17},{10,2},{18,10},{26,18},{... | collective-permute-start | bytes 98312 | tf_op jit(solution)/shard_map/ppermute | solution.py:18
  104.7 3.1 %collective-permute-done.27 = bf16[1,4,16,256]{3,2,1,0:T(8,128)(2,1)S(1)} collective-permute-done((bf16[1,4,16,256]{3,2,1,0:T(8,128)(2,1)S(1)}, bf16[1,4,16,256]{3,2,1,0:T(8,128)(2,1)S(1)}, u32[]{:S(2)}, u32[]{:S(2)}) %collective-permute-start.27) | collective-permute-done | bytes 32800 | tf_op jit(solution)/shard_map/ppermute | solution.py:18
  (125 shorter events, 24.2 us)
Async XLA Ops:
  5.1 13.2 %collective-permute-start.3 = (bf16[2,256,512]{2,1,0:T(8,128)(2,1)S(1)}, bf16[2,256,512]{2,1,0:T(8,128)(2,1)S(1)}, u32[]{:S(2)}, u32[]{:S(2)}) collective-permute-start(bf16[2,256,512]{2,1,0:T(8,128)(2,1)S(1)} %broadcast_select_fusion.2), channel_id=1, source_target_pairs={{0,2},{1,3},{2,0},{3,1},{4,6},{5,7},{6,4},{7,5},{8,10},{9,11},{10,... | collective-permute-start | bytes 1572872 | tf_op jit(solution)/shard_map/ppermute | solution.py:49
  5.2 13.2 %collective-permute-start.2 = (bf16[2,256,512]{2,1,0:T(8,128)(2,1)S(1)}, bf16[2,256,512]{2,1,0:T(8,128)(2,1)S(1)}, u32[]{:S(2)}, u32[]{:S(2)}) collective-permute-start(bf16[2,256,512]{2,1,0:T(8,128)(2,1)S(1)} %broadcast_select_fusion.7), channel_id=1, source_target_pairs={{0,1},{1,0},{2,3},{3,2},{4,5},{5,4},{6,7},{7,6},{8,9},{9,8},{10,11... | collective-permute-start | bytes 1572872 | tf_op jit(solution)/shard_map/ppermute | solution.py:49
  18.7 6.7 %collective-permute-start.5 = (bf16[2,128,512]{2,1,0:T(8,128)(2,1)S(1)}, bf16[2,128,512]{2,1,0:T(8,128)(2,1)S(1)}, u32[]{:S(2)}, u32[]{:S(2)}) collective-permute-start(bf16[2,128,512]{2,1,0:T(8,128)(2,1)S(1)} %broadcast_select_fusion.8), channel_id=1, source_target_pairs={{0,16},{1,17},{2,18},{3,19},{4,20},{5,21},{6,22},{7,23},{8,24},{9,... | collective-permute-start | bytes 786440 | tf_op jit(solution)/shard_map/ppermute | solution.py:49
  19.9 6.1 %collective-permute-start.4 = (bf16[2,128,512]{2,1,0:T(8,128)(2,1)S(1)}, bf16[2,128,512]{2,1,0:T(8,128)(2,1)S(1)}, u32[]{:S(2)}, u32[]{:S(2)}) collective-permute-start(bf16[2,128,512]{2,1,0:T(8,128)(2,1)S(1)} %broadcast_select_fusion.9), channel_id=1, source_target_pairs={{0,2},{1,3},{2,0},{3,1},{4,6},{5,7},{6,4},{7,5},{8,10},{9,11},{10,... | collective-permute-start | bytes 786440 | tf_op jit(solution)/shard_map/ppermute | solution.py:49
  26.1 3.9 %collective-permute-start.7 = (bf16[2,64,512]{2,1,0:T(8,128)(2,1)S(1)}, bf16[2,64,512]{2,1,0:T(8,128)(2,1)S(1)}, u32[]{:S(2)}, u32[]{:S(2)}) collective-permute-start(bf16[2,64,512]{2,1,0:T(8,128)(2,1)S(1)} %broadcast_select_fusion.10), channel_id=1, source_target_pairs={{0,1},{1,0},{2,3},{3,2},{4,5},{5,4},{6,7},{7,6},{8,9},{9,8},{10,11... | collective-permute-start | bytes 393224 | tf_op jit(solution)/shard_map/ppermute | solution.py:49
  31.4 4.2 %collective-permute-start.9 = (bf16[2,32,512]{2,1,0:T(8,128)(2,1)S(1)}, bf16[2,32,512]{2,1,0:T(8,128)(2,1)S(1)}, u32[]{:S(2)}, u32[]{:S(2)}) collective-permute-start(bf16[2,32,512]{2,1,0:T(8,128)(2,1)S(1)} %broadcast_select_fusion.12), channel_id=1, source_target_pairs={{0,4},{1,5},{2,6},{3,7},{4,0},{5,1},{6,2},{7,3},{8,12},{9,13},{10,... | collective-permute-start | bytes 196616 | tf_op jit(solution)/shard_map/ppermute | solution.py:49
  33.8 4.1 %collective-permute-start.8 = (bf16[2,32,512]{2,1,0:T(8,128)(2,1)S(1)}, bf16[2,32,512]{2,1,0:T(8,128)(2,1)S(1)}, u32[]{:S(2)}, u32[]{:S(2)}) collective-permute-start(bf16[2,32,512]{2,1,0:T(8,128)(2,1)S(1)} %broadcast_select_fusion.13), channel_id=1, source_target_pairs={{0,4},{1,5},{2,6},{3,7},{4,0},{5,1},{6,2},{7,3},{8,12},{9,13},{10,... | collective-permute-start | bytes 196616 | tf_op jit(solution)/shard_map/ppermute | solution.py:49
  38.0 5.8 %collective-permute-start.14 = (bf16[2,32,512]{2,1,0:T(8,128)(2,1)S(1)}, bf16[2,32,512]{2,1,0:T(8,128)(2,1)S(1)}, u32[]{:S(2)}, u32[]{:S(2)}) collective-permute-start(bf16[2,32,512]{2,1,0:T(8,128)(2,1)S(1)} %get-tuple-element.31), channel_id=1, source_target_pairs={{0,4},{1,5},{2,6},{3,7},{4,0},{5,1},{6,2},{7,3},{8,12},{9,13},{10,... | collective-permute-start | bytes 196616 | tf_op jit(solution)/shard_map/ppermute | solution.py:49
  40.2 4.3 %collective-permute-start.15 = (bf16[2,32,512]{2,1,0:T(8,128)(2,1)S(1)}, bf16[2,32,512]{2,1,0:T(8,128)(2,1)S(1)}, u32[]{:S(2)}, u32[]{:S(2)}) collective-permute-start(bf16[2,32,512]{2,1,0:T(8,128)(2,1)S(1)} %get-tuple-element.32), channel_id=1, source_target_pairs={{0,4},{1,5},{2,6},{3,7},{4,0},{5,1},{6,2},{7,3},{8,12},{9,13},{10,... | collective-permute-start | bytes 196616 | tf_op jit(solution)/shard_map/ppermute | solution.py:49
  44.5 3.9 %collective-permute-start.20 = (bf16[2,64,512]{2,1,0:T(8,128)(2,1)S(1)}, bf16[2,64,512]{2,1,0:T(8,128)(2,1)S(1)}, u32[]{:S(2)}, u32[]{:S(2)}) collective-permute-start(bf16[2,64,512]{2,1,0:T(8,128)(2,1)S(1)} %maximum_select_fusion.9), channel_id=1, source_target_pairs={{0,1},{1,0},{2,3},{3,2},{4,5},{5,4},{6,7},{7,6},{8,9},{9,8},{10,11... | collective-permute-start | bytes 393224 | tf_op jit(solution)/shard_map/ppermute | solution.py:49
  44.8 6.2 %collective-permute-start.16 = (bf16[2,64,512]{2,1,0:T(8,128)(2,1)S(1)}, bf16[2,64,512]{2,1,0:T(8,128)(2,1)S(1)}, u32[]{:S(2)}, u32[]{:S(2)}) collective-permute-start(bf16[2,64,512]{2,1,0:T(8,128)(2,1)S(1)} %maximum_select_fusion.8), channel_id=1, source_target_pairs={{0,16},{1,17},{2,18},{3,19},{4,20},{5,21},{6,22},{7,23},{8,24},{9,... | collective-permute-start | bytes 393224 | tf_op jit(solution)/shard_map/ppermute | solution.py:49
  48.5 5.3 %collective-permute-start.21 = (bf16[2,128,512]{2,1,0:T(8,128)(2,1)S(1)}, bf16[2,128,512]{2,1,0:T(8,128)(2,1)S(1)}, u32[]{:S(2)}, u32[]{:S(2)}) collective-permute-start(bf16[2,128,512]{2,1,0:T(8,128)(2,1)S(1)} %maximum_select_fusion.7), channel_id=1, source_target_pairs={{0,16},{1,17},{2,18},{3,19},{4,20},{5,21},{6,22},{7,23},{8,24},{9,... | collective-permute-start | bytes 786440 | tf_op jit(solution)/shard_map/ppermute | solution.py:49
  48.9 20.8 %collective-permute-start.10 = (bf16[2,16,1152]{2,1,0:T(8,128)(2,1)S(1)}, bf16[2,16,1152]{2,1,0:T(8,128)(2,1)S(1)}, u32[]{:S(2)}, u32[]{:S(2)}) collective-permute-start(bf16[2,16,1152]{2,1,0:T(8,128)(2,1)S(1)} %get-tuple-element.48), channel_id=1, source_target_pairs={{0,1},{1,2},{2,3},{3,4},{4,5},{5,6},{6,7},{8,9},{9,10},{10,11},{11... | collective-permute-start | bytes 221192 | tf_op jit(solution)/shard_map/ppermute | solution.py:141
  51.1 21.2 %collective-permute-start.17 = (bf16[2,128,512]{2,1,0:T(8,128)(2,1)S(1)}, bf16[2,128,512]{2,1,0:T(8,128)(2,1)S(1)}, u32[]{:S(2)}, u32[]{:S(2)}) collective-permute-start(bf16[2,128,512]{2,1,0:T(8,128)(2,1)S(1)} %maximum_select_fusion.6), channel_id=1, source_target_pairs={{0,2},{1,3},{2,0},{3,1},{4,6},{5,7},{6,4},{7,5},{8,10},{9,11},{10,... | collective-permute-start | bytes 786440 | tf_op jit(solution)/shard_map/ppermute | solution.py:49
  54.0 19.6 %collective-permute-start.22 = (bf16[2,256,512]{2,1,0:T(8,128)(2,1)S(1)}, bf16[2,256,512]{2,1,0:T(8,128)(2,1)S(1)}, u32[]{:S(2)}, u32[]{:S(2)}) collective-permute-start(bf16[2,256,512]{2,1,0:T(8,128)(2,1)S(1)} %maximum_select_fusion.5), channel_id=1, source_target_pairs={{0,2},{1,3},{2,0},{3,1},{4,6},{5,7},{6,4},{7,5},{8,10},{9,11},{10,... | collective-permute-start | bytes 1572872 | tf_op jit(solution)/shard_map/ppermute | solution.py:49
  56.6 18.1 %collective-permute-start.11 = (bf16[2,16,1152]{2,1,0:T(8,128)(2,1)S(1)}, bf16[2,16,1152]{2,1,0:T(8,128)(2,1)S(1)}, u32[]{:S(2)}, u32[]{:S(2)}) collective-permute-start(bf16[2,16,1152]{2,1,0:T(8,128)(2,1)S(1)} %get-tuple-element.47), channel_id=1, source_target_pairs={{1,0},{2,1},{3,2},{4,3},{5,4},{6,5},{7,6},{9,8},{10,9},{11,10},{12... | collective-permute-start | bytes 221192 | tf_op jit(solution)/shard_map/ppermute | solution.py:141
  58.5 16.2 %collective-permute-start.13 = (bf16[4,16,1152]{2,1,0:T(8,128)(2,1)S(1)}, bf16[4,16,1152]{2,1,0:T(8,128)(2,1)S(1)}, u32[]{:S(2)}, u32[]{:S(2)}) collective-permute-start(bf16[4,16,1152]{2,1,0:T(8,128)(2,1)S(1)} %get-tuple-element.45), channel_id=1, source_target_pairs={{8,0},{16,8},{24,16},{9,1},{17,9},{25,17},{10,2},{18,10},{26,18},{... | collective-permute-start | bytes 442376 | tf_op jit(solution)/shard_map/ppermute | solution.py:141
  69.7 5.0 %collective-permute-start.12 = (bf16[4,16,1152]{2,1,0:T(8,128)(2,1)S(1)}, bf16[4,16,1152]{2,1,0:T(8,128)(2,1)S(1)}, u32[]{:S(2)}, u32[]{:S(2)}) collective-permute-start(bf16[4,16,1152]{2,1,0:T(8,128)(2,1)S(1)} %get-tuple-element.46), channel_id=1, source_target_pairs={{0,8},{8,16},{16,24},{1,9},{9,17},{17,25},{2,10},{10,18},{18,26},{... | collective-permute-start | bytes 442376 | tf_op jit(solution)/shard_map/ppermute | solution.py:141
  72.6 13.7 %collective-permute-start.18 = (bf16[2,256,512]{2,1,0:T(8,128)(2,1)S(1)}, bf16[2,256,512]{2,1,0:T(8,128)(2,1)S(1)}, u32[]{:S(2)}, u32[]{:S(2)}) collective-permute-start(bf16[2,256,512]{2,1,0:T(8,128)(2,1)S(1)} %maximum_select_fusion.4), channel_id=1, source_target_pairs={{0,1},{1,0},{2,3},{3,2},{4,5},{5,4},{6,7},{7,6},{8,9},{9,8},{10,11... | collective-permute-start | bytes 1572872 | tf_op jit(solution)/shard_map/ppermute | solution.py:49
  74.0 13.9 %collective-permute-start.23 = (bf16[2,512,512]{2,1,0:T(8,128)(2,1)S(1)}, bf16[2,512,512]{2,1,0:T(8,128)(2,1)S(1)}, u32[]{:S(2)}, u32[]{:S(2)}) collective-permute-start(bf16[2,512,512]{2,1,0:T(8,128)(2,1)S(1)} %maximum_select_fusion.3), channel_id=1, source_target_pairs={{0,8},{1,9},{2,10},{3,11},{4,12},{5,13},{6,14},{7,15},{8,0},{9,1},... | collective-permute-start | bytes 3145736 | tf_op jit(solution)/shard_map/ppermute | solution.py:49
  94.2 10.6 %collective-permute-start.24 = (bf16[2,1,16,256]{3,2,1,0:T(8,128)(2,1)S(1)}, bf16[2,1,16,256]{3,2,1,0:T(8,128)(2,1)S(1)}, u32[]{:S(2)}, u32[]{:S(2)}) collective-permute-start(bf16[2,1,16,256]{3,2,1,0:T(8,128)(2,1)S(1)} %get-tuple-element.49), channel_id=1, source_target_pairs={{0,1},{1,2},{2,3},{3,4},{4,5},{5,6},{6,7},{8,9},{9,10},{10,11},{11... | collective-permute-start | bytes 49160 | tf_op jit(solution)/shard_map/ppermute | solution.py:15
  97.0 7.7 %collective-permute-start.25 = (bf16[2,1,16,256]{3,2,1,0:T(8,128)(2,1)S(1)}, bf16[2,1,16,256]{3,2,1,0:T(8,128)(2,1)S(1)}, u32[]{:S(2)}, u32[]{:S(2)}) collective-permute-start(bf16[2,1,16,256]{3,2,1,0:T(8,128)(2,1)S(1)} %get-tuple-element.50), channel_id=1, source_target_pairs={{1,0},{2,1},{3,2},{4,3},{5,4},{6,5},{7,6},{9,8},{10,9},{11,10},{12... | collective-permute-start | bytes 49160 | tf_op jit(solution)/shard_map/ppermute | solution.py:18
  100.4 4.4 %collective-permute-start.26 = (bf16[1,4,16,256]{3,2,1,0:T(8,128)(2,1)S(1)}, bf16[1,4,16,256]{3,2,1,0:T(8,128)(2,1)S(1)}, u32[]{:S(2)}, u32[]{:S(2)}) collective-permute-start(bf16[1,4,16,256]{3,2,1,0:T(8,128)(2,1)S(1)} %get-tuple-element.53), channel_id=1, source_target_pairs={{0,8},{8,16},{16,24},{1,9},{9,17},{17,25},{2,10},{10,18},{18,26},{... | collective-permute-start | bytes 98312 | tf_op jit(solution)/shard_map/ppermute | solution.py:15
  102.6 5.2 %collective-permute-start.27 = (bf16[1,4,16,256]{3,2,1,0:T(8,128)(2,1)S(1)}, bf16[1,4,16,256]{3,2,1,0:T(8,128)(2,1)S(1)}, u32[]{:S(2)}, u32[]{:S(2)}) collective-permute-start(bf16[1,4,16,256]{3,2,1,0:T(8,128)(2,1)S(1)} %get-tuple-element.54), channel_id=1, source_target_pairs={{8,0},{16,8},{24,16},{9,1},{17,9},{25,17},{10,2},{18,10},{26,18},{... | collective-permute-start | bytes 98312 | tf_op jit(solution)/shard_map/ppermute | solution.py:18
  (9 other events, 27.7 us)

commit v8 on v7

--- a/solution.py
+++ b/solution.py
@@ -43,21 +43,26 @@
     return bits if (1 << bits) == count else None
 
 
-def swap(block, bit, col_bits):
+def swap(block, bits, core):
     count = lax.axis_size("col") * lax.axis_size("row")
-    pairs = [(i, i ^ (1 << bit)) for i in range(count)]
+    pairs = [(i, i ^ (1 << bits[(i >> core) & 1])) for i in range(count)]
     return lax.ppermute(block, ("row", "col"), pairs)
 
 
-def scatter_gather(blocks, owner, orders, col_bits, me, tie):
-    stages = len(orders[0])
+def scatter_gather(blocks, owner, orders, core, me, tie):
+    stages = len(orders[0][0])
     full = (1 << stages) - 1
-    done_mask = [0] * len(blocks)
+    my_core = (me >> core) & 1
+    done_mask = [[0, 0] for _ in blocks]
+
+    def pick(pair):
+        return jnp.where(my_core == 1, pair[1], pair[0])
+
     for step in range(stages):
         gots, keeps = [], []
         for s, block in enumerate(blocks):
-            bit = orders[s][step]
-            mine = ((me >> bit) & 1) == 1
+            bits = (orders[s][0][step], orders[s][1][step])
+            mine = ((me >> pick(bits)) & 1) == 1
             if step == 0:
                 half = block.shape[0] // 2
                 keep = jnp.where(mine, block[half:], block[:half])[None]
@@ -66,20 +71,24 @@
                 half = block.shape[1] // 2
                 keep = jnp.where(mine, block[:, half:], block[:, :half])
                 give = jnp.where(mine, block[:, :half], block[:, half:])
-            got = swap(give, bit, col_bits)
+            got = swap(give, bits, core)
             keeps.append(keep)
             gots.append(got[None] if step == 0 else got)
         for s in range(len(blocks)):
-            have = ((me ^ owner) & (full & ~done_mask[s])) == 0
+            outside = pick([full & ~done_mask[s][0], full & ~done_mask[s][1]])
+            have = ((me ^ owner) & outside) == 0
             blocks[s] = jnp.where(have[:, None, None], keeps[s], gots[s])
-            done_mask[s] |= 1 << orders[s][step]
+            for c in range(2):
+                done_mask[s][c] |= 1 << orders[s][c][step]
         blocks = list(lax.optimization_barrier(tuple(blocks)))
     blocks, tie = lax.optimization_barrier((tuple(blocks), tie))
     blocks = list(blocks)
     for step in reversed(range(stages)):
-        gots = [swap(block, orders[s][step], col_bits) for s, block in enumerate(blocks)]
+        gots = []
+        for s, block in enumerate(blocks):
+            gots.append(swap(block, (orders[s][0][step], orders[s][1][step]), core))
         for s in range(len(blocks)):
-            mine = ((me >> orders[s][step]) & 1) == 1
+            mine = ((me >> pick((orders[s][0][step], orders[s][1][step]))) & 1) == 1
             blocks[s] = jnp.where(
                 mine, jnp.concatenate([gots[s], blocks[s]], axis=1), jnp.concatenate([blocks[s], gots[s]], axis=1)
             )
@@ -108,10 +117,14 @@
     offset = 0
     for s in range(streams):
         cols = sizes[s] * 128
-        orders.append([core] + middle[s:] + middle[:s] + last)
+        pair = []
+        for c in range(2):
+            turn = (2 * s + c) % len(middle)
+            pair.append([core] + middle[turn:] + middle[:turn] + last)
+        orders.append(pair)
         blocks.append(own_operator[:, offset : offset + cols])
         offset += cols
-    parts, tie = scatter_gather(blocks, owner, orders, col_bits, me, tie)
+    parts, tie = scatter_gather(blocks, owner, orders, core, me, tie)
     return parts, tie
 
 

time: 111 us -> 109 us (0.982)
  waiting for transfers between devices: 47.6 us -> 39.4 us
  starting transfers between devices: 48.2 us -> 55.3 us
    ppermute x20, waiting for transfers between devices: 44.5 us -> 35.9 us  [swap(): return lax.ppermute(block, ('row', 'col'), pairs)]
    ppermute x4, starting transfers between devices: 17.9 us -> 24 us  [shift(): return lax.ppermute(block, axis, pairs)]
    ppermute x2, starting transfers between devices: 5.09 us -> 7.3 us  [with_halo(): lax.ppermute(lax.slice_in_dim(block, block.shape[dim] - width, None, axis...]
where the time goes in v8:
time: 109 us
  starting transfers between devices  55.3 us (51%)
  waiting for transfers between devices  39.4 us (36%)
  other arithmetic  8.03 us (7%)
  matrix products  4.44 us (4%)
  local copies, waits for them, and re-layouts  1.13 us (1%)
    ppermute x20, waiting for transfers between devices, swap(): return lax.ppermute(block, ('row', 'col'), pairs)  35.9 us
    ppermute x4, starting transfers between devices, shift(): return lax.ppermute(block, axis, pairs)  24 us
    ppermute x20, starting transfers between devices, swap(): return lax.ppermute(block, ('row', 'col'), pairs)  19.2 us
    ppermute x2, starting transfers between devices, with_halo(): lax.ppermute(lax.slice_in_dim(block, block.shape[dim] - width, None, axis...  7.3 us
    ppermute x2, starting transfers between devices, with_halo(): lax.ppermute(lax.slice_in_dim(block, 0, width, axis=dim), axis, backward)  4.79 us
    dot_general x12, matrix products, sweep(): jnp.dot(rows, part[k], preferred_element_type=jnp.float32)  4.44 us
    ppermute x2, waiting for transfers between devices, with_halo(): lax.ppermute(lax.slice_in_dim(block, 0, width, axis=dim), axis, backward)  3.26 us
    select_n x10, other arithmetic, scatter_gather(): jnp.where(mine, jnp.concatenate([gots[s], blocks[s]], axis=1), jnp.concat...  2.84 us
  transfers between devices with their start and end apart: 28, of which 17 were waited for; matrix products, arithmetic and copies ran while one was open for 4% of the time, Pallas kernels for 0%

profile of v8, /device:TPU:9, one launch (start us, length us, event | category | flops | bytes accessed | tf_op | source)
XLA Modules:
  0.0 108.9 jit_solution(1471043832348893466)
XLA Ops:
  0.0 1.7 %broadcast_select_fusion.4 = (bf16[512,512]{1,0:T(8,128)(2,1)S(1)}, bf16[512,512]{1,0:T(8,128)(2,1)S(1)}, bf16[512,512]{1,0:T(8,128)(2,1)S(1)}, bf16[512,512]{1,0:T(8,128)(2,1)S(1)}) fusion(pred[]{:T(512)S(6)} %eq.59, bf16[1024,1024]{1,0:T(8,128)(2,1)} %bitcast.68), kind=kLoop, calls=%fused_computation.40 | loop fusion | flops 1048576 | bytes 4194305 | tf_op jit(solution)/shard_map/jit(_where)/select_n | solution.py:68
  6.8 9.7 %collective-permute-done.3 = bf16[2,256,512]{2,1,0:T(8,128)(2,1)S(1)} collective-permute-done((bf16[2,256,512]{2,1,0:T(8,128)(2,1)S(1)}, bf16[2,256,512]{2,1,0:T(8,128)(2,1)S(1)}, u32[]{:S(2)}, u32[]{:S(2)}) %collective-permute-start.3) | collective-permute-done | bytes 524320 | tf_op jit(solution)/shard_map/ppermute | solution.py:49
  16.9 3.0 %collective-permute-start.4 = (bf16[2,128,512]{2,1,0:T(8,128)(2,1)S(1)}, bf16[2,128,512]{2,1,0:T(8,128)(2,1)S(1)}, u32[]{:S(2)}, u32[]{:S(2)}) collective-permute-start(bf16[2,128,512]{2,1,0:T(8,128)(2,1)S(1)} %broadcast_select_fusion.9), channel_id=1, source_target_pairs={{0,2},{1,3},{2,0},{3,1},{4,6},{5,7},{6,4},{7,5},{8,24},{9,25},{10,... | collective-permute-start | bytes 786440 | tf_op jit(solution)/shard_map/ppermute | solution.py:49
  20.1 2.0 %collective-permute-done.5 = bf16[2,128,512]{2,1,0:T(8,128)(2,1)S(1)} collective-permute-done((bf16[2,128,512]{2,1,0:T(8,128)(2,1)S(1)}, bf16[2,128,512]{2,1,0:T(8,128)(2,1)S(1)}, u32[]{:S(2)}, u32[]{:S(2)}) %collective-permute-start.5) | collective-permute-done | bytes 262176 | tf_op jit(solution)/shard_map/ppermute | solution.py:49
  22.2 1.8 %collective-permute-done.4 = bf16[2,128,512]{2,1,0:T(8,128)(2,1)S(1)} collective-permute-done((bf16[2,128,512]{2,1,0:T(8,128)(2,1)S(1)}, bf16[2,128,512]{2,1,0:T(8,128)(2,1)S(1)}, u32[]{:S(2)}, u32[]{:S(2)}) %collective-permute-start.4) | collective-permute-done | bytes 262176 | tf_op jit(solution)/shard_map/ppermute | solution.py:49
  26.4 1.6 %collective-permute-done.7 = bf16[2,64,512]{2,1,0:T(8,128)(2,1)S(1)} collective-permute-done((bf16[2,64,512]{2,1,0:T(8,128)(2,1)S(1)}, bf16[2,64,512]{2,1,0:T(8,128)(2,1)S(1)}, u32[]{:S(2)}, u32[]{:S(2)}) %collective-permute-start.7) | collective-permute-done | bytes 131104 | tf_op jit(solution)/shard_map/ppermute | solution.py:49
  29.7 1.8 %collective-permute-start.9 = (bf16[2,32,512]{2,1,0:T(8,128)(2,1)S(1)}, bf16[2,32,512]{2,1,0:T(8,128)(2,1)S(1)}, u32[]{:S(2)}, u32[]{:S(2)}) collective-permute-start(bf16[2,32,512]{2,1,0:T(8,128)(2,1)S(1)} %broadcast_select_fusion.12), channel_id=1, source_target_pairs={{0,4},{1,5},{2,6},{3,7},{4,0},{5,1},{6,2},{7,3},{8,12},{9,13},{10,... | collective-permute-start | bytes 196616 | tf_op jit(solution)/shard_map/ppermute | solution.py:49
  32.2 1.8 %collective-permute-done.9 = bf16[2,32,512]{2,1,0:T(8,128)(2,1)S(1)} collective-permute-done((bf16[2,32,512]{2,1,0:T(8,128)(2,1)S(1)}, bf16[2,32,512]{2,1,0:T(8,128)(2,1)S(1)}, u32[]{:S(2)}, u32[]{:S(2)}) %collective-permute-start.9) | collective-permute-done | bytes 65568 | tf_op jit(solution)/shard_map/ppermute | solution.py:49
  34.0 1.6 %collective-permute-done.8 = bf16[2,32,512]{2,1,0:T(8,128)(2,1)S(1)} collective-permute-done((bf16[2,32,512]{2,1,0:T(8,128)(2,1)S(1)}, bf16[2,32,512]{2,1,0:T(8,128)(2,1)S(1)}, u32[]{:S(2)}, u32[]{:S(2)}) %collective-permute-start.8) | collective-permute-done | bytes 65568 | tf_op jit(solution)/shard_map/ppermute | solution.py:49
  35.7 2.1 %collective-permute-start.14 = (bf16[2,32,512]{2,1,0:T(8,128)(2,1)S(1)}, bf16[2,32,512]{2,1,0:T(8,128)(2,1)S(1)}, u32[]{:S(2)}, u32[]{:S(2)}) collective-permute-start(bf16[2,32,512]{2,1,0:T(8,128)(2,1)S(1)} %get-tuple-element.31), channel_id=1, source_target_pairs={{0,4},{1,5},{2,6},{3,7},{4,0},{5,1},{6,2},{7,3},{8,12},{9,13},{10,... | collective-permute-start | bytes 196616 | tf_op jit(solution)/shard_map/ppermute | solution.py:49
  38.3 3.6 %collective-permute-done.14 = bf16[2,32,512]{2,1,0:T(8,128)(2,1)S(1)} collective-permute-done((bf16[2,32,512]{2,1,0:T(8,128)(2,1)S(1)}, bf16[2,32,512]{2,1,0:T(8,128)(2,1)S(1)}, u32[]{:S(2)}, u32[]{:S(2)}) %collective-permute-start.14) | collective-permute-done | bytes 65568 | tf_op jit(solution)/shard_map/ppermute | solution.py:49
  44.1 2.6 %collective-permute-done.20 = bf16[2,64,512]{2,1,0:T(8,128)(2,1)S(1)} collective-permute-done((bf16[2,64,512]{2,1,0:T(8,128)(2,1)S(1)}, bf16[2,64,512]{2,1,0:T(8,128)(2,1)S(1)}, u32[]{:S(2)}, u32[]{:S(2)}) %collective-permute-start.20) | collective-permute-done | bytes 131104 | tf_op jit(solution)/shard_map/ppermute | solution.py:49
  46.8 1.7 %collective-permute-start.21 = (bf16[2,128,512]{2,1,0:T(8,128)(2,1)S(1)}, bf16[2,128,512]{2,1,0:T(8,128)(2,1)S(1)}, u32[]{:S(2)}, u32[]{:S(2)}) collective-permute-start(bf16[2,128,512]{2,1,0:T(8,128)(2,1)S(1)} %maximum_select_fusion.7), channel_id=1, source_target_pairs={{0,1},{1,0},{2,3},{3,2},{4,5},{5,4},{6,7},{7,6},{8,10},{9,11},{10,... | collective-permute-start | bytes 786440 | tf_op jit(solution)/shard_map/ppermute | solution.py:49
  48.5 3.4 %collective-permute-start.10 = (bf16[2,16,1152]{2,1,0:T(8,128)(2,1)S(1)}, bf16[2,16,1152]{2,1,0:T(8,128)(2,1)S(1)}, u32[]{:S(2)}, u32[]{:S(2)}) collective-permute-start(bf16[2,16,1152]{2,1,0:T(8,128)(2,1)S(1)} %get-tuple-element.48), channel_id=1, source_target_pairs={{0,1},{1,2},{2,3},{3,4},{4,5},{5,6},{6,7},{8,9},{9,10},{10,11},{11... | collective-permute-start | bytes 221192 | tf_op jit(solution)/shard_map/ppermute | solution.py:154
  52.8 1.7 %collective-permute-start.22 = (bf16[2,256,512]{2,1,0:T(8,128)(2,1)S(1)}, bf16[2,256,512]{2,1,0:T(8,128)(2,1)S(1)}, u32[]{:S(2)}, u32[]{:S(2)}) collective-permute-start(bf16[2,256,512]{2,1,0:T(8,128)(2,1)S(1)} %maximum_select_fusion.5), channel_id=1, source_target_pairs={{0,16},{1,17},{2,18},{3,19},{4,20},{5,21},{6,22},{7,23},{8,9},{9,8... | collective-permute-start | bytes 1572872 | tf_op jit(solution)/shard_map/ppermute | solution.py:49
  54.5 2.6 %collective-permute-start.11 = (bf16[2,16,1152]{2,1,0:T(8,128)(2,1)S(1)}, bf16[2,16,1152]{2,1,0:T(8,128)(2,1)S(1)}, u32[]{:S(2)}, u32[]{:S(2)}) collective-permute-start(bf16[2,16,1152]{2,1,0:T(8,128)(2,1)S(1)} %get-tuple-element.47), channel_id=1, source_target_pairs={{1,0},{2,1},{3,2},{4,3},{5,4},{6,5},{7,6},{9,8},{10,9},{11,10},{12... | collective-permute-start | bytes 221192 | tf_op jit(solution)/shard_map/ppermute | solution.py:154
  57.1 15.0 %collective-permute-start.13 = (bf16[4,16,1152]{2,1,0:T(8,128)(2,1)S(1)}, bf16[4,16,1152]{2,1,0:T(8,128)(2,1)S(1)}, u32[]{:S(2)}, u32[]{:S(2)}) collective-permute-start(bf16[4,16,1152]{2,1,0:T(8,128)(2,1)S(1)} %get-tuple-element.45), channel_id=1, source_target_pairs={{8,0},{16,8},{24,16},{9,1},{17,9},{25,17},{10,2},{18,10},{26,18},{... | collective-permute-start | bytes 442376 | tf_op jit(solution)/shard_map/ppermute | solution.py:154
  72.1 3.1 %collective-permute-start.12 = (bf16[4,16,1152]{2,1,0:T(8,128)(2,1)S(1)}, bf16[4,16,1152]{2,1,0:T(8,128)(2,1)S(1)}, u32[]{:S(2)}, u32[]{:S(2)}) collective-permute-start(bf16[4,16,1152]{2,1,0:T(8,128)(2,1)S(1)} %get-tuple-element.46), channel_id=1, source_target_pairs={{0,8},{8,16},{16,24},{1,9},{9,17},{17,25},{2,10},{10,18},{18,26},{... | collective-permute-start | bytes 442376 | tf_op jit(solution)/shard_map/ppermute | solution.py:154
  77.3 6.3 %collective-permute-done.18 = bf16[2,256,512]{2,1,0:T(8,128)(2,1)S(1)} collective-permute-done((bf16[2,256,512]{2,1,0:T(8,128)(2,1)S(1)}, bf16[2,256,512]{2,1,0:T(8,128)(2,1)S(1)}, u32[]{:S(2)}, u32[]{:S(2)}) %collective-permute-start.18) | collective-permute-done | bytes 524320 | tf_op jit(solution)/shard_map/ppermute | solution.py:49
  91.2 3.3 %collective-permute-start.24 = (bf16[2,1,16,256]{3,2,1,0:T(8,128)(2,1)S(1)}, bf16[2,1,16,256]{3,2,1,0:T(8,128)(2,1)S(1)}, u32[]{:S(2)}, u32[]{:S(2)}) collective-permute-start(bf16[2,1,16,256]{3,2,1,0:T(8,128)(2,1)S(1)} %get-tuple-element.49), channel_id=1, source_target_pairs={{0,1},{1,2},{2,3},{3,4},{4,5},{5,6},{6,7},{8,9},{9,10},{10,11},{11... | collective-permute-start | bytes 49160 | tf_op jit(solution)/shard_map/ppermute | solution.py:15
  94.6 2.9 %collective-permute-start.25 = (bf16[2,1,16,256]{3,2,1,0:T(8,128)(2,1)S(1)}, bf16[2,1,16,256]{3,2,1,0:T(8,128)(2,1)S(1)}, u32[]{:S(2)}, u32[]{:S(2)}) collective-permute-start(bf16[2,1,16,256]{3,2,1,0:T(8,128)(2,1)S(1)} %get-tuple-element.50), channel_id=1, source_target_pairs={{1,0},{2,1},{3,2},{4,3},{5,4},{6,5},{7,6},{9,8},{10,9},{11,10},{12... | collective-permute-start | bytes 49160 | tf_op jit(solution)/shard_map/ppermute | solution.py:18
  97.4 4.0 %collective-permute-start.26 = (bf16[1,4,16,256]{3,2,1,0:T(8,128)(2,1)S(1)}, bf16[1,4,16,256]{3,2,1,0:T(8,128)(2,1)S(1)}, u32[]{:S(2)}, u32[]{:S(2)}) collective-permute-start(bf16[1,4,16,256]{3,2,1,0:T(8,128)(2,1)S(1)} %get-tuple-element.53), channel_id=1, source_target_pairs={{0,8},{8,16},{16,24},{1,9},{9,17},{17,25},{2,10},{10,18},{18,26},{... | collective-permute-start | bytes 98312 | tf_op jit(solution)/shard_map/ppermute | solution.py:15
  101.4 1.9 %collective-permute-start.27 = (bf16[1,4,16,256]{3,2,1,0:T(8,128)(2,1)S(1)}, bf16[1,4,16,256]{3,2,1,0:T(8,128)(2,1)S(1)}, u32[]{:S(2)}, u32[]{:S(2)}) collective-permute-start(bf16[1,4,16,256]{3,2,1,0:T(8,128)(2,1)S(1)} %get-tuple-element.54), channel_id=1, source_target_pairs={{8,0},{16,8},{24,16},{9,1},{17,9},{25,17},{10,2},{18,10},{26,18},{... | collective-permute-start | bytes 98312 | tf_op jit(solution)/shard_map/ppermute | solution.py:18
  103.4 3.3 %collective-permute-done.27 = bf16[1,4,16,256]{3,2,1,0:T(8,128)(2,1)S(1)} collective-permute-done((bf16[1,4,16,256]{3,2,1,0:T(8,128)(2,1)S(1)}, bf16[1,4,16,256]{3,2,1,0:T(8,128)(2,1)S(1)}, u32[]{:S(2)}, u32[]{:S(2)}) %collective-permute-start.27) | collective-permute-done | bytes 32800 | tf_op jit(solution)/shard_map/ppermute | solution.py:18
  (125 shorter events, 25.8 us)
Async XLA Ops:
  5.1 11.5 %collective-permute-start.3 = (bf16[2,256,512]{2,1,0:T(8,128)(2,1)S(1)}, bf16[2,256,512]{2,1,0:T(8,128)(2,1)S(1)}, u32[]{:S(2)}, u32[]{:S(2)}) collective-permute-start(bf16[2,256,512]{2,1,0:T(8,128)(2,1)S(1)} %broadcast_select_fusion.2), channel_id=1, source_target_pairs={{0,16},{1,17},{2,18},{3,19},{4,20},{5,21},{6,22},{7,23},{8,9},{9,8... | collective-permute-start | bytes 1572872 | tf_op jit(solution)/shard_map/ppermute | solution.py:49
  6.4 10.1 %collective-permute-start.2 = (bf16[2,256,512]{2,1,0:T(8,128)(2,1)S(1)}, bf16[2,256,512]{2,1,0:T(8,128)(2,1)S(1)}, u32[]{:S(2)}, u32[]{:S(2)}) collective-permute-start(bf16[2,256,512]{2,1,0:T(8,128)(2,1)S(1)} %broadcast_select_fusion.7), channel_id=1, source_target_pairs={{0,1},{1,0},{2,3},{3,2},{4,5},{5,4},{6,7},{7,6},{8,10},{9,11},{10,... | collective-permute-start | bytes 1572872 | tf_op jit(solution)/shard_map/ppermute | solution.py:49
  16.8 5.3 %collective-permute-start.5 = (bf16[2,128,512]{2,1,0:T(8,128)(2,1)S(1)}, bf16[2,128,512]{2,1,0:T(8,128)(2,1)S(1)}, u32[]{:S(2)}, u32[]{:S(2)}) collective-permute-start(bf16[2,128,512]{2,1,0:T(8,128)(2,1)S(1)} %broadcast_select_fusion.8), channel_id=1, source_target_pairs={{0,1},{1,0},{2,3},{3,2},{4,5},{5,4},{6,7},{7,6},{8,10},{9,11},{10,... | collective-permute-start | bytes 786440 | tf_op jit(solution)/shard_map/ppermute | solution.py:49
  16.9 7.1 %collective-permute-start.4 = (bf16[2,128,512]{2,1,0:T(8,128)(2,1)S(1)}, bf16[2,128,512]{2,1,0:T(8,128)(2,1)S(1)}, u32[]{:S(2)}, u32[]{:S(2)}) collective-permute-start(bf16[2,128,512]{2,1,0:T(8,128)(2,1)S(1)} %broadcast_select_fusion.9), channel_id=1, source_target_pairs={{0,2},{1,3},{2,0},{3,1},{4,6},{5,7},{6,4},{7,5},{8,24},{9,25},{10,... | collective-permute-start | bytes 786440 | tf_op jit(solution)/shard_map/ppermute | solution.py:49
  24.1 3.9 %collective-permute-start.7 = (bf16[2,64,512]{2,1,0:T(8,128)(2,1)S(1)}, bf16[2,64,512]{2,1,0:T(8,128)(2,1)S(1)}, u32[]{:S(2)}, u32[]{:S(2)}) collective-permute-start(bf16[2,64,512]{2,1,0:T(8,128)(2,1)S(1)} %broadcast_select_fusion.10), channel_id=1, source_target_pairs={{0,2},{1,3},{2,0},{3,1},{4,6},{5,7},{6,4},{7,5},{8,24},{9,25},{10,... | collective-permute-start | bytes 393224 | tf_op jit(solution)/shard_map/ppermute | solution.py:49
  29.7 4.3 %collective-permute-start.9 = (bf16[2,32,512]{2,1,0:T(8,128)(2,1)S(1)}, bf16[2,32,512]{2,1,0:T(8,128)(2,1)S(1)}, u32[]{:S(2)}, u32[]{:S(2)}) collective-permute-start(bf16[2,32,512]{2,1,0:T(8,128)(2,1)S(1)} %broadcast_select_fusion.12), channel_id=1, source_target_pairs={{0,4},{1,5},{2,6},{3,7},{4,0},{5,1},{6,2},{7,3},{8,12},{9,13},{10,... | collective-permute-start | bytes 196616 | tf_op jit(solution)/shard_map/ppermute | solution.py:49
  31.5 4.1 %collective-permute-start.8 = (bf16[2,32,512]{2,1,0:T(8,128)(2,1)S(1)}, bf16[2,32,512]{2,1,0:T(8,128)(2,1)S(1)}, u32[]{:S(2)}, u32[]{:S(2)}) collective-permute-start(bf16[2,32,512]{2,1,0:T(8,128)(2,1)S(1)} %broadcast_select_fusion.13), channel_id=1, source_target_pairs={{0,4},{1,5},{2,6},{3,7},{4,0},{5,1},{6,2},{7,3},{8,12},{9,13},{10,... | collective-permute-start | bytes 196616 | tf_op jit(solution)/shard_map/ppermute | solution.py:49
  35.7 6.2 %collective-permute-start.14 = (bf16[2,32,512]{2,1,0:T(8,128)(2,1)S(1)}, bf16[2,32,512]{2,1,0:T(8,128)(2,1)S(1)}, u32[]{:S(2)}, u32[]{:S(2)}) collective-permute-start(bf16[2,32,512]{2,1,0:T(8,128)(2,1)S(1)} %get-tuple-element.31), channel_id=1, source_target_pairs={{0,4},{1,5},{2,6},{3,7},{4,0},{5,1},{6,2},{7,3},{8,12},{9,13},{10,... | collective-permute-start | bytes 196616 | tf_op jit(solution)/shard_map/ppermute | solution.py:49
  37.9 4.6 %collective-permute-start.15 = (bf16[2,32,512]{2,1,0:T(8,128)(2,1)S(1)}, bf16[2,32,512]{2,1,0:T(8,128)(2,1)S(1)}, u32[]{:S(2)}, u32[]{:S(2)}) collective-permute-start(bf16[2,32,512]{2,1,0:T(8,128)(2,1)S(1)} %get-tuple-element.32), channel_id=1, source_target_pairs={{0,4},{1,5},{2,6},{3,7},{4,0},{5,1},{6,2},{7,3},{8,12},{9,13},{10,... | collective-permute-start | bytes 196616 | tf_op jit(solution)/shard_map/ppermute | solution.py:49
  42.6 4.2 %collective-permute-start.20 = (bf16[2,64,512]{2,1,0:T(8,128)(2,1)S(1)}, bf16[2,64,512]{2,1,0:T(8,128)(2,1)S(1)}, u32[]{:S(2)}, u32[]{:S(2)}) collective-permute-start(bf16[2,64,512]{2,1,0:T(8,128)(2,1)S(1)} %maximum_select_fusion.9), channel_id=1, source_target_pairs={{0,2},{1,3},{2,0},{3,1},{4,6},{5,7},{6,4},{7,5},{8,24},{9,25},{10,... | collective-permute-start | bytes 393224 | tf_op jit(solution)/shard_map/ppermute | solution.py:49
  43.7 8.2 %collective-permute-start.16 = (bf16[2,64,512]{2,1,0:T(8,128)(2,1)S(1)}, bf16[2,64,512]{2,1,0:T(8,128)(2,1)S(1)}, u32[]{:S(2)}, u32[]{:S(2)}) collective-permute-start(bf16[2,64,512]{2,1,0:T(8,128)(2,1)S(1)} %maximum_select_fusion.8), channel_id=1, source_target_pairs={{0,16},{1,17},{2,18},{3,19},{4,20},{5,21},{6,22},{7,23},{8,9},{9,8... | collective-permute-start | bytes 393224 | tf_op jit(solution)/shard_map/ppermute | solution.py:49
  46.8 5.7 %collective-permute-start.21 = (bf16[2,128,512]{2,1,0:T(8,128)(2,1)S(1)}, bf16[2,128,512]{2,1,0:T(8,128)(2,1)S(1)}, u32[]{:S(2)}, u32[]{:S(2)}) collective-permute-start(bf16[2,128,512]{2,1,0:T(8,128)(2,1)S(1)} %maximum_select_fusion.7), channel_id=1, source_target_pairs={{0,1},{1,0},{2,3},{3,2},{4,5},{5,4},{6,7},{7,6},{8,10},{9,11},{10,... | collective-permute-start | bytes 786440 | tf_op jit(solution)/shard_map/ppermute | solution.py:49
  48.5 23.6 %collective-permute-start.10 = (bf16[2,16,1152]{2,1,0:T(8,128)(2,1)S(1)}, bf16[2,16,1152]{2,1,0:T(8,128)(2,1)S(1)}, u32[]{:S(2)}, u32[]{:S(2)}) collective-permute-start(bf16[2,16,1152]{2,1,0:T(8,128)(2,1)S(1)} %get-tuple-element.48), channel_id=1, source_target_pairs={{0,1},{1,2},{2,3},{3,4},{4,5},{5,6},{6,7},{8,9},{9,10},{10,11},{11... | collective-permute-start | bytes 221192 | tf_op jit(solution)/shard_map/ppermute | solution.py:154
  52.0 23.3 %collective-permute-start.17 = (bf16[2,128,512]{2,1,0:T(8,128)(2,1)S(1)}, bf16[2,128,512]{2,1,0:T(8,128)(2,1)S(1)}, u32[]{:S(2)}, u32[]{:S(2)}) collective-permute-start(bf16[2,128,512]{2,1,0:T(8,128)(2,1)S(1)} %maximum_select_fusion.6), channel_id=1, source_target_pairs={{0,2},{1,3},{2,0},{3,1},{4,6},{5,7},{6,4},{7,5},{8,24},{9,25},{10,... | collective-permute-start | bytes 786440 | tf_op jit(solution)/shard_map/ppermute | solution.py:49
  52.8 22.8 %collective-permute-start.22 = (bf16[2,256,512]{2,1,0:T(8,128)(2,1)S(1)}, bf16[2,256,512]{2,1,0:T(8,128)(2,1)S(1)}, u32[]{:S(2)}, u32[]{:S(2)}) collective-permute-start(bf16[2,256,512]{2,1,0:T(8,128)(2,1)S(1)} %maximum_select_fusion.5), channel_id=1, source_target_pairs={{0,16},{1,17},{2,18},{3,19},{4,20},{5,21},{6,22},{7,23},{8,9},{9,8... | collective-permute-start | bytes 1572872 | tf_op jit(solution)/shard_map/ppermute | solution.py:49
  54.5 22.5 %collective-permute-start.11 = (bf16[2,16,1152]{2,1,0:T(8,128)(2,1)S(1)}, bf16[2,16,1152]{2,1,0:T(8,128)(2,1)S(1)}, u32[]{:S(2)}, u32[]{:S(2)}) collective-permute-start(bf16[2,16,1152]{2,1,0:T(8,128)(2,1)S(1)} %get-tuple-element.47), channel_id=1, source_target_pairs={{1,0},{2,1},{3,2},{4,3},{5,4},{6,5},{7,6},{9,8},{10,9},{11,10},{12... | collective-permute-start | bytes 221192 | tf_op jit(solution)/shard_map/ppermute | solution.py:154
  57.1 20.2 %collective-permute-start.13 = (bf16[4,16,1152]{2,1,0:T(8,128)(2,1)S(1)}, bf16[4,16,1152]{2,1,0:T(8,128)(2,1)S(1)}, u32[]{:S(2)}, u32[]{:S(2)}) collective-permute-start(bf16[4,16,1152]{2,1,0:T(8,128)(2,1)S(1)} %get-tuple-element.45), channel_id=1, source_target_pairs={{8,0},{16,8},{24,16},{9,1},{17,9},{25,17},{10,2},{18,10},{26,18},{... | collective-permute-start | bytes 442376 | tf_op jit(solution)/shard_map/ppermute | solution.py:154
  72.1 5.2 %collective-permute-start.12 = (bf16[4,16,1152]{2,1,0:T(8,128)(2,1)S(1)}, bf16[4,16,1152]{2,1,0:T(8,128)(2,1)S(1)}, u32[]{:S(2)}, u32[]{:S(2)}) collective-permute-start(bf16[4,16,1152]{2,1,0:T(8,128)(2,1)S(1)} %get-tuple-element.46), channel_id=1, source_target_pairs={{0,8},{8,16},{16,24},{1,9},{9,17},{17,25},{2,10},{10,18},{18,26},{... | collective-permute-start | bytes 442376 | tf_op jit(solution)/shard_map/ppermute | solution.py:154
  75.4 8.2 %collective-permute-start.18 = (bf16[2,256,512]{2,1,0:T(8,128)(2,1)S(1)}, bf16[2,256,512]{2,1,0:T(8,128)(2,1)S(1)}, u32[]{:S(2)}, u32[]{:S(2)}) collective-permute-start(bf16[2,256,512]{2,1,0:T(8,128)(2,1)S(1)} %maximum_select_fusion.4), channel_id=1, source_target_pairs={{0,1},{1,0},{2,3},{3,2},{4,5},{5,4},{6,7},{7,6},{8,10},{9,11},{10,... | collective-permute-start | bytes 1572872 | tf_op jit(solution)/shard_map/ppermute | solution.py:49
  76.0 9.1 %collective-permute-start.23 = (bf16[2,512,512]{2,1,0:T(8,128)(2,1)S(1)}, bf16[2,512,512]{2,1,0:T(8,128)(2,1)S(1)}, u32[]{:S(2)}, u32[]{:S(2)}) collective-permute-start(bf16[2,512,512]{2,1,0:T(8,128)(2,1)S(1)} %maximum_select_fusion.3), channel_id=1, source_target_pairs={{0,8},{1,9},{2,10},{3,11},{4,12},{5,13},{6,14},{7,15},{8,0},{9,1},... | collective-permute-start | bytes 3145736 | tf_op jit(solution)/shard_map/ppermute | solution.py:49
  91.2 12.1 %collective-permute-start.24 = (bf16[2,1,16,256]{3,2,1,0:T(8,128)(2,1)S(1)}, bf16[2,1,16,256]{3,2,1,0:T(8,128)(2,1)S(1)}, u32[]{:S(2)}, u32[]{:S(2)}) collective-permute-start(bf16[2,1,16,256]{3,2,1,0:T(8,128)(2,1)S(1)} %get-tuple-element.49), channel_id=1, source_target_pairs={{0,1},{1,2},{2,3},{3,4},{4,5},{5,6},{6,7},{8,9},{9,10},{10,11},{11... | collective-permute-start | bytes 49160 | tf_op jit(solution)/shard_map/ppermute | solution.py:15
  94.6 8.8 %collective-permute-start.25 = (bf16[2,1,16,256]{3,2,1,0:T(8,128)(2,1)S(1)}, bf16[2,1,16,256]{3,2,1,0:T(8,128)(2,1)S(1)}, u32[]{:S(2)}, u32[]{:S(2)}) collective-permute-start(bf16[2,1,16,256]{3,2,1,0:T(8,128)(2,1)S(1)} %get-tuple-element.50), channel_id=1, source_target_pairs={{1,0},{2,1},{3,2},{4,3},{5,4},{6,5},{7,6},{9,8},{10,9},{11,10},{12... | collective-permute-start | bytes 49160 | tf_op jit(solution)/shard_map/ppermute | solution.py:18
  97.4 6.0 %collective-permute-start.26 = (bf16[1,4,16,256]{3,2,1,0:T(8,128)(2,1)S(1)}, bf16[1,4,16,256]{3,2,1,0:T(8,128)(2,1)S(1)}, u32[]{:S(2)}, u32[]{:S(2)}) collective-permute-start(bf16[1,4,16,256]{3,2,1,0:T(8,128)(2,1)S(1)} %get-tuple-element.53), channel_id=1, source_target_pairs={{0,8},{8,16},{16,24},{1,9},{9,17},{17,25},{2,10},{10,18},{18,26},{... | collective-permute-start | bytes 98312 | tf_op jit(solution)/shard_map/ppermute | solution.py:15
  101.4 5.2 %collective-permute-start.27 = (bf16[1,4,16,256]{3,2,1,0:T(8,128)(2,1)S(1)}, bf16[1,4,16,256]{3,2,1,0:T(8,128)(2,1)S(1)}, u32[]{:S(2)}, u32[]{:S(2)}) collective-permute-start(bf16[1,4,16,256]{3,2,1,0:T(8,128)(2,1)S(1)} %get-tuple-element.54), channel_id=1, source_target_pairs={{8,0},{16,8},{24,16},{9,1},{17,9},{25,17},{10,2},{18,10},{26,18},{... | collective-permute-start | bytes 98312 | tf_op jit(solution)/shard_map/ppermute | solution.py:18
  (9 other events, 28.9 us)

commit v9 on v8

--- a/solution.py
+++ b/solution.py
@@ -7,17 +7,17 @@
 SWEEPS = 3
 
 
-def with_halo(block, sides, width):
-    for axis, dim in sides:
-        count = lax.axis_size(axis)
+def neighbours(send_low, send_high, axis):
+    count = lax.axis_size(axis)
+    if count % 2:
         forward = [(i, i + 1) for i in range(count - 1)]
-        backward = [(target, source) for source, target in forward]
-        low = lax.ppermute(
-            lax.slice_in_dim(block, block.shape[dim] - width, None, axis=dim), axis, forward
-        )
-        high = lax.ppermute(lax.slice_in_dim(block, 0, width, axis=dim), axis, backward)
-        block = jnp.concatenate([low, block, high], axis=dim)
-    return block
+        backward = [(i + 1, i) for i in range(count - 1)]
+        return lax.ppermute(send_high, axis, forward), lax.ppermute(send_low, axis, backward)
+    even = lax.axis_index(axis) % 2 == 0
+    inner = lax.ppermute(jnp.where(even, send_high, send_low), axis, [(i, i ^ 1) for i in range(count)])
+    outer_pairs = [p for i in range(1, count - 1, 2) for p in ((i, i + 1), (i + 1, i))]
+    outer = lax.ppermute(jnp.where(even, send_low, send_high), axis, outer_pairs)
+    return jnp.where(even, outer, inner), jnp.where(even, inner, outer)
 
 
 def pass_traces(outgoing):
@@ -26,14 +26,12 @@
     east_face = outgoing[..., face_len : 2 * face_len]
     north_face = outgoing[..., 2 * face_len : 3 * face_len]
     south_face = outgoing[..., 3 * face_len :]
-    side_send = jnp.stack([west_face[:, 0], east_face[:, -1]], axis=1)
-    side_got = with_halo(side_send, (("col", 1),), 1)
-    new_west = jnp.concatenate([side_got[:, 0][:, None], east_face[:, :-1]], axis=1)
-    new_east = jnp.concatenate([west_face[:, 1:], side_got[:, 3][:, None]], axis=1)
-    end_send = jnp.stack([north_face[0], south_face[-1]], axis=0)
-    end_got = with_halo(end_send, (("row", 0),), 1)
-    new_north = jnp.concatenate([end_got[0][None], south_face[:-1]], axis=0)
-    new_south = jnp.concatenate([north_face[1:], end_got[3][None]], axis=0)
+    west_in, east_in = neighbours(west_face[:, 0], east_face[:, -1], "col")
+    new_west = jnp.concatenate([west_in[:, None], east_face[:, :-1]], axis=1)
+    new_east = jnp.concatenate([west_face[:, 1:], east_in[:, None]], axis=1)
+    north_in, south_in = neighbours(north_face[0], south_face[-1], "row")
+    new_north = jnp.concatenate([north_in[None], south_face[:-1]], axis=0)
+    new_south = jnp.concatenate([north_face[1:], south_in[None]], axis=0)
     return jnp.concatenate([new_west, new_east, new_north, new_south], axis=-1)
 
 
@@ -167,10 +165,8 @@
         axis=-1,
     )
     parts, tagged = broadcast_parts(bank[0, 0], owner, tagged)
-    from_west = shift(tagged[:, -1], "col", 1)
-    from_east = shift(tagged[:, 0], "col", -1)
-    from_north = shift(tagged[-1], "row", 1)
-    from_south = shift(tagged[0], "row", -1)
+    from_west, from_east = neighbours(tagged[:, 0], tagged[:, -1], "col")
+    from_north, from_south = neighbours(tagged[0], tagged[-1], "row")
     row_ids = row_at * cell_rows + jnp.arange(cell_rows, dtype=jnp.int32)
     col_ids = col_at * cell_cols + jnp.arange(cell_cols, dtype=jnp.int32)
     flat_ids = (row_ids[:, None] * width + col_ids[None, :]).reshape(-1)

time: 109 us -> 108 us (level); the launches traced: 109 us -> 107 us
  waiting for transfers between devices: 39.4 us -> 31.4 us
  starting transfers between devices: 55.3 us -> 61 us
    ppermute x20, starting transfers between devices: 19.2 us -> 33.2 us  [swap(): return lax.ppermute(block, ('row', 'col'), pairs)]
    ppermute x8, starting transfers between devices: 36.1 us -> 27.7 us  [the longest x4 26.9 us: neighbours(): lax.ppermute(jnp.where(even, send_low, send_high), axis, outer_pairs)]
    ppermute x20, waiting for transfers between devices: 35.9 us -> 29.9 us  [swap(): return lax.ppermute(block, ('row', 'col'), pairs)]
    ppermute x8, waiting for transfers between devices: 3.48 us -> 1.49 us  [the longest x4 1.48 us: neighbours(): lax.ppermute(jnp.where(even, send_low, send_high), axis, outer_pairs)]
  transfers between devices with their start and end apart: 28 -> 28, of which waited for: 17 -> 15; matrix products, arithmetic and copies ran while one was open for 4% -> 4% of each run, Pallas kernels for 0% -> 0%
where the time goes in v9:
time: 108 us; the launch traced here: 107 us
  starting transfers between devices  61 us (56%)
  waiting for transfers between devices  31.4 us (29%)
  other arithmetic  8.2 us (8%)
  matrix products  4.43 us (4%)
    ppermute x20, starting transfers between devices, swap(): return lax.ppermute(block, ('row', 'col'), pairs)  33.2 us
    ppermute x20, waiting for transfers between devices, swap(): return lax.ppermute(block, ('row', 'col'), pairs)  29.9 us
    ppermute x4, starting transfers between devices, neighbours(): lax.ppermute(jnp.where(even, send_low, send_high), axis, outer_pairs)  26.9 us
    dot_general x12, matrix products, sweep(): jnp.dot(rows, part[k], preferred_element_type=jnp.float32)  4.43 us
    select_n x10, other arithmetic, scatter_gather(): jnp.where(mine, jnp.concatenate([gots[s], blocks[s]], axis=1), jnp.concat...  2.84 us
  transfers between devices with their start and end apart: 28, of which 15 were waited for; matrix products, arithmetic and copies ran while one was open for 4% of the time, Pallas kernels for 0%

profile of v9, /device:TPU:9, one launch (start us, length us, event | category | flops | bytes accessed | tf_op | source)
XLA Modules:
  0.0 106.5 jit_solution(716655173405352603)
XLA Ops:
  0.0 1.7 %broadcast_select_fusion.4 = (bf16[512,512]{1,0:T(8,128)(2,1)S(1)}, bf16[512,512]{1,0:T(8,128)(2,1)S(1)}, bf16[512,512]{1,0:T(8,128)(2,1)S(1)}, bf16[512,512]{1,0:T(8,128)(2,1)S(1)}) fusion(pred[]{:T(512)S(6)} %eq.69, bf16[1024,1024]{1,0:T(8,128)(2,1)} %bitcast.98), kind=kLoop, calls=%fused_computation.43 | loop fusion | flops 1048576 | bytes 4194305 | tf_op jit(solution)/shard_map/jit(_where)/select_n | solution.py:66
  5.2 1.4 %collective-permute-start.3 = (bf16[2,256,512]{2,1,0:T(8,128)(2,1)S(1)}, bf16[2,256,512]{2,1,0:T(8,128)(2,1)S(1)}, u32[]{:S(2)}, u32[]{:S(2)}) collective-permute-start(bf16[2,256,512]{2,1,0:T(8,128)(2,1)S(1)} %broadcast_select_fusion.2), channel_id=1, source_target_pairs={{0,16},{1,17},{2,18},{3,19},{4,20},{5,21},{6,22},{7,23},{8,9},{9,8... | collective-permute-start | bytes 1572872 | tf_op jit(solution)/shard_map/ppermute | solution.py:47
  6.8 6.6 %collective-permute-done.2 = bf16[2,256,512]{2,1,0:T(8,128)(2,1)S(1)} collective-permute-done((bf16[2,256,512]{2,1,0:T(8,128)(2,1)S(1)}, bf16[2,256,512]{2,1,0:T(8,128)(2,1)S(1)}, u32[]{:S(2)}, u32[]{:S(2)}) %collective-permute-start.2) | collective-permute-done | bytes 524320 | tf_op jit(solution)/shard_map/ppermute | solution.py:47
  13.4 5.1 %collective-permute-done.3 = bf16[2,256,512]{2,1,0:T(8,128)(2,1)S(1)} collective-permute-done((bf16[2,256,512]{2,1,0:T(8,128)(2,1)S(1)}, bf16[2,256,512]{2,1,0:T(8,128)(2,1)S(1)}, u32[]{:S(2)}, u32[]{:S(2)}) %collective-permute-start.3) | collective-permute-done | bytes 524320 | tf_op jit(solution)/shard_map/ppermute | solution.py:47
  19.6 1.8 %collective-permute-start.4 = (bf16[2,128,512]{2,1,0:T(8,128)(2,1)S(1)}, bf16[2,128,512]{2,1,0:T(8,128)(2,1)S(1)}, u32[]{:S(2)}, u32[]{:S(2)}) collective-permute-start(bf16[2,128,512]{2,1,0:T(8,128)(2,1)S(1)} %broadcast_select_fusion.9), channel_id=1, source_target_pairs={{0,2},{1,3},{2,0},{3,1},{4,6},{5,7},{6,4},{7,5},{8,24},{9,25},{10,... | collective-permute-start | bytes 786440 | tf_op jit(solution)/shard_map/ppermute | solution.py:47
  21.6 2.8 %collective-permute-done.5 = bf16[2,128,512]{2,1,0:T(8,128)(2,1)S(1)} collective-permute-done((bf16[2,128,512]{2,1,0:T(8,128)(2,1)S(1)}, bf16[2,128,512]{2,1,0:T(8,128)(2,1)S(1)}, u32[]{:S(2)}, u32[]{:S(2)}) %collective-permute-start.5) | collective-permute-done | bytes 262176 | tf_op jit(solution)/shard_map/ppermute | solution.py:47
  25.6 1.5 %collective-permute-start.7 = (bf16[2,64,512]{2,1,0:T(8,128)(2,1)S(1)}, bf16[2,64,512]{2,1,0:T(8,128)(2,1)S(1)}, u32[]{:S(2)}, u32[]{:S(2)}) collective-permute-start(bf16[2,64,512]{2,1,0:T(8,128)(2,1)S(1)} %broadcast_select_fusion.12), channel_id=1, source_target_pairs={{0,2},{1,3},{2,0},{3,1},{4,6},{5,7},{6,4},{7,5},{8,24},{9,25},{10,... | collective-permute-start | bytes 393224 | tf_op jit(solution)/shard_map/ppermute | solution.py:47
  29.6 1.5 %collective-permute-done.6 = bf16[2,64,512]{2,1,0:T(8,128)(2,1)S(1)} collective-permute-done((bf16[2,64,512]{2,1,0:T(8,128)(2,1)S(1)}, bf16[2,64,512]{2,1,0:T(8,128)(2,1)S(1)}, u32[]{:S(2)}, u32[]{:S(2)}) %collective-permute-start.6) | collective-permute-done | bytes 131104 | tf_op jit(solution)/shard_map/ppermute | solution.py:47
  31.2 2.4 %collective-permute-start.8 = (bf16[2,32,512]{2,1,0:T(8,128)(2,1)S(1)}, bf16[2,32,512]{2,1,0:T(8,128)(2,1)S(1)}, u32[]{:S(2)}, u32[]{:S(2)}) collective-permute-start(bf16[2,32,512]{2,1,0:T(8,128)(2,1)S(1)} %broadcast_select_fusion.17), channel_id=1, source_target_pairs={{0,4},{1,5},{2,6},{3,7},{4,0},{5,1},{6,2},{7,3},{8,12},{9,13},{10,... | collective-permute-start | bytes 196616 | tf_op jit(solution)/shard_map/ppermute | solution.py:47
  33.8 1.5 %collective-permute-done.8 = bf16[2,32,512]{2,1,0:T(8,128)(2,1)S(1)} collective-permute-done((bf16[2,32,512]{2,1,0:T(8,128)(2,1)S(1)}, bf16[2,32,512]{2,1,0:T(8,128)(2,1)S(1)}, u32[]{:S(2)}, u32[]{:S(2)}) %collective-permute-start.8) | collective-permute-done | bytes 65568 | tf_op jit(solution)/shard_map/ppermute | solution.py:47
  35.3 2.4 %collective-permute-done.9 = bf16[2,32,512]{2,1,0:T(8,128)(2,1)S(1)} collective-permute-done((bf16[2,32,512]{2,1,0:T(8,128)(2,1)S(1)}, bf16[2,32,512]{2,1,0:T(8,128)(2,1)S(1)}, u32[]{:S(2)}, u32[]{:S(2)}) %collective-permute-start.9) | collective-permute-done | bytes 65568 | tf_op jit(solution)/shard_map/ppermute | solution.py:47
  37.8 2.1 %collective-permute-start.15 = (bf16[2,32,512]{2,1,0:T(8,128)(2,1)S(1)}, bf16[2,32,512]{2,1,0:T(8,128)(2,1)S(1)}, u32[]{:S(2)}, u32[]{:S(2)}) collective-permute-start(bf16[2,32,512]{2,1,0:T(8,128)(2,1)S(1)} %get-tuple-element.32), channel_id=1, source_target_pairs={{0,4},{1,5},{2,6},{3,7},{4,0},{5,1},{6,2},{7,3},{8,12},{9,13},{10,... | collective-permute-start | bytes 196616 | tf_op jit(solution)/shard_map/ppermute | solution.py:47
  40.4 2.2 %collective-permute-done.15 = bf16[2,32,512]{2,1,0:T(8,128)(2,1)S(1)} collective-permute-done((bf16[2,32,512]{2,1,0:T(8,128)(2,1)S(1)}, bf16[2,32,512]{2,1,0:T(8,128)(2,1)S(1)}, u32[]{:S(2)}, u32[]{:S(2)}) %collective-permute-start.15) | collective-permute-done | bytes 65568 | tf_op jit(solution)/shard_map/ppermute | solution.py:47
  42.6 1.5 %collective-permute-done.14 = bf16[2,32,512]{2,1,0:T(8,128)(2,1)S(1)} collective-permute-done((bf16[2,32,512]{2,1,0:T(8,128)(2,1)S(1)}, bf16[2,32,512]{2,1,0:T(8,128)(2,1)S(1)}, u32[]{:S(2)}, u32[]{:S(2)}) %collective-permute-start.14) | collective-permute-done | bytes 65568 | tf_op jit(solution)/shard_map/ppermute | solution.py:47
  44.1 1.6 %collective-permute-start.16 = (bf16[2,64,512]{2,1,0:T(8,128)(2,1)S(1)}, bf16[2,64,512]{2,1,0:T(8,128)(2,1)S(1)}, u32[]{:S(2)}, u32[]{:S(2)}) collective-permute-start(bf16[2,64,512]{2,1,0:T(8,128)(2,1)S(1)} %maximum_select_fusion.8), channel_id=1, source_target_pairs={{0,16},{1,17},{2,18},{3,19},{4,20},{5,21},{6,22},{7,23},{8,9},{9,8... | collective-permute-start | bytes 393224 | tf_op jit(solution)/shard_map/ppermute | solution.py:47
  46.0 2.0 %collective-permute-done.16 = bf16[2,64,512]{2,1,0:T(8,128)(2,1)S(1)} collective-permute-done((bf16[2,64,512]{2,1,0:T(8,128)(2,1)S(1)}, bf16[2,64,512]{2,1,0:T(8,128)(2,1)S(1)}, u32[]{:S(2)}, u32[]{:S(2)}) %collective-permute-start.16) | collective-permute-done | bytes 131104 | tf_op jit(solution)/shard_map/ppermute | solution.py:47
  48.7 5.3 %collective-permute-start.10 = (bf16[2,16,1152]{2,1,0:T(8,128)(2,1)S(1)}, bf16[2,16,1152]{2,1,0:T(8,128)(2,1)S(1)}, u32[]{:S(2)}, u32[]{:S(2)}) collective-permute-start(bf16[2,16,1152]{2,1,0:T(8,128)(2,1)S(1)} %get-tuple-element.45), channel_id=1, source_target_pairs={{1,2},{2,1},{3,4},{4,3},{5,6},{6,5},{9,10},{10,9},{11,12},{12,11},... | collective-permute-start | bytes 221192 | tf_op jit(solution)/shard_map/ppermute | solution.py:19
  55.0 3.2 %collective-permute-start.18 = (bf16[2,256,512]{2,1,0:T(8,128)(2,1)S(1)}, bf16[2,256,512]{2,1,0:T(8,128)(2,1)S(1)}, u32[]{:S(2)}, u32[]{:S(2)}) collective-permute-start(bf16[2,256,512]{2,1,0:T(8,128)(2,1)S(1)} %maximum_select_fusion.4), channel_id=1, source_target_pairs={{0,1},{1,0},{2,3},{3,2},{4,5},{5,4},{6,7},{7,6},{8,10},{9,11},{10,... | collective-permute-start | bytes 1572872 | tf_op jit(solution)/shard_map/ppermute | solution.py:47
  58.2 13.4 %collective-permute-start.12 = (bf16[4,16,1152]{2,1,0:T(8,128)(2,1)S(1)}, bf16[4,16,1152]{2,1,0:T(8,128)(2,1)S(1)}, u32[]{:S(2)}, u32[]{:S(2)}) collective-permute-start(bf16[4,16,1152]{2,1,0:T(8,128)(2,1)S(1)} %get-tuple-element.49), channel_id=1, source_target_pairs={{8,16},{16,8},{9,17},{17,9},{10,18},{18,10},{11,19},{19,11},{12,20... | collective-permute-start | bytes 442376 | tf_op jit(solution)/shard_map/ppermute | solution.py:19
  72.5 8.0 %collective-permute-start.19 = (bf16[2,512,512]{2,1,0:T(8,128)(2,1)S(1)}, bf16[2,512,512]{2,1,0:T(8,128)(2,1)S(1)}, u32[]{:S(2)}, u32[]{:S(2)}) collective-permute-start(bf16[2,512,512]{2,1,0:T(8,128)(2,1)S(1)} %maximum_select_fusion.2), channel_id=1, source_target_pairs={{0,8},{1,9},{2,10},{3,11},{4,12},{5,13},{6,14},{7,15},{8,0},{9,1},... | collective-permute-start | bytes 3145736 | tf_op jit(solution)/shard_map/ppermute | solution.py:47
  81.0 6.7 %collective-permute-start.23 = (bf16[2,512,512]{2,1,0:T(8,128)(2,1)S(1)}, bf16[2,512,512]{2,1,0:T(8,128)(2,1)S(1)}, u32[]{:S(2)}, u32[]{:S(2)}) collective-permute-start(bf16[2,512,512]{2,1,0:T(8,128)(2,1)S(1)} %maximum_select_fusion.3), channel_id=1, source_target_pairs={{0,8},{1,9},{2,10},{3,11},{4,12},{5,13},{6,14},{7,15},{8,0},{9,1},... | collective-permute-start | bytes 3145736 | tf_op jit(solution)/shard_map/ppermute | solution.py:47
  94.3 4.2 %collective-permute-start.24 = (bf16[2,16,256]{2,1,0:T(8,128)(2,1)S(1)}, bf16[2,16,256]{2,1,0:T(8,128)(2,1)S(1)}, u32[]{:S(2)}, u32[]{:S(2)}) collective-permute-start(bf16[2,16,256]{2,1,0:T(8,128)(2,1)S(1)} %get-tuple-element.53), channel_id=1, source_target_pairs={{1,2},{2,1},{3,4},{4,3},{5,6},{6,5},{9,10},{10,9},{11,12},{12,11},... | collective-permute-start | bytes 49160 | tf_op jit(solution)/shard_map/ppermute | solution.py:19
  98.6 4.1 %collective-permute-start.26 = (bf16[4,16,256]{2,1,0:T(8,128)(2,1)S(1)}, bf16[4,16,256]{2,1,0:T(8,128)(2,1)S(1)}, u32[]{:S(2)}, u32[]{:S(2)}) collective-permute-start(bf16[4,16,256]{2,1,0:T(8,128)(2,1)S(1)} %get-tuple-element.56), channel_id=1, source_target_pairs={{8,16},{16,8},{9,17},{17,9},{10,18},{18,10},{11,19},{19,11},{12,20... | collective-permute-start | bytes 98312 | tf_op jit(solution)/shard_map/ppermute | solution.py:19
  102.8 1.5 %collective-permute-done.26 = bf16[4,16,256]{2,1,0:T(8,128)(2,1)S(1)} collective-permute-done((bf16[4,16,256]{2,1,0:T(8,128)(2,1)S(1)}, bf16[4,16,256]{2,1,0:T(8,128)(2,1)S(1)}, u32[]{:S(2)}, u32[]{:S(2)}) %collective-permute-start.26) | collective-permute-done | bytes 32800 | tf_op jit(solution)/shard_map/ppermute | solution.py:19
  (124 shorter events, 21.5 us)
Async XLA Ops:
  5.1 8.4 %collective-permute-start.2 = (bf16[2,256,512]{2,1,0:T(8,128)(2,1)S(1)}, bf16[2,256,512]{2,1,0:T(8,128)(2,1)S(1)}, u32[]{:S(2)}, u32[]{:S(2)}) collective-permute-start(bf16[2,256,512]{2,1,0:T(8,128)(2,1)S(1)} %broadcast_select_fusion.7), channel_id=1, source_target_pairs={{0,1},{1,0},{2,3},{3,2},{4,5},{5,4},{6,7},{7,6},{8,10},{9,11},{10,... | collective-permute-start | bytes 1572872 | tf_op jit(solution)/shard_map/ppermute | solution.py:47
  5.2 13.4 %collective-permute-start.3 = (bf16[2,256,512]{2,1,0:T(8,128)(2,1)S(1)}, bf16[2,256,512]{2,1,0:T(8,128)(2,1)S(1)}, u32[]{:S(2)}, u32[]{:S(2)}) collective-permute-start(bf16[2,256,512]{2,1,0:T(8,128)(2,1)S(1)} %broadcast_select_fusion.2), channel_id=1, source_target_pairs={{0,16},{1,17},{2,18},{3,19},{4,20},{5,21},{6,22},{7,23},{8,9},{9,8... | collective-permute-start | bytes 1572872 | tf_op jit(solution)/shard_map/ppermute | solution.py:47
  18.8 5.6 %collective-permute-start.5 = (bf16[2,128,512]{2,1,0:T(8,128)(2,1)S(1)}, bf16[2,128,512]{2,1,0:T(8,128)(2,1)S(1)}, u32[]{:S(2)}, u32[]{:S(2)}) collective-permute-start(bf16[2,128,512]{2,1,0:T(8,128)(2,1)S(1)} %broadcast_select_fusion.8), channel_id=1, source_target_pairs={{0,1},{1,0},{2,3},{3,2},{4,5},{5,4},{6,7},{7,6},{8,10},{9,11},{10,... | collective-permute-start | bytes 786440 | tf_op jit(solution)/shard_map/ppermute | solution.py:47
  19.6 5.9 %collective-permute-start.4 = (bf16[2,128,512]{2,1,0:T(8,128)(2,1)S(1)}, bf16[2,128,512]{2,1,0:T(8,128)(2,1)S(1)}, u32[]{:S(2)}, u32[]{:S(2)}) collective-permute-start(bf16[2,128,512]{2,1,0:T(8,128)(2,1)S(1)} %broadcast_select_fusion.9), channel_id=1, source_target_pairs={{0,2},{1,3},{2,0},{3,1},{4,6},{5,7},{6,4},{7,5},{8,24},{9,25},{10,... | collective-permute-start | bytes 786440 | tf_op jit(solution)/shard_map/ppermute | solution.py:47
  25.6 3.9 %collective-permute-start.7 = (bf16[2,64,512]{2,1,0:T(8,128)(2,1)S(1)}, bf16[2,64,512]{2,1,0:T(8,128)(2,1)S(1)}, u32[]{:S(2)}, u32[]{:S(2)}) collective-permute-start(bf16[2,64,512]{2,1,0:T(8,128)(2,1)S(1)} %broadcast_select_fusion.12), channel_id=1, source_target_pairs={{0,2},{1,3},{2,0},{3,1},{4,6},{5,7},{6,4},{7,5},{8,24},{9,25},{10,... | collective-permute-start | bytes 393224 | tf_op jit(solution)/shard_map/ppermute | solution.py:47
  31.2 4.1 %collective-permute-start.8 = (bf16[2,32,512]{2,1,0:T(8,128)(2,1)S(1)}, bf16[2,32,512]{2,1,0:T(8,128)(2,1)S(1)}, u32[]{:S(2)}, u32[]{:S(2)}) collective-permute-start(bf16[2,32,512]{2,1,0:T(8,128)(2,1)S(1)} %broadcast_select_fusion.17), channel_id=1, source_target_pairs={{0,4},{1,5},{2,6},{3,7},{4,0},{5,1},{6,2},{7,3},{8,12},{9,13},{10,... | collective-permute-start | bytes 196616 | tf_op jit(solution)/shard_map/ppermute | solution.py:47
  33.6 4.1 %collective-permute-start.9 = (bf16[2,32,512]{2,1,0:T(8,128)(2,1)S(1)}, bf16[2,32,512]{2,1,0:T(8,128)(2,1)S(1)}, u32[]{:S(2)}, u32[]{:S(2)}) collective-permute-start(bf16[2,32,512]{2,1,0:T(8,128)(2,1)S(1)} %broadcast_select_fusion.16), channel_id=1, source_target_pairs={{0,4},{1,5},{2,6},{3,7},{4,0},{5,1},{6,2},{7,3},{8,12},{9,13},{10,... | collective-permute-start | bytes 196616 | tf_op jit(solution)/shard_map/ppermute | solution.py:47
  37.8 4.8 %collective-permute-start.15 = (bf16[2,32,512]{2,1,0:T(8,128)(2,1)S(1)}, bf16[2,32,512]{2,1,0:T(8,128)(2,1)S(1)}, u32[]{:S(2)}, u32[]{:S(2)}) collective-permute-start(bf16[2,32,512]{2,1,0:T(8,128)(2,1)S(1)} %get-tuple-element.32), channel_id=1, source_target_pairs={{0,4},{1,5},{2,6},{3,7},{4,0},{5,1},{6,2},{7,3},{8,12},{9,13},{10,... | collective-permute-start | bytes 196616 | tf_op jit(solution)/shard_map/ppermute | solution.py:47
  40.0 4.1 %collective-permute-start.14 = (bf16[2,32,512]{2,1,0:T(8,128)(2,1)S(1)}, bf16[2,32,512]{2,1,0:T(8,128)(2,1)S(1)}, u32[]{:S(2)}, u32[]{:S(2)}) collective-permute-start(bf16[2,32,512]{2,1,0:T(8,128)(2,1)S(1)} %get-tuple-element.31), channel_id=1, source_target_pairs={{0,4},{1,5},{2,6},{3,7},{4,0},{5,1},{6,2},{7,3},{8,12},{9,13},{10,... | collective-permute-start | bytes 196616 | tf_op jit(solution)/shard_map/ppermute | solution.py:47
  44.1 3.9 %collective-permute-start.16 = (bf16[2,64,512]{2,1,0:T(8,128)(2,1)S(1)}, bf16[2,64,512]{2,1,0:T(8,128)(2,1)S(1)}, u32[]{:S(2)}, u32[]{:S(2)}) collective-permute-start(bf16[2,64,512]{2,1,0:T(8,128)(2,1)S(1)} %maximum_select_fusion.8), channel_id=1, source_target_pairs={{0,16},{1,17},{2,18},{3,19},{4,20},{5,21},{6,22},{7,23},{8,9},{9,8... | collective-permute-start | bytes 393224 | tf_op jit(solution)/shard_map/ppermute | solution.py:47
  45.7 8.9 %collective-permute-start.20 = (bf16[2,64,512]{2,1,0:T(8,128)(2,1)S(1)}, bf16[2,64,512]{2,1,0:T(8,128)(2,1)S(1)}, u32[]{:S(2)}, u32[]{:S(2)}) collective-permute-start(bf16[2,64,512]{2,1,0:T(8,128)(2,1)S(1)} %maximum_select_fusion.9), channel_id=1, source_target_pairs={{0,2},{1,3},{2,0},{3,1},{4,6},{5,7},{6,4},{7,5},{8,24},{9,25},{10,... | collective-permute-start | bytes 393224 | tf_op jit(solution)/shard_map/ppermute | solution.py:47
  48.1 6.7 %collective-permute-start.17 = (bf16[2,128,512]{2,1,0:T(8,128)(2,1)S(1)}, bf16[2,128,512]{2,1,0:T(8,128)(2,1)S(1)}, u32[]{:S(2)}, u32[]{:S(2)}) collective-permute-start(bf16[2,128,512]{2,1,0:T(8,128)(2,1)S(1)} %maximum_select_fusion.6), channel_id=1, source_target_pairs={{0,2},{1,3},{2,0},{3,1},{4,6},{5,7},{6,4},{7,5},{8,24},{9,25},{10,... | collective-permute-start | bytes 786440 | tf_op jit(solution)/shard_map/ppermute | solution.py:47
  48.7 23.7 %collective-permute-start.10 = (bf16[2,16,1152]{2,1,0:T(8,128)(2,1)S(1)}, bf16[2,16,1152]{2,1,0:T(8,128)(2,1)S(1)}, u32[]{:S(2)}, u32[]{:S(2)}) collective-permute-start(bf16[2,16,1152]{2,1,0:T(8,128)(2,1)S(1)} %get-tuple-element.45), channel_id=1, source_target_pairs={{1,2},{2,1},{3,4},{4,3},{5,6},{6,5},{9,10},{10,9},{11,12},{12,11},... | collective-permute-start | bytes 221192 | tf_op jit(solution)/shard_map/ppermute | solution.py:19
  54.0 26.5 %collective-permute-start.11 = (bf16[2,16,1152]{2,1,0:T(8,128)(2,1)S(1)}, bf16[2,16,1152]{2,1,0:T(8,128)(2,1)S(1)}, u32[]{:S(2)}, u32[]{:S(2)}) collective-permute-start(bf16[2,16,1152]{2,1,0:T(8,128)(2,1)S(1)} %get-tuple-element.46), channel_id=1, source_target_pairs={{0,1},{1,0},{2,3},{3,2},{4,5},{5,4},{6,7},{7,6},{8,9},{9,8},{10,11... | collective-permute-start | bytes 221192 | tf_op jit(solution)/shard_map/ppermute | solution.py:17
  54.7 16.9 %collective-permute-start.21 = (bf16[2,128,512]{2,1,0:T(8,128)(2,1)S(1)}, bf16[2,128,512]{2,1,0:T(8,128)(2,1)S(1)}, u32[]{:S(2)}, u32[]{:S(2)}) collective-permute-start(bf16[2,128,512]{2,1,0:T(8,128)(2,1)S(1)} %maximum_select_fusion.7), channel_id=1, source_target_pairs={{0,1},{1,0},{2,3},{3,2},{4,5},{5,4},{6,7},{7,6},{8,10},{9,11},{10,... | collective-permute-start | bytes 786440 | tf_op jit(solution)/shard_map/ppermute | solution.py:47
  55.0 16.9 %collective-permute-start.18 = (bf16[2,256,512]{2,1,0:T(8,128)(2,1)S(1)}, bf16[2,256,512]{2,1,0:T(8,128)(2,1)S(1)}, u32[]{:S(2)}, u32[]{:S(2)}) collective-permute-start(bf16[2,256,512]{2,1,0:T(8,128)(2,1)S(1)} %maximum_select_fusion.4), channel_id=1, source_target_pairs={{0,1},{1,0},{2,3},{3,2},{4,5},{5,4},{6,7},{7,6},{8,10},{9,11},{10,... | collective-permute-start | bytes 1572872 | tf_op jit(solution)/shard_map/ppermute | solution.py:47
  58.2 29.4 %collective-permute-start.12 = (bf16[4,16,1152]{2,1,0:T(8,128)(2,1)S(1)}, bf16[4,16,1152]{2,1,0:T(8,128)(2,1)S(1)}, u32[]{:S(2)}, u32[]{:S(2)}) collective-permute-start(bf16[4,16,1152]{2,1,0:T(8,128)(2,1)S(1)} %get-tuple-element.49), channel_id=1, source_target_pairs={{8,16},{16,8},{9,17},{17,9},{10,18},{18,10},{11,19},{19,11},{12,20... | collective-permute-start | bytes 442376 | tf_op jit(solution)/shard_map/ppermute | solution.py:19
  71.6 16.1 %collective-permute-start.13 = (bf16[4,16,1152]{2,1,0:T(8,128)(2,1)S(1)}, bf16[4,16,1152]{2,1,0:T(8,128)(2,1)S(1)}, u32[]{:S(2)}, u32[]{:S(2)}) collective-permute-start(bf16[4,16,1152]{2,1,0:T(8,128)(2,1)S(1)} %get-tuple-element.50), channel_id=1, source_target_pairs={{0,8},{8,0},{16,24},{24,16},{1,9},{9,1},{17,25},{25,17},{2,10},{10... | collective-permute-start | bytes 442376 | tf_op jit(solution)/shard_map/ppermute | solution.py:17
  71.9 8.6 %collective-permute-start.22 = (bf16[2,256,512]{2,1,0:T(8,128)(2,1)S(1)}, bf16[2,256,512]{2,1,0:T(8,128)(2,1)S(1)}, u32[]{:S(2)}, u32[]{:S(2)}) collective-permute-start(bf16[2,256,512]{2,1,0:T(8,128)(2,1)S(1)} %maximum_select_fusion.5), channel_id=1, source_target_pairs={{0,16},{1,17},{2,18},{3,19},{4,20},{5,21},{6,22},{7,23},{8,9},{9,8... | collective-permute-start | bytes 1572872 | tf_op jit(solution)/shard_map/ppermute | solution.py:47
  72.5 15.7 %collective-permute-start.19 = (bf16[2,512,512]{2,1,0:T(8,128)(2,1)S(1)}, bf16[2,512,512]{2,1,0:T(8,128)(2,1)S(1)}, u32[]{:S(2)}, u32[]{:S(2)}) collective-permute-start(bf16[2,512,512]{2,1,0:T(8,128)(2,1)S(1)} %maximum_select_fusion.2), channel_id=1, source_target_pairs={{0,8},{1,9},{2,10},{3,11},{4,12},{5,13},{6,14},{7,15},{8,0},{9,1},... | collective-permute-start | bytes 3145736 | tf_op jit(solution)/shard_map/ppermute | solution.py:47
  81.0 9.0 %collective-permute-start.23 = (bf16[2,512,512]{2,1,0:T(8,128)(2,1)S(1)}, bf16[2,512,512]{2,1,0:T(8,128)(2,1)S(1)}, u32[]{:S(2)}, u32[]{:S(2)}) collective-permute-start(bf16[2,512,512]{2,1,0:T(8,128)(2,1)S(1)} %maximum_select_fusion.3), channel_id=1, source_target_pairs={{0,8},{1,9},{2,10},{3,11},{4,12},{5,13},{6,14},{7,15},{8,0},{9,1},... | collective-permute-start | bytes 3145736 | tf_op jit(solution)/shard_map/ppermute | solution.py:47
  94.3 8.5 %collective-permute-start.24 = (bf16[2,16,256]{2,1,0:T(8,128)(2,1)S(1)}, bf16[2,16,256]{2,1,0:T(8,128)(2,1)S(1)}, u32[]{:S(2)}, u32[]{:S(2)}) collective-permute-start(bf16[2,16,256]{2,1,0:T(8,128)(2,1)S(1)} %get-tuple-element.53), channel_id=1, source_target_pairs={{1,2},{2,1},{3,4},{4,3},{5,6},{6,5},{9,10},{10,9},{11,12},{12,11},... | collective-permute-start | bytes 49160 | tf_op jit(solution)/shard_map/ppermute | solution.py:19
  98.5 4.3 %collective-permute-start.25 = (bf16[2,16,256]{2,1,0:T(8,128)(2,1)S(1)}, bf16[2,16,256]{2,1,0:T(8,128)(2,1)S(1)}, u32[]{:S(2)}, u32[]{:S(2)}) collective-permute-start(bf16[2,16,256]{2,1,0:T(8,128)(2,1)S(1)} %get-tuple-element.54), channel_id=1, source_target_pairs={{0,1},{1,0},{2,3},{3,2},{4,5},{5,4},{6,7},{7,6},{8,9},{9,8},{10,11... | collective-permute-start | bytes 49160 | tf_op jit(solution)/shard_map/ppermute | solution.py:17
  98.6 5.7 %collective-permute-start.26 = (bf16[4,16,256]{2,1,0:T(8,128)(2,1)S(1)}, bf16[4,16,256]{2,1,0:T(8,128)(2,1)S(1)}, u32[]{:S(2)}, u32[]{:S(2)}) collective-permute-start(bf16[4,16,256]{2,1,0:T(8,128)(2,1)S(1)} %get-tuple-element.56), channel_id=1, source_target_pairs={{8,16},{16,8},{9,17},{17,9},{10,18},{18,10},{11,19},{19,11},{12,20... | collective-permute-start | bytes 98312 | tf_op jit(solution)/shard_map/ppermute | solution.py:19
  (9 other events, 27.0 us)

commit v10 on v9

--- a/solution.py
+++ b/solution.py
@@ -63,19 +63,21 @@
             mine = ((me >> pick(bits)) & 1) == 1
             if step == 0:
                 half = block.shape[0] // 2
-                keep = jnp.where(mine, block[half:], block[:half])[None]
+                keep = jnp.where(mine, block[half:], block[:half])
+                keep = jnp.concatenate([keep] * TYPES, axis=1)
                 give = jnp.where(mine, block[:half], block[half:])
             else:
-                half = block.shape[1] // 2
-                keep = jnp.where(mine, block[:, half:], block[:, :half])
-                give = jnp.where(mine, block[:, :half], block[:, half:])
+                half = block.shape[0] // 2
+                keep = jnp.where(mine, block[half:], block[:half])
+                give = jnp.where(mine, block[:half], block[half:])
             got = swap(give, bits, core)
             keeps.append(keep)
-            gots.append(got[None] if step == 0 else got)
+            gots.append(jnp.concatenate([got] * TYPES, axis=1) if step == 0 else got)
         for s in range(len(blocks)):
             outside = pick([full & ~done_mask[s][0], full & ~done_mask[s][1]])
             have = ((me ^ owner) & outside) == 0
-            blocks[s] = jnp.where(have[:, None, None], keeps[s], gots[s])
+            lanes = jnp.repeat(have, keeps[s].shape[1] // TYPES)
+            blocks[s] = jnp.where(lanes[None, :], keeps[s], gots[s])
             for c in range(2):
                 done_mask[s][c] |= 1 << orders[s][c][step]
         blocks = list(lax.optimization_barrier(tuple(blocks)))
@@ -88,7 +90,7 @@
         for s in range(len(blocks)):
             mine = ((me >> pick((orders[s][0][step], orders[s][1][step]))) & 1) == 1
             blocks[s] = jnp.where(
-                mine, jnp.concatenate([gots[s], blocks[s]], axis=1), jnp.concatenate([blocks[s], gots[s]], axis=1)
+                mine, jnp.concatenate([gots[s], blocks[s]], axis=0), jnp.concatenate([blocks[s], gots[s]], axis=0)
             )
         if step == stages - 1:
             blocks = list(lax.optimization_barrier(tuple(blocks)))
@@ -103,7 +105,8 @@
     order_len = None if col_bits is None or row_bits is None else col_bits + row_bits
     if order_len is None or row_bits < 1 or col_bits < 1 or (own_operator.shape[0] >> order_len) < 8:
         mask = (me == owner)[:, None, None]
-        return [lax.psum(jnp.where(mask, stacked, jnp.zeros_like(stacked)), ("row", "col"))], tie
+        summed = lax.psum(jnp.where(mask, stacked, jnp.zeros_like(stacked)), ("row", "col"))
+        return [jnp.concatenate([summed[k] for k in range(TYPES)], axis=1)], tie
     core = col_bits
     middle = list(range(col_bits - 1)) + list(range(col_bits + 1, col_bits + row_bits))
     last = [col_bits - 1]
@@ -129,9 +132,10 @@
 def sweep(traces, kinds, ids, parts, port_cell, excite):
     count, port_count, order = traces.shape
     rows = traces.reshape(count * port_count, order)
+    both = [jnp.dot(rows, part, preferred_element_type=jnp.float32) for part in parts]
     products = [
         jnp.concatenate(
-            [jnp.dot(rows, part[k], preferred_element_type=jnp.float32) for part in parts], axis=-1
+            [prod[:, k * (prod.shape[1] // TYPES) : (k + 1) * (prod.shape[1] // TYPES)] for prod in both], axis=-1
         ).reshape(count, port_count, order)
         for k in range(TYPES)
     ]

time: 108 us -> 108 us (level)
    dot_general x12 -> x6, matrix products: 4.43 us -> 3.49 us  [sweep(): jnp.dot(rows, part, preferred_element_type=jnp.float32)]
  transfers between devices with their start and end apart: 28 -> 28, of which waited for: 15 -> 15; matrix products, arithmetic and copies ran while one was open for 4% -> 5% of each run, Pallas kernels for 0% -> 0%
where the time goes in v10:
time: 108 us; the launch traced here: 106 us
  starting transfers between devices  60.7 us (56%)
  waiting for transfers between devices  30.8 us (29%)
  other arithmetic  8.77 us (8%)
  matrix products  3.49 us (3%)
  local copies, waits for them, and re-layouts  2.02 us (2%)
    ppermute x20, starting transfers between devices, swap(): return lax.ppermute(block, ('row', 'col'), pairs)  33 us
    ppermute x20, waiting for transfers between devices, swap(): return lax.ppermute(block, ('row', 'col'), pairs)  29.3 us
    ppermute x4, starting transfers between devices, neighbours(): lax.ppermute(jnp.where(even, send_low, send_high), axis, outer_pairs)  26.9 us
    dot_general x6, matrix products, sweep(): jnp.dot(rows, part, preferred_element_type=jnp.float32)  3.49 us
    select_n x10, other arithmetic, scatter_gather(): jnp.where(mine, jnp.concatenate([gots[s], blocks[s]], axis=0), jnp.concat...  3.37 us
  transfers between devices with their start and end apart: 28, of which 15 were waited for; matrix products, arithmetic and copies ran while one was open for 5% of the time, Pallas kernels for 0%

profile of v10, /device:TPU:9, one launch (start us, length us, event | category | flops | bytes accessed | tf_op | source)
XLA Modules:
  0.0 106.5 jit_solution(3499821348009563341)
XLA Ops:
  0.0 1.7 %broadcast_select_fusion.1 = (bf16[512,512]{1,0:T(8,128)(2,1)S(1)}, bf16[512,512]{1,0:T(8,128)(2,1)S(1)}, bf16[512,512]{1,0:T(8,128)(2,1)S(1)}, bf16[512,512]{1,0:T(8,128)(2,1)S(1)}) fusion(pred[]{:T(512)S(6)} %eq.69, bf16[1024,1024]{1,0:T(8,128)(2,1)} %bitcast.82), kind=kLoop, calls=%fused_computation.26 | loop fusion | flops 1048576 | bytes 4194305 | tf_op jit(solution)/shard_map/jit(_where)/select_n | solution.py:68
  5.6 1.4 %collective-permute-start.3 = (bf16[256,1024]{1,0:T(8,128)(2,1)S(1)}, bf16[256,1024]{1,0:T(8,128)(2,1)S(1)}, u32[]{:S(2)}, u32[]{:S(2)}) collective-permute-start(bf16[256,1024]{1,0:T(8,128)(2,1)S(1)} %broadcast_select_fusion), channel_id=1, source_target_pairs={{0,16},{1,17},{2,18},{3,19},{4,20},{5,21},{6,22},{7,23},{8,9},{9,8... | collective-permute-start | bytes 1572872 | tf_op jit(solution)/shard_map/ppermute | solution.py:47
  7.2 6.6 %collective-permute-done.2 = bf16[256,1024]{1,0:T(8,128)(2,1)S(1)} collective-permute-done((bf16[256,1024]{1,0:T(8,128)(2,1)S(1)}, bf16[256,1024]{1,0:T(8,128)(2,1)S(1)}, u32[]{:S(2)}, u32[]{:S(2)}) %collective-permute-start.2) | collective-permute-done | bytes 524320 | tf_op jit(solution)/shard_map/ppermute | solution.py:47
  13.8 5.1 %collective-permute-done.3 = bf16[256,1024]{1,0:T(8,128)(2,1)S(1)} collective-permute-done((bf16[256,1024]{1,0:T(8,128)(2,1)S(1)}, bf16[256,1024]{1,0:T(8,128)(2,1)S(1)}, u32[]{:S(2)}, u32[]{:S(2)}) %collective-permute-start.3) | collective-permute-done | bytes 524320 | tf_op jit(solution)/shard_map/ppermute | solution.py:47
  20.0 1.8 %collective-permute-start.4 = (bf16[128,1024]{1,0:T(8,128)(2,1)S(1)}, bf16[128,1024]{1,0:T(8,128)(2,1)S(1)}, u32[]{:S(2)}, u32[]{:S(2)}) collective-permute-start(bf16[128,1024]{1,0:T(8,128)(2,1)S(1)} %broadcast_select_fusion.7), channel_id=1, source_target_pairs={{0,2},{1,3},{2,0},{3,1},{4,6},{5,7},{6,4},{7,5},{8,24},{9,25},{10,... | collective-permute-start | bytes 786440 | tf_op jit(solution)/shard_map/ppermute | solution.py:47
  22.4 2.4 %collective-permute-done.5 = bf16[128,1024]{1,0:T(8,128)(2,1)S(1)} collective-permute-done((bf16[128,1024]{1,0:T(8,128)(2,1)S(1)}, bf16[128,1024]{1,0:T(8,128)(2,1)S(1)}, u32[]{:S(2)}, u32[]{:S(2)}) %collective-permute-start.5) | collective-permute-done | bytes 262176 | tf_op jit(solution)/shard_map/ppermute | solution.py:47
  25.9 1.5 %collective-permute-start.7 = (bf16[64,1024]{1,0:T(8,128)(2,1)S(1)}, bf16[64,1024]{1,0:T(8,128)(2,1)S(1)}, u32[]{:S(2)}, u32[]{:S(2)}) collective-permute-start(bf16[64,1024]{1,0:T(8,128)(2,1)S(1)} %broadcast_select_fusion.10), channel_id=1, source_target_pairs={{0,2},{1,3},{2,0},{3,1},{4,6},{5,7},{6,4},{7,5},{8,24},{9,25},{10,... | collective-permute-start | bytes 393224 | tf_op jit(solution)/shard_map/ppermute | solution.py:47
  29.9 1.5 %collective-permute-done.6 = bf16[64,1024]{1,0:T(8,128)(2,1)S(1)} collective-permute-done((bf16[64,1024]{1,0:T(8,128)(2,1)S(1)}, bf16[64,1024]{1,0:T(8,128)(2,1)S(1)}, u32[]{:S(2)}, u32[]{:S(2)}) %collective-permute-start.6) | collective-permute-done | bytes 131104 | tf_op jit(solution)/shard_map/ppermute | solution.py:47
  31.4 2.4 %collective-permute-start.8 = (bf16[32,1024]{1,0:T(8,128)(2,1)S(1)}, bf16[32,1024]{1,0:T(8,128)(2,1)S(1)}, u32[]{:S(2)}, u32[]{:S(2)}) collective-permute-start(bf16[32,1024]{1,0:T(8,128)(2,1)S(1)} %broadcast_select_fusion.15), channel_id=1, source_target_pairs={{0,4},{1,5},{2,6},{3,7},{4,0},{5,1},{6,2},{7,3},{8,12},{9,13},{10,... | collective-permute-start | bytes 196616 | tf_op jit(solution)/shard_map/ppermute | solution.py:47
  34.1 1.4 %collective-permute-done.8 = bf16[32,1024]{1,0:T(8,128)(2,1)S(1)} collective-permute-done((bf16[32,1024]{1,0:T(8,128)(2,1)S(1)}, bf16[32,1024]{1,0:T(8,128)(2,1)S(1)}, u32[]{:S(2)}, u32[]{:S(2)}) %collective-permute-start.8) | collective-permute-done | bytes 65568 | tf_op jit(solution)/shard_map/ppermute | solution.py:47
  35.5 2.4 %collective-permute-done.9 = bf16[32,1024]{1,0:T(8,128)(2,1)S(1)} collective-permute-done((bf16[32,1024]{1,0:T(8,128)(2,1)S(1)}, bf16[32,1024]{1,0:T(8,128)(2,1)S(1)}, u32[]{:S(2)}, u32[]{:S(2)}) %collective-permute-start.9) | collective-permute-done | bytes 65568 | tf_op jit(solution)/shard_map/ppermute | solution.py:47
  37.9 2.1 %collective-permute-start.15 = (bf16[32,1024]{1,0:T(8,128)(2,1)S(1)}, bf16[32,1024]{1,0:T(8,128)(2,1)S(1)}, u32[]{:S(2)}, u32[]{:S(2)}) collective-permute-start(bf16[32,1024]{1,0:T(8,128)(2,1)S(1)} %get-tuple-element.32), channel_id=1, source_target_pairs={{0,4},{1,5},{2,6},{3,7},{4,0},{5,1},{6,2},{7,3},{8,12},{9,13},{10,... | collective-permute-start | bytes 196616 | tf_op jit(solution)/shard_map/ppermute | solution.py:47
  40.6 2.3 %collective-permute-done.15 = bf16[32,1024]{1,0:T(8,128)(2,1)S(1)} collective-permute-done((bf16[32,1024]{1,0:T(8,128)(2,1)S(1)}, bf16[32,1024]{1,0:T(8,128)(2,1)S(1)}, u32[]{:S(2)}, u32[]{:S(2)}) %collective-permute-start.15) | collective-permute-done | bytes 65568 | tf_op jit(solution)/shard_map/ppermute | solution.py:47
  42.9 1.4 %collective-permute-done.14 = bf16[32,1024]{1,0:T(8,128)(2,1)S(1)} collective-permute-done((bf16[32,1024]{1,0:T(8,128)(2,1)S(1)}, bf16[32,1024]{1,0:T(8,128)(2,1)S(1)}, u32[]{:S(2)}, u32[]{:S(2)}) %collective-permute-start.14) | collective-permute-done | bytes 65568 | tf_op jit(solution)/shard_map/ppermute | solution.py:47
  44.3 1.6 %collective-permute-start.16 = (bf16[64,1024]{1,0:T(8,128)(2,1)S(1)}, bf16[64,1024]{1,0:T(8,128)(2,1)S(1)}, u32[]{:S(2)}, u32[]{:S(2)}) collective-permute-start(bf16[64,1024]{1,0:T(8,128)(2,1)S(1)} %maximum_select_fusion.10), channel_id=1, source_target_pairs={{0,16},{1,17},{2,18},{3,19},{4,20},{5,21},{6,22},{7,23},{8,9},{9,8... | collective-permute-start | bytes 393224 | tf_op jit(solution)/shard_map/ppermute | solution.py:47
  46.2 2.0 %collective-permute-done.16 = bf16[64,1024]{1,0:T(8,128)(2,1)S(1)} collective-permute-done((bf16[64,1024]{1,0:T(8,128)(2,1)S(1)}, bf16[64,1024]{1,0:T(8,128)(2,1)S(1)}, u32[]{:S(2)}, u32[]{:S(2)}) %collective-permute-start.16) | collective-permute-done | bytes 131104 | tf_op jit(solution)/shard_map/ppermute | solution.py:47
  49.0 5.3 %collective-permute-start.10 = (bf16[2,16,1152]{2,1,0:T(8,128)(2,1)S(1)}, bf16[2,16,1152]{2,1,0:T(8,128)(2,1)S(1)}, u32[]{:S(2)}, u32[]{:S(2)}) collective-permute-start(bf16[2,16,1152]{2,1,0:T(8,128)(2,1)S(1)} %get-tuple-element.57), channel_id=1, source_target_pairs={{1,2},{2,1},{3,4},{4,3},{5,6},{6,5},{9,10},{10,9},{11,12},{12,11},... | collective-permute-start | bytes 221192 | tf_op jit(solution)/shard_map/ppermute | solution.py:19
  55.0 3.2 %collective-permute-start.18 = (bf16[256,1024]{1,0:T(8,128)(2,1)S(1)}, bf16[256,1024]{1,0:T(8,128)(2,1)S(1)}, u32[]{:S(2)}, u32[]{:S(2)}) collective-permute-start(bf16[256,1024]{1,0:T(8,128)(2,1)S(1)} %maximum_select_fusion.6), channel_id=1, source_target_pairs={{0,1},{1,0},{2,3},{3,2},{4,5},{5,4},{6,7},{7,6},{8,10},{9,11},{10,... | collective-permute-start | bytes 1572872 | tf_op jit(solution)/shard_map/ppermute | solution.py:47
  58.3 13.4 %collective-permute-start.12 = (bf16[4,16,1152]{2,1,0:T(8,128)(2,1)S(1)}, bf16[4,16,1152]{2,1,0:T(8,128)(2,1)S(1)}, u32[]{:S(2)}, u32[]{:S(2)}) collective-permute-start(bf16[4,16,1152]{2,1,0:T(8,128)(2,1)S(1)} %get-tuple-element.61), channel_id=1, source_target_pairs={{8,16},{16,8},{9,17},{17,9},{10,18},{18,10},{11,19},{19,11},{12,20... | collective-permute-start | bytes 442376 | tf_op jit(solution)/shard_map/ppermute | solution.py:19
  72.6 8.1 %collective-permute-start.19 = (bf16[512,1024]{1,0:T(8,128)(2,1)S(1)}, bf16[512,1024]{1,0:T(8,128)(2,1)S(1)}, u32[]{:S(2)}, u32[]{:S(2)}) collective-permute-start(bf16[512,1024]{1,0:T(8,128)(2,1)S(1)} %maximum_select_fusion.4), channel_id=1, source_target_pairs={{0,8},{1,9},{2,10},{3,11},{4,12},{5,13},{6,14},{7,15},{8,0},{9,1},... | collective-permute-start | bytes 3145736 | tf_op jit(solution)/shard_map/ppermute | solution.py:47
  81.5 6.2 %collective-permute-start.23 = (bf16[512,1024]{1,0:T(8,128)(2,1)S(1)}, bf16[512,1024]{1,0:T(8,128)(2,1)S(1)}, u32[]{:S(2)}, u32[]{:S(2)}) collective-permute-start(bf16[512,1024]{1,0:T(8,128)(2,1)S(1)} %maximum_select_fusion.5), channel_id=1, source_target_pairs={{0,8},{1,9},{2,10},{3,11},{4,12},{5,13},{6,14},{7,15},{8,0},{9,1},... | collective-permute-start | bytes 3145736 | tf_op jit(solution)/shard_map/ppermute | solution.py:47
  94.5 4.4 %collective-permute-start.24 = (bf16[2,16,256]{2,1,0:T(8,128)(2,1)S(1)}, bf16[2,16,256]{2,1,0:T(8,128)(2,1)S(1)}, u32[]{:S(2)}, u32[]{:S(2)}) collective-permute-start(bf16[2,16,256]{2,1,0:T(8,128)(2,1)S(1)} %get-tuple-element.65), channel_id=1, source_target_pairs={{1,2},{2,1},{3,4},{4,3},{5,6},{6,5},{9,10},{10,9},{11,12},{12,11},... | collective-permute-start | bytes 49160 | tf_op jit(solution)/shard_map/ppermute | solution.py:19
  99.0 3.9 %collective-permute-start.26 = (bf16[4,16,256]{2,1,0:T(8,128)(2,1)S(1)}, bf16[4,16,256]{2,1,0:T(8,128)(2,1)S(1)}, u32[]{:S(2)}, u32[]{:S(2)}) collective-permute-start(bf16[4,16,256]{2,1,0:T(8,128)(2,1)S(1)} %get-tuple-element.68), channel_id=1, source_target_pairs={{8,16},{16,8},{9,17},{17,9},{10,18},{18,10},{11,19},{19,11},{12,20... | collective-permute-start | bytes 98312 | tf_op jit(solution)/shard_map/ppermute | solution.py:19
  103.0 1.5 %collective-permute-done.26 = bf16[4,16,256]{2,1,0:T(8,128)(2,1)S(1)} collective-permute-done((bf16[4,16,256]{2,1,0:T(8,128)(2,1)S(1)}, bf16[4,16,256]{2,1,0:T(8,128)(2,1)S(1)}, u32[]{:S(2)}, u32[]{:S(2)}) %collective-permute-start.26) | collective-permute-done | bytes 32800 | tf_op jit(solution)/shard_map/ppermute | solution.py:19
  (137 shorter events, 22.2 us)
Async XLA Ops:
  5.5 8.4 %collective-permute-start.2 = (bf16[256,1024]{1,0:T(8,128)(2,1)S(1)}, bf16[256,1024]{1,0:T(8,128)(2,1)S(1)}, u32[]{:S(2)}, u32[]{:S(2)}) collective-permute-start(bf16[256,1024]{1,0:T(8,128)(2,1)S(1)} %broadcast_select_fusion.5), channel_id=1, source_target_pairs={{0,1},{1,0},{2,3},{3,2},{4,5},{5,4},{6,7},{7,6},{8,10},{9,11},{10,... | collective-permute-start | bytes 1572872 | tf_op jit(solution)/shard_map/ppermute | solution.py:47
  5.6 13.4 %collective-permute-start.3 = (bf16[256,1024]{1,0:T(8,128)(2,1)S(1)}, bf16[256,1024]{1,0:T(8,128)(2,1)S(1)}, u32[]{:S(2)}, u32[]{:S(2)}) collective-permute-start(bf16[256,1024]{1,0:T(8,128)(2,1)S(1)} %broadcast_select_fusion), channel_id=1, source_target_pairs={{0,16},{1,17},{2,18},{3,19},{4,20},{5,21},{6,22},{7,23},{8,9},{9,8... | collective-permute-start | bytes 1572872 | tf_op jit(solution)/shard_map/ppermute | solution.py:47
  19.2 5.6 %collective-permute-start.5 = (bf16[128,1024]{1,0:T(8,128)(2,1)S(1)}, bf16[128,1024]{1,0:T(8,128)(2,1)S(1)}, u32[]{:S(2)}, u32[]{:S(2)}) collective-permute-start(bf16[128,1024]{1,0:T(8,128)(2,1)S(1)} %broadcast_select_fusion.6), channel_id=1, source_target_pairs={{0,1},{1,0},{2,3},{3,2},{4,5},{5,4},{6,7},{7,6},{8,10},{9,11},{10,... | collective-permute-start | bytes 786440 | tf_op jit(solution)/shard_map/ppermute | solution.py:47
  20.0 5.9 %collective-permute-start.4 = (bf16[128,1024]{1,0:T(8,128)(2,1)S(1)}, bf16[128,1024]{1,0:T(8,128)(2,1)S(1)}, u32[]{:S(2)}, u32[]{:S(2)}) collective-permute-start(bf16[128,1024]{1,0:T(8,128)(2,1)S(1)} %broadcast_select_fusion.7), channel_id=1, source_target_pairs={{0,2},{1,3},{2,0},{3,1},{4,6},{5,7},{6,4},{7,5},{8,24},{9,25},{10,... | collective-permute-start | bytes 786440 | tf_op jit(solution)/shard_map/ppermute | solution.py:47
  25.9 3.9 %collective-permute-start.7 = (bf16[64,1024]{1,0:T(8,128)(2,1)S(1)}, bf16[64,1024]{1,0:T(8,128)(2,1)S(1)}, u32[]{:S(2)}, u32[]{:S(2)}) collective-permute-start(bf16[64,1024]{1,0:T(8,128)(2,1)S(1)} %broadcast_select_fusion.10), channel_id=1, source_target_pairs={{0,2},{1,3},{2,0},{3,1},{4,6},{5,7},{6,4},{7,5},{8,24},{9,25},{10,... | collective-permute-start | bytes 393224 | tf_op jit(solution)/shard_map/ppermute | solution.py:47
  31.4 4.1 %collective-permute-start.8 = (bf16[32,1024]{1,0:T(8,128)(2,1)S(1)}, bf16[32,1024]{1,0:T(8,128)(2,1)S(1)}, u32[]{:S(2)}, u32[]{:S(2)}) collective-permute-start(bf16[32,1024]{1,0:T(8,128)(2,1)S(1)} %broadcast_select_fusion.15), channel_id=1, source_target_pairs={{0,4},{1,5},{2,6},{3,7},{4,0},{5,1},{6,2},{7,3},{8,12},{9,13},{10,... | collective-permute-start | bytes 196616 | tf_op jit(solution)/shard_map/ppermute | solution.py:47
  33.8 4.1 %collective-permute-start.9 = (bf16[32,1024]{1,0:T(8,128)(2,1)S(1)}, bf16[32,1024]{1,0:T(8,128)(2,1)S(1)}, u32[]{:S(2)}, u32[]{:S(2)}) collective-permute-start(bf16[32,1024]{1,0:T(8,128)(2,1)S(1)} %broadcast_select_fusion.14), channel_id=1, source_target_pairs={{0,4},{1,5},{2,6},{3,7},{4,0},{5,1},{6,2},{7,3},{8,12},{9,13},{10,... | collective-permute-start | bytes 196616 | tf_op jit(solution)/shard_map/ppermute | solution.py:47
  37.9 4.9 %collective-permute-start.15 = (bf16[32,1024]{1,0:T(8,128)(2,1)S(1)}, bf16[32,1024]{1,0:T(8,128)(2,1)S(1)}, u32[]{:S(2)}, u32[]{:S(2)}) collective-permute-start(bf16[32,1024]{1,0:T(8,128)(2,1)S(1)} %get-tuple-element.32), channel_id=1, source_target_pairs={{0,4},{1,5},{2,6},{3,7},{4,0},{5,1},{6,2},{7,3},{8,12},{9,13},{10,... | collective-permute-start | bytes 196616 | tf_op jit(solution)/shard_map/ppermute | solution.py:47
  40.2 4.1 %collective-permute-start.14 = (bf16[32,1024]{1,0:T(8,128)(2,1)S(1)}, bf16[32,1024]{1,0:T(8,128)(2,1)S(1)}, u32[]{:S(2)}, u32[]{:S(2)}) collective-permute-start(bf16[32,1024]{1,0:T(8,128)(2,1)S(1)} %get-tuple-element.31), channel_id=1, source_target_pairs={{0,4},{1,5},{2,6},{3,7},{4,0},{5,1},{6,2},{7,3},{8,12},{9,13},{10,... | collective-permute-start | bytes 196616 | tf_op jit(solution)/shard_map/ppermute | solution.py:47
  44.3 3.9 %collective-permute-start.16 = (bf16[64,1024]{1,0:T(8,128)(2,1)S(1)}, bf16[64,1024]{1,0:T(8,128)(2,1)S(1)}, u32[]{:S(2)}, u32[]{:S(2)}) collective-permute-start(bf16[64,1024]{1,0:T(8,128)(2,1)S(1)} %maximum_select_fusion.10), channel_id=1, source_target_pairs={{0,16},{1,17},{2,18},{3,19},{4,20},{5,21},{6,22},{7,23},{8,9},{9,8... | collective-permute-start | bytes 393224 | tf_op jit(solution)/shard_map/ppermute | solution.py:47
  45.9 8.9 %collective-permute-start.20 = (bf16[64,1024]{1,0:T(8,128)(2,1)S(1)}, bf16[64,1024]{1,0:T(8,128)(2,1)S(1)}, u32[]{:S(2)}, u32[]{:S(2)}) collective-permute-start(bf16[64,1024]{1,0:T(8,128)(2,1)S(1)} %maximum_select_fusion.11), channel_id=1, source_target_pairs={{0,2},{1,3},{2,0},{3,1},{4,6},{5,7},{6,4},{7,5},{8,24},{9,25},{10,... | collective-permute-start | bytes 393224 | tf_op jit(solution)/shard_map/ppermute | solution.py:47
  48.3 6.6 %collective-permute-start.17 = (bf16[128,1024]{1,0:T(8,128)(2,1)S(1)}, bf16[128,1024]{1,0:T(8,128)(2,1)S(1)}, u32[]{:S(2)}, u32[]{:S(2)}) collective-permute-start(bf16[128,1024]{1,0:T(8,128)(2,1)S(1)} %maximum_select_fusion.8), channel_id=1, source_target_pairs={{0,2},{1,3},{2,0},{3,1},{4,6},{5,7},{6,4},{7,5},{8,24},{9,25},{10,... | collective-permute-start | bytes 786440 | tf_op jit(solution)/shard_map/ppermute | solution.py:47
  49.0 23.6 %collective-permute-start.10 = (bf16[2,16,1152]{2,1,0:T(8,128)(2,1)S(1)}, bf16[2,16,1152]{2,1,0:T(8,128)(2,1)S(1)}, u32[]{:S(2)}, u32[]{:S(2)}) collective-permute-start(bf16[2,16,1152]{2,1,0:T(8,128)(2,1)S(1)} %get-tuple-element.57), channel_id=1, source_target_pairs={{1,2},{2,1},{3,4},{4,3},{5,6},{6,5},{9,10},{10,9},{11,12},{12,11},... | collective-permute-start | bytes 221192 | tf_op jit(solution)/shard_map/ppermute | solution.py:19
  54.3 26.4 %collective-permute-start.11 = (bf16[2,16,1152]{2,1,0:T(8,128)(2,1)S(1)}, bf16[2,16,1152]{2,1,0:T(8,128)(2,1)S(1)}, u32[]{:S(2)}, u32[]{:S(2)}) collective-permute-start(bf16[2,16,1152]{2,1,0:T(8,128)(2,1)S(1)} %get-tuple-element.58), channel_id=1, source_target_pairs={{0,1},{1,0},{2,3},{3,2},{4,5},{5,4},{6,7},{7,6},{8,9},{9,8},{10,11... | collective-permute-start | bytes 221192 | tf_op jit(solution)/shard_map/ppermute | solution.py:17
  54.8 16.9 %collective-permute-start.21 = (bf16[128,1024]{1,0:T(8,128)(2,1)S(1)}, bf16[128,1024]{1,0:T(8,128)(2,1)S(1)}, u32[]{:S(2)}, u32[]{:S(2)}) collective-permute-start(bf16[128,1024]{1,0:T(8,128)(2,1)S(1)} %maximum_select_fusion.9), channel_id=1, source_target_pairs={{0,1},{1,0},{2,3},{3,2},{4,5},{5,4},{6,7},{7,6},{8,10},{9,11},{10,... | collective-permute-start | bytes 786440 | tf_op jit(solution)/shard_map/ppermute | solution.py:47
  55.0 16.9 %collective-permute-start.18 = (bf16[256,1024]{1,0:T(8,128)(2,1)S(1)}, bf16[256,1024]{1,0:T(8,128)(2,1)S(1)}, u32[]{:S(2)}, u32[]{:S(2)}) collective-permute-start(bf16[256,1024]{1,0:T(8,128)(2,1)S(1)} %maximum_select_fusion.6), channel_id=1, source_target_pairs={{0,1},{1,0},{2,3},{3,2},{4,5},{5,4},{6,7},{7,6},{8,10},{9,11},{10,... | collective-permute-start | bytes 1572872 | tf_op jit(solution)/shard_map/ppermute | solution.py:47
  58.3 22.4 %collective-permute-start.12 = (bf16[4,16,1152]{2,1,0:T(8,128)(2,1)S(1)}, bf16[4,16,1152]{2,1,0:T(8,128)(2,1)S(1)}, u32[]{:S(2)}, u32[]{:S(2)}) collective-permute-start(bf16[4,16,1152]{2,1,0:T(8,128)(2,1)S(1)} %get-tuple-element.61), channel_id=1, source_target_pairs={{8,16},{16,8},{9,17},{17,9},{10,18},{18,10},{11,19},{19,11},{12,20... | collective-permute-start | bytes 442376 | tf_op jit(solution)/shard_map/ppermute | solution.py:19
  71.7 9.0 %collective-permute-start.13 = (bf16[4,16,1152]{2,1,0:T(8,128)(2,1)S(1)}, bf16[4,16,1152]{2,1,0:T(8,128)(2,1)S(1)}, u32[]{:S(2)}, u32[]{:S(2)}) collective-permute-start(bf16[4,16,1152]{2,1,0:T(8,128)(2,1)S(1)} %get-tuple-element.62), channel_id=1, source_target_pairs={{0,8},{8,0},{16,24},{24,16},{1,9},{9,1},{17,25},{25,17},{2,10},{10... | collective-permute-start | bytes 442376 | tf_op jit(solution)/shard_map/ppermute | solution.py:17
  71.9 9.1 %collective-permute-start.22 = (bf16[256,1024]{1,0:T(8,128)(2,1)S(1)}, bf16[256,1024]{1,0:T(8,128)(2,1)S(1)}, u32[]{:S(2)}, u32[]{:S(2)}) collective-permute-start(bf16[256,1024]{1,0:T(8,128)(2,1)S(1)} %maximum_select_fusion.7), channel_id=1, source_target_pairs={{0,16},{1,17},{2,18},{3,19},{4,20},{5,21},{6,22},{7,23},{8,9},{9,8... | collective-permute-start | bytes 1572872 | tf_op jit(solution)/shard_map/ppermute | solution.py:47
  72.6 15.4 %collective-permute-start.19 = (bf16[512,1024]{1,0:T(8,128)(2,1)S(1)}, bf16[512,1024]{1,0:T(8,128)(2,1)S(1)}, u32[]{:S(2)}, u32[]{:S(2)}) collective-permute-start(bf16[512,1024]{1,0:T(8,128)(2,1)S(1)} %maximum_select_fusion.4), channel_id=1, source_target_pairs={{0,8},{1,9},{2,10},{3,11},{4,12},{5,13},{6,14},{7,15},{8,0},{9,1},... | collective-permute-start | bytes 3145736 | tf_op jit(solution)/shard_map/ppermute | solution.py:47
  81.5 8.5 %collective-permute-start.23 = (bf16[512,1024]{1,0:T(8,128)(2,1)S(1)}, bf16[512,1024]{1,0:T(8,128)(2,1)S(1)}, u32[]{:S(2)}, u32[]{:S(2)}) collective-permute-start(bf16[512,1024]{1,0:T(8,128)(2,1)S(1)} %maximum_select_fusion.5), channel_id=1, source_target_pairs={{0,8},{1,9},{2,10},{3,11},{4,12},{5,13},{6,14},{7,15},{8,0},{9,1},... | collective-permute-start | bytes 3145736 | tf_op jit(solution)/shard_map/ppermute | solution.py:47
  94.5 8.5 %collective-permute-start.24 = (bf16[2,16,256]{2,1,0:T(8,128)(2,1)S(1)}, bf16[2,16,256]{2,1,0:T(8,128)(2,1)S(1)}, u32[]{:S(2)}, u32[]{:S(2)}) collective-permute-start(bf16[2,16,256]{2,1,0:T(8,128)(2,1)S(1)} %get-tuple-element.65), channel_id=1, source_target_pairs={{1,2},{2,1},{3,4},{4,3},{5,6},{6,5},{9,10},{10,9},{11,12},{12,11},... | collective-permute-start | bytes 49160 | tf_op jit(solution)/shard_map/ppermute | solution.py:19
  98.9 4.1 %collective-permute-start.25 = (bf16[2,16,256]{2,1,0:T(8,128)(2,1)S(1)}, bf16[2,16,256]{2,1,0:T(8,128)(2,1)S(1)}, u32[]{:S(2)}, u32[]{:S(2)}) collective-permute-start(bf16[2,16,256]{2,1,0:T(8,128)(2,1)S(1)} %get-tuple-element.66), channel_id=1, source_target_pairs={{0,1},{1,0},{2,3},{3,2},{4,5},{5,4},{6,7},{7,6},{8,9},{9,8},{10,11... | collective-permute-start | bytes 49160 | tf_op jit(solution)/shard_map/ppermute | solution.py:17
  99.0 5.5 %collective-permute-start.26 = (bf16[4,16,256]{2,1,0:T(8,128)(2,1)S(1)}, bf16[4,16,256]{2,1,0:T(8,128)(2,1)S(1)}, u32[]{:S(2)}, u32[]{:S(2)}) collective-permute-start(bf16[4,16,256]{2,1,0:T(8,128)(2,1)S(1)} %get-tuple-element.68), channel_id=1, source_target_pairs={{8,16},{16,8},{9,17},{17,9},{10,18},{18,10},{11,19},{19,11},{12,20... | collective-permute-start | bytes 98312 | tf_op jit(solution)/shard_map/ppermute | solution.py:19
  (9 other events, 29.5 us)
